TPU v7x, 32 devices: a whole 2x2x4 slice. The times are simulated.
32 devices in a mesh: req: 4 (over z), exp: 8 (over y, x, core).
Axes of the slice: x: 2, y: 2, z: 4, core: 2. Of those that a mesh axis runs over, the one named last changes fastest.
Arguments:
- resid: bfloat16 [8192, 1536], P(('req', 'exp')), may hold values from -18 to 18
- queries: bfloat16 [8192, 1536], P(('req', 'exp')), may hold values from -40 to 40
- draft_kv: bfloat16 [8192, 1024], P(('req', 'exp')), may hold values from -6 to 6
- prompt_key_value: bfloat16 [16, 1024, 1024], P('exp', 'req'), may hold values from -6 to 6
- cache_page_store: bfloat16 [1536, 64, 1024], P(('req', 'exp')), may hold values from -6 to 6
- page_table: int32 [256, 6], P(('req', 'exp')), may hold values from 0 to 47, as said below
- cache_len: int32 [256], P(('req', 'exp')), may hold values from 1 to 384, as said below
- parents: int32 [256, 32], P(('req', 'exp')), may hold values from -1 to 30, as said below
- groups: int32 [256], P(('req', 'exp')), may hold values from 0 to 1
- w_out: bfloat16 [1536, 1536], replicated, may hold values from -0.15625 to 0.15625
- norm_gain: float32 [1536], replicated, may hold values from 0.25 to 1.75
- routes: int32 [8192, 8], P(('req', 'exp')), may hold values from 0 to 15, all different within a row; in each aligned block of 256 rows (0 to 255, 256 to 511, ...) at most 192 rows name the same one
- route_weight: float32 [8192, 8], P(('req', 'exp')), may hold values from 0.05 to 1
- w_in: bfloat16 [16, 1536, 1024], P('exp'), may hold values from -0.15625 to 0.15625
- w_down: bfloat16 [16, 512, 1536], P('exp'), may hold values from -0.25 to 0.25
Outputs:
- layer_out: bfloat16 [8192, 1536], P(('req', 'exp'))
Inputs may be any that keep to these rules, and one draw needn't show every extreme that they name: `routes`: in each aligned block of 256 rows (the rows of one device) no expert is named by more than 192 rows, a bound that some block reaches; a row names 8 different experts. `page_table`: entries number the 48 pages held with the request's own block of 8 requests; slots past a request's cached positions are not read. `cache_len`: some request has exactly 384 cached positions. parents[r, 0] = -1 marks the root; for u > 0 the parent lies in 0 to u - 1.
All inputs are finite; a program needn't handle non-finite values.
Results may differ from a plain program's by a relative error of at most 0.01.
Values may be sent and summed in bfloat16 or wider, within the bound.
No kernel may reach another device: no remote copies, remote signals or barrier semaphores. Data moves between devices by JAX's collectives and lax.ppermute only.
A program may use at most 192 MiB of HBM per device.

v0:
```python
import math

import jax
import jax.numpy as jnp
from jax import lax
from jax.sharding import PartitionSpec as P

D = 1536
QUERY_HEADS = 24
KEY_VALUE_HEADS = 8
HEAD_WIDTH = 64
FF = 512
TOPK = 8
TREE_TOKENS = 32
GROUPS_PER_COLUMN = 2
PAGE_POSITIONS = 64
MAXP = 6


def ancestry(parent_rows):
    tree_size = parent_rows.shape[1]
    positions = jnp.arange(tree_size, dtype=jnp.int32)
    linked = (parent_rows[:, :, None] == positions[None, None, :]).astype(jnp.float32)
    reach = jnp.eye(tree_size, dtype=jnp.float32)[None] + linked
    for sweep in range((tree_size - 1).bit_length()):
        reach = jnp.minimum(
            jnp.einsum("bij,bjk->bik", reach, reach, precision=lax.Precision.HIGHEST),
            jnp.float32(1.0),
        )
    return reach > 0.5


def prompt_scores(queries_per_request, request_groups, piece, scale_factor):
    key_value_width = KEY_VALUE_HEADS * HEAD_WIDTH
    position_extent = piece.shape[1]
    selected_entries = piece[request_groups]
    key_matrix = selected_entries[..., :key_value_width].reshape(
        selected_entries.shape[0], position_extent, KEY_VALUE_HEADS, HEAD_WIDTH
    )
    value_matrix = selected_entries[..., key_value_width:].reshape(
        selected_entries.shape[0], position_extent, KEY_VALUE_HEADS, HEAD_WIDTH
    )
    scores = (
        jnp.einsum(
            "btkrd,bpkd->btkrp", queries_per_request, key_matrix, preferred_element_type=jnp.float32
        )
        * scale_factor
    )
    return (scores, value_matrix, jnp.max(scores, -1))


def per_device(
    resid,
    queries,
    draft_kv,
    prompt_key_value,
    cache_page_store,
    page_table,
    cache_len,
    parents,
    groups,
    w_out,
    norm_gain,
    routes,
    route_weight,
    w_in,
    w_down,
):
    count_of_tokens = queries.shape[0]
    count_of_requests = page_table.shape[0]
    key_value_width = KEY_VALUE_HEADS * HEAD_WIDTH
    heads_repeated = QUERY_HEADS // KEY_VALUE_HEADS
    scale_factor = HEAD_WIDTH ** (-0.5)
    context_output = MAXP * PAGE_POSITIONS
    queries_per_head = queries.reshape(count_of_tokens, KEY_VALUE_HEADS, heads_repeated, HEAD_WIDTH)
    queries_per_request = queries_per_head.reshape(
        count_of_requests, TREE_TOKENS, KEY_VALUE_HEADS, heads_repeated, HEAD_WIDTH
    )
    pages = cache_page_store[page_table].reshape(
        count_of_requests, context_output, 2 * key_value_width
    )
    local_rows = jnp.concatenate(
        [pages, draft_kv.reshape(count_of_requests, TREE_TOKENS, 2 * key_value_width)], 1
    )
    local_keys = local_rows[..., :key_value_width].reshape(
        count_of_requests, context_output + TREE_TOKENS, KEY_VALUE_HEADS, HEAD_WIDTH
    )
    local_values = local_rows[..., key_value_width:].reshape(
        count_of_requests, context_output + TREE_TOKENS, KEY_VALUE_HEADS, HEAD_WIDTH
    )
    local_scores = (
        jnp.einsum(
            "btkrd,blkd->btkrl", queries_per_request, local_keys, preferred_element_type=jnp.float32
        )
        * scale_factor
    )
    cached = jnp.arange(context_output, dtype=jnp.int32)[None, :] < cache_len[:, None]
    visible = jnp.concatenate(
        [
            jnp.broadcast_to(cached[:, None, :], (count_of_requests, TREE_TOKENS, context_output)),
            ancestry(parents),
        ],
        2,
    )
    local_scores = jnp.where(visible[:, :, None, None, :], local_scores, -jnp.inf)
    local_maximum = jnp.max(local_scores, -1)
    expd = jnp.exp(local_scores - local_maximum[..., None])
    numer = jnp.einsum(
        "btkrl,blkd->btkrd",
        expd.astype(jnp.bfloat16),
        local_values,
        preferred_element_type=jnp.float32,
    )
    home_numer = numer.reshape(count_of_tokens, QUERY_HEADS * HEAD_WIDTH)
    home_denom = jnp.sum(expd, -1).reshape(count_of_tokens, QUERY_HEADS)
    start_carry = (
        local_maximum.reshape(count_of_tokens, KEY_VALUE_HEADS, heads_repeated),
        home_denom.reshape(count_of_tokens, KEY_VALUE_HEADS, heads_repeated),
        home_numer.reshape(count_of_tokens, KEY_VALUE_HEADS, heads_repeated, HEAD_WIDTH),
    )
    piece = lax.all_gather(prompt_key_value, "req", axis=1, tiled=True)
    position_extent = piece.shape[1]
    sub_span = math.gcd(position_extent, 256)
    sub_total = position_extent // sub_span
    portions = piece.reshape(GROUPS_PER_COLUMN, sub_total, sub_span, 2 * key_value_width).transpose(
        1, 0, 2, 3
    )

    def advance(state, portion):
        peak_old, denom_old, numer_old = state
        scores, value_matrix, peak_part = prompt_scores(
            queries_per_request, groups, portion, scale_factor
        )
        peak_new = jnp.maximum(
            peak_old, peak_part.reshape(count_of_tokens, KEY_VALUE_HEADS, heads_repeated)
        )
        expd = jnp.exp(
            scores
            - peak_new.reshape(count_of_requests, TREE_TOKENS, KEY_VALUE_HEADS, heads_repeated)[
                ..., None
            ]
        )
        decay = jnp.exp(peak_old - peak_new)
        fresh = jnp.einsum(
            "btkrp,bpkd->btkrd",
            expd.astype(jnp.bfloat16),
            value_matrix,
            preferred_element_type=jnp.float32,
        )
        numer = numer_old * decay[..., None] + fresh.reshape(
            count_of_tokens, KEY_VALUE_HEADS, heads_repeated, HEAD_WIDTH
        )
        denom = denom_old * decay + jnp.sum(expd, -1).reshape(
            count_of_tokens, KEY_VALUE_HEADS, heads_repeated
        )
        return ((peak_new, denom, numer), None)

    carry_out, unused = lax.scan(advance, start_carry, portions)
    final_peak, denom_all, numer_all = carry_out
    numerator = numer_all.reshape(count_of_tokens, QUERY_HEADS * HEAD_WIDTH)
    denominator = denom_all.reshape(count_of_tokens, QUERY_HEADS)
    attended = (
        (numerator.reshape(count_of_tokens, QUERY_HEADS, HEAD_WIDTH) / denominator[..., None])
        .reshape(count_of_tokens, QUERY_HEADS * HEAD_WIDTH)
        .astype(jnp.bfloat16)
    )
    mixed = resid.astype(jnp.float32) + jnp.dot(attended, w_out, preferred_element_type=jnp.float32)
    spread = jnp.mean(mixed * mixed, -1, keepdims=True)
    normed = (mixed * lax.rsqrt(spread + 1e-05) * norm_gain).astype(jnp.bfloat16)
    exp_devices = lax.axis_size("exp")
    experts_all = w_in.shape[0] * exp_devices
    capacity = 3 * count_of_tokens * TOPK // (2 * experts_all)
    flat_experts = routes.reshape(-1)
    one_hot = (flat_experts[:, None] == jnp.arange(experts_all, dtype=jnp.int32)[None, :]).astype(
        jnp.int32
    )
    earlier = jnp.cumsum(one_hot, 0) - one_hot
    slot = jnp.sum(earlier * one_hot, 1)
    target = flat_experts * capacity + slot
    source = jnp.arange(count_of_tokens * TOPK, dtype=jnp.int32) // TOPK
    outgoing = jnp.zeros((experts_all * capacity, D), jnp.bfloat16).at[target].set(normed[source])
    outgoing = outgoing.reshape(exp_devices, w_in.shape[0], capacity, D)
    both = jnp.einsum(
        "secd,edf->secf",
        lax.all_to_all(outgoing, "exp", split_axis=0, concat_axis=0, tiled=True),
        w_in,
        preferred_element_type=jnp.float32,
    )
    act = (jax.nn.silu(both[..., :FF]) * both[..., FF:]).astype(jnp.bfloat16)
    result = jnp.einsum("secf,efd->secd", act, w_down, preferred_element_type=jnp.float32).astype(
        jnp.bfloat16
    )
    returned = lax.all_to_all(result, "exp", split_axis=0, concat_axis=0, tiled=True)
    per_choice = returned.reshape(experts_all * capacity, D)[target].reshape(
        count_of_tokens, TOPK, D
    )
    blended = jnp.sum(route_weight[..., None] * per_choice.astype(jnp.float32), 1)
    return (mixed + blended).astype(jnp.bfloat16)


def solution(mesh):
    in_specs = (
        P(("req", "exp"), None),
        P(("req", "exp"), None),
        P(("req", "exp"), None),
        P("exp", "req", None),
        P(("req", "exp"), None, None),
        P(("req", "exp"), None),
        P(("req", "exp")),
        P(("req", "exp"), None),
        P(("req", "exp")),
        P(),
        P(),
        P(("req", "exp"), None),
        P(("req", "exp"), None),
        P("exp", None, None),
        P("exp", None, None),
    )
    out_specs = P(("req", "exp"), None)
    return jax.shard_map(
        per_device, mesh=mesh, in_specs=in_specs, out_specs=out_specs, check_vma=False
    )
```

profile of v0, /device:TPU:0, one launch (start us, length us, event | category | flops | bytes accessed | tf_op | source)
XLA Modules:
  0.0 589.6 jit_solution(9648546325195599911)
XLA Ops:
  9.3 7.7 %gather_fusion.1 = bf16[48,64,1024]{2,1,0:T(8,128)(2,1)} fusion(bf16[48,64,1024]{2,1,0:T(8,128)(2,1)} %param.21, s32[1024]{0:T(1024)S(1)} %pad_clamp_fusion.1), kind=kCustom, calls=%fused_computation.1 | custom fusion | bytes 12583104 | tf_op jit(solution)/shard_map/gather | solution.py:79
  17.0 8.8 %copy.67 = bf16[8,384,1024]{1,2,0:T(8,128)(2,1)} copy(bf16[8,384,1024]{2,1,0:T(8,128)(2,1)} %bitcast.177) | data formatting | bytes 12582912 | tf_op jit(solution)/shard_map/reshape | solution.py:79
  25.8 2.7 copy.68
  28.5 5.1 reshape_reshape.12
  33.7 2.8 copy.69
  38.0 3.6 pad_maximum_fusion
  41.6 6.4 %fusion.15 = (f32[8,32,8,3]{1,3,2,0:T(4,128)S(1)}, f32[8,8,416,32,3]{2,3,4,1,0:T(8,128)}) fusion(pred[8,32,416]{2,1,0:T(8,128)(4,1)S(1)} %pad_add_fusion, bf16[8,416,8,64,1]{1,3,4,2,0:T(8,128)(2,1)S(1)} %bitcast.178, bf16[8,32,8,3,64]{4,1,3,2,0:T(8,128)(2,1)S(1)} %copy.69), kind=kOutput, calls=%fused_computation.28 | convolution fusion | flops 334817280 | bytes 14548992 | tf_op jit(solution)/shard_map/btkrd,blkd->btkrl/dot_general | solution.py:92
  48.1 6.3 %fusion.38 = f32[8,32,8,3,64]{4,1,3,2,0:T(8,128)S(1)} fusion(bf16[8,416,8,64,1]{1,3,4,2,0:T(8,128)(2,1)S(1)} %bitcast.180, f32[8,8,416,32,3]{2,3,4,1,0:T(8,128)} %get-tuple-element.89, f32[8,32,8,3]{1,3,2,0:T(4,128)S(1)} %get-tuple-element.88, pred[8,32,416]{2,1,0:T(8,128)(4,1)S(1)} %pad_add_fusion), kind=kOutput, calls=%fused_computation.51 | convolution fusion | flops 337379328 | bytes 15335424 | tf_op jit(solution)/shard_map/btkrl,blkd->btkrd/dot_general | solution.py:108
  54.3 3.5 copy.72
  57.8 6.8 %fusion.14 = f32[8,32,8,3]{1,3,2,0:T(4,128)S(1)} fusion(f32[8,8,416,32,3]{2,3,4,1,0:T(8,128)} %get-tuple-element.89, f32[8,32,8,3]{1,3,2,0:T(4,128)S(1)} %get-tuple-element.88, pred[8,32,416]{2,1,0:T(8,128)(4,1)S(1)} %pad_add_fusion), kind=kLoop, calls=%fused_computation.27 | loop fusion | flops 10217472 | bytes 10379264 | tf_op jit(solution)/shard_map/reduce_sum | solution.py:115
  65.5 8.5 %reduce-window.6 = s32[16,16,128]{2,1,0:T(8,128)S(1)} reduce-window(s32[16,16,128]{2,1,0:T(8,128)} %fusion.48, s32[]{:T(128)} %copy.122), window={size=1x1x128 pad=0_0x0_0x127_0}, to_apply=%region_6.7 | reduce-window | flops 4161536 | bytes 262148 | tf_op jit(solution)/shard_map/reduce-window
  76.7 15.7 %all-gather.2.cloned.1.call-done = bf16[2,1024,1024]{2,1,0:T(8,128)(2,1)} async-done(((bf16[2,256,1024]{2,1,0:T(8,128)(2,1)}), bf16[2,1024,1024]{2,1,0:T(8,128)(2,1)}) %all-gather.2.cloned.1.call-update) | async-done | bytes 4194320 | tf_op jit(solution)/shard_map/all_gather | solution.py:121
  92.4 157.2 %while.14 = (s32[]{:T(128)}, f32[256,8,3]{0,1,2:T(8,128)S(1)}, f32[256,8,3]{0,1,2:T(8,128)S(1)}, f32[256,8,3,64]{3,1,2,0:T(8,128)}, bf16[4,2,256,1024]{3,2,0,1:T...) while((s32[]{:T(128)}, f32[256,8,3]{0,1,2:T(8,128)S(1)}, ...), condition=%wide.region_5.6_spmd, body=%wide.region_2.5_spmd.sunk | while | flops 416035872 | bytes 73978160 | solution.py:158
  92.4 2.3 dynamic-slice_bitcast_fusion.2
  94.8 4.1 gather_fusion
  98.8 4.6 fusion.85
  103.4 3.9 copy.103
  107.3 5.6 bitcast_reduce_fusion.2
  113.3 3.8 fusion.86
  118.3 3.9 copy.107
  122.2 4.4 fusion.87
  126.7 1.8 copy.108
  130.1 1.7 copy-done.2
  131.7 2.3 dynamic-slice_bitcast_fusion.2
  134.1 4.1 gather_fusion
  138.1 4.6 fusion.85
  142.7 3.9 copy.103
  146.6 5.6 bitcast_reduce_fusion.2
  152.6 3.8 fusion.86
  157.6 3.9 copy.107
  161.5 4.4 fusion.87
  165.9 1.8 copy.108
  169.3 1.7 copy-done.2
  171.0 2.3 dynamic-slice_bitcast_fusion.2
  173.4 4.1 gather_fusion
  177.4 4.6 fusion.85
  182.0 3.9 copy.103
  185.9 5.6 bitcast_reduce_fusion.2
  191.9 3.8 fusion.86
  196.9 3.9 copy.107
  200.8 4.4 fusion.87
  205.2 1.8 copy.108
  208.6 1.7 copy-done.2
  210.3 2.3 dynamic-slice_bitcast_fusion.2
  212.6 4.1 gather_fusion
  216.7 4.6 fusion.85
  221.3 3.9 copy.103
  225.2 5.6 bitcast_reduce_fusion.2
  231.2 3.8 fusion.86
  236.2 3.9 copy.107
  240.1 4.4 fusion.87
  244.5 1.8 copy.108
  247.9 1.7 copy-done.2
  249.6 3.2 copy.75
  254.4 4.0 multiply_reduce_fusion
  260.7 39.5 %scatter_custom_fusion = bf16[3072,1536]{1,0:T(8,128)(2,1)} fusion(s32[2048]{0:T(1024)S(1)} %bitcast.184, bf16[256,1536]{1,0:T(8,128)(2,1)} %multiply_convert_fusion, s32[2048]{0:T(1024)S(1)} %broadcast_clamp_fusion.1, bf16[]{:T(256)} %constant.58.clone.1), kind=kCustom, calls=%fused_computation.38 | custom fusion | bytes 9437696 | tf_op jit(solution)/shard_map/scatter | solution.py:181
  300.2 109.3 %all_to_all.10 = bf16[8,2,192,1536]{3,2,1,0:T(8,128)(2,1)S(1)} all-to-all(bf16[8,2,192,1536]{3,2,1,0:T(8,128)(2,1)} %bitcast.176), channel_id=1, replica_groups=mesh['req'=4,'exp'=8] {'exp'}, dimensions={0} | all-to-all | bytes 18874368 | tf_op jit(solution)/shard_map/all_to_all | solution.py:185
  409.5 15.3 %fusion.29 = f32[8,2,192,1024]{3,2,0,1:T(8,128)} fusion(bf16[2,1536,1024]{2,1,0:T(8,128)(2,1)} %param.30, bf16[8,2,192,1536]{3,2,1,0:T(8,128)(2,1)S(1)} %all_to_all.10), kind=kOutput, calls=%fused_computation.45 | convolution fusion | flops 9663676416 | bytes 28311552 | tf_op jit(solution)/shard_map/secd,edf->secf/dot_general | solution.py:183
  424.8 10.5 %convert_bitcast_fusion = bf16[8,2,192,1536]{3,2,0,1:T(8,128)(2,1)} fusion(f32[8,2,192,1024]{3,2,0,1:T(8,128)} %fusion.29, bf16[2,512,1536]{2,1,0:T(8,128)(2,1)S(1)} %copy-done), kind=kOutput, calls=%fused_computation.31 | convolution fusion | flops 4845993984 | bytes 25165824 | tf_op jit(solution)/shard_map/secf,efd->secd/dot_general | solution.py:190
  435.3 8.1 %copy.82 = bf16[8,2,192,1536]{3,2,1,0:T(8,128)(2,1)} copy(bf16[8,2,192,1536]{3,2,0,1:T(8,128)(2,1)} %convert_bitcast_fusion) | data formatting | bytes 18874368 | tf_op jit(solution)/shard_map/convert_element_type | solution.py:190
  443.4 5.4 all-to-all-start.1
  449.0 105.2 %all-to-all-done.1 = bf16[8,2,192,1536]{3,2,1,0:T(8,128)(2,1)} async-done(((bf16[8,2,192,1536]{3,2,1,0:T(8,128)(2,1)}), bf16[8,2,192,1536]{3,2,1,0:T(8,128)(2,1)}, u32[]{:S(2)}, u32[]{:S(2)}) %all-to-all-start.1) | async-done | bytes 9437216 | tf_op jit(solution)/shard_map/all_to_all | solution.py:193
  554.1 18.2 %gather_fusion.2 = bf16[2048,1536]{1,0:T(8,128)(2,1)} fusion(bf16[3072,1536]{1,0:T(8,128)(2,1)} %bitcast.38, s32[2048]{0:T(1024)S(1)} %broadcast_clamp_fusion), kind=kCustom, calls=%fused_computation.3 | custom fusion | bytes 12591104 | tf_op jit(solution)/shard_map/gather | solution.py:194
  572.3 9.0 %fusion.12 = f32[256,1536]{1,0:T(8,128)S(1)} fusion(bf16[2048,1536]{1,0:T(8,128)(2,1)} %gather_fusion.2, f32[256,8]{1,0:T(8,128)S(1)} %copy.77), kind=kLoop, calls=%fused_computation.23 | loop fusion | flops 9043968 | bytes 7872512 | tf_op jit(solution)/shard_map/reduce_sum | solution.py:197
  (134 shorter events, 25.1 us)
Async XLA Ops:
  6.5 418.2 %copy-start = (bf16[2,512,1536]{2,1,0:T(8,128)(2,1)S(1)}, bf16[2,512,1536]{2,1,0:T(8,128)(2,1)}, u32[]{:S(2)}) copy-start(bf16[2,512,1536]{2,1,0:T(8,128)(2,1)} %param.31) | copy-start | bytes 9437188
  6.5 85.9 %all-gather.2.cloned.1.call-start = ((), (), s32[]{:S(2)}) async-start(), calls=%async_computation.2 | async-start | bytes 5242880 | tf_op jit(solution)/shard_map/all_gather | solution.py:121
  25.8 10.6 %copy-start.11 = (s32[8,32]{1,0:T(8,128)S(1)}, s32[8,32]{1,0:T(8,128)}, u32[]{:S(2)}) copy-start(s32[8,32]{1,0:T(8,128)} %param.24) | copy-start | bytes 3076
  25.8 11.0 %copy-start.12 = (s32[8]{0:T(128)S(1)}, s32[8]{0:T(128)}, u32[]{:S(2)}) copy-start(s32[8]{0:T(128)} %param.23) | copy-start | bytes 100
  33.6 4.4 copy-start.7
  36.4 5.2 copy-start.3
  57.8 16.8 %copy-start.8 = (s32[256,8]{0,1:T(8,128)S(1)}, s32[256,8]{0,1:T(8,128)}, u32[]{:S(2)}) copy-start(s32[256,8]{0,1:T(8,128)} %param.28) | copy-start | bytes 24580
  57.8 34.6 %copy-start.13 = (s32[8]{0:T(128)S(1)}, s32[8]{0:T(128)}, u32[]{:S(2)}) copy-start(s32[8]{0:T(128)} %param.25) | copy-start | bytes 100
  122.2 6.2 %copy-start.1 = (f32[256,8,3,64]{3,1,2,0:T(8,128)S(1)}, f32[256,8,3,64]{3,1,2,0:T(8,128)}, u32[]{:S(2)}) copy-start(f32[256,8,3,64]{3,1,2,0:T(8,128)} %get-tuple-element.158) | copy-start | bytes 4718596 | tf_op jit(solution)/shard_map/while
  122.2 6.2 %copy-start.4 = (f32[256,8,3]{1,2,0:T(4,128)S(1)}, f32[256,8,3]{1,2,0:T(4,128)}, u32[]{:S(2)}) copy-start(f32[256,8,3]{1,2,0:T(4,128)} %copy.109) | copy-start | bytes 73732 | tf_op jit(solution)/shard_map/while
  130.0 1.7 copy-start.2
  161.5 6.2 %copy-start.1 = (f32[256,8,3,64]{3,1,2,0:T(8,128)S(1)}, f32[256,8,3,64]{3,1,2,0:T(8,128)}, u32[]{:S(2)}) copy-start(f32[256,8,3,64]{3,1,2,0:T(8,128)} %get-tuple-element.158) | copy-start | bytes 4718596 | tf_op jit(solution)/shard_map/while
  161.5 6.2 %copy-start.4 = (f32[256,8,3]{1,2,0:T(4,128)S(1)}, f32[256,8,3]{1,2,0:T(4,128)}, u32[]{:S(2)}) copy-start(f32[256,8,3]{1,2,0:T(4,128)} %copy.109) | copy-start | bytes 73732 | tf_op jit(solution)/shard_map/while
  169.3 1.7 copy-start.2
  200.8 6.2 %copy-start.1 = (f32[256,8,3,64]{3,1,2,0:T(8,128)S(1)}, f32[256,8,3,64]{3,1,2,0:T(8,128)}, u32[]{:S(2)}) copy-start(f32[256,8,3,64]{3,1,2,0:T(8,128)} %get-tuple-element.158) | copy-start | bytes 4718596 | tf_op jit(solution)/shard_map/while
  200.8 6.2 %copy-start.4 = (f32[256,8,3]{1,2,0:T(4,128)S(1)}, f32[256,8,3]{1,2,0:T(4,128)}, u32[]{:S(2)}) copy-start(f32[256,8,3]{1,2,0:T(4,128)} %copy.109) | copy-start | bytes 73732 | tf_op jit(solution)/shard_map/while
  208.6 1.7 copy-start.2
  240.1 6.2 %copy-start.1 = (f32[256,8,3,64]{3,1,2,0:T(8,128)S(1)}, f32[256,8,3,64]{3,1,2,0:T(8,128)}, u32[]{:S(2)}) copy-start(f32[256,8,3,64]{3,1,2,0:T(8,128)} %get-tuple-element.158) | copy-start | bytes 4718596 | tf_op jit(solution)/shard_map/while
  240.1 6.2 %copy-start.4 = (f32[256,8,3]{1,2,0:T(4,128)S(1)}, f32[256,8,3]{1,2,0:T(4,128)}, u32[]{:S(2)}) copy-start(f32[256,8,3]{1,2,0:T(4,128)} %copy.109) | copy-start | bytes 73732 | tf_op jit(solution)/shard_map/while
  247.9 1.7 copy-start.2
  254.4 5.2 copy-start.9
  258.5 1.2 copy-start.5
  443.4 5.4 copy-start.10
  443.4 110.7 %all-to-all-start.1 = ((bf16[8,2,192,1536]{3,2,1,0:T(8,128)(2,1)}), bf16[8,2,192,1536]{3,2,1,0:T(8,128)(2,1)}, u32[]{:S(2)}, u32[]{:S(2)}) async-start(bf16[8,2,192,1536]{3,2,1,0:T(8,128)(2,1)} %copy.82), calls=%async_computation.1 | async-start | bytes 18874368 | tf_op jit(solution)/shard_map/all_to_all | solution.py:193
  572.3 9.0 %copy-start.6 = (f32[256,1536]{1,0:T(8,128)S(1)}, f32[256,1536]{1,0:T(8,128)}, u32[]{:S(2)}) copy-start(f32[256,1536]{1,0:T(8,128)} %copy-done.5) | copy-start | bytes 4718596
Sparse Core Ops, SparseCore 0:
  8.9 83.4 all-gather.1
where the time goes:
time: 601 us; the launch traced here: 590 us
  local copies, waits for them, and re-layouts  200 us (33%)
  waiting for transfers between devices  122 us (20%)
  blocking collectives  109 us (18%)
  matrix products  84.1 us (14%)
  other arithmetic  55.1 us (9%)
  between operations  14.1 us (2%)
    all_to_all x1, blocking collectives, per_device(): lax.all_to_all(outgoing, 'exp', split_axis=0, concat_axis=0, tiled=True)  109 us
    all_to_all x1, waiting for transfers between devices, per_device(): lax.all_to_all(result, 'exp', split_axis=0, concat_axis=0, tiled=True)  105 us
    scatter x1, local copies, waits for them, and re-layouts, per_device(): jnp.zeros((experts_all * capacity, D), jnp.bfloat16).at[target]  39.5 us
    slice x8, local copies, waits for them, and re-layouts, prompt_scores(): selected_entries[..., key_value_width:]  33.9 us
    dot_general x4, matrix products, prompt_scores(): jnp.einsum('btkrd,bpkd->btkrp', queries_per_request, key_matrix, preferre...  22.6 us
    gather x1, local copies, waits for them, and re-layouts, per_device(): returned.reshape(experts_all * capacity, D)[target]  18.2 us
    dot_general x4, matrix products, advance(): jnp.einsum('btkrp,bpkd->btkrd', expd.astype(jnp.bfloat16), value_matrix,...  17.7 us
    gather x4, local copies, waits for them, and re-layouts, prompt_scores(): selected_entries = piece[request_groups]  16.3 us
  transfers between devices with their start and end apart: 2, of which 2 were waited for; matrix products, arithmetic and copies ran while one was open for 12% of the time, Pallas kernels for 0%

commit v1 on v0

--- a/solution.py
+++ b/solution.py
@@ -167,34 +167,29 @@
     mixed = resid.astype(jnp.float32) + jnp.dot(attended, w_out, preferred_element_type=jnp.float32)
     spread = jnp.mean(mixed * mixed, -1, keepdims=True)
     normed = (mixed * lax.rsqrt(spread + 1e-05) * norm_gain).astype(jnp.bfloat16)
-    exp_devices = lax.axis_size("exp")
-    experts_all = w_in.shape[0] * exp_devices
-    capacity = 3 * count_of_tokens * TOPK // (2 * experts_all)
-    flat_experts = routes.reshape(-1)
-    one_hot = (flat_experts[:, None] == jnp.arange(experts_all, dtype=jnp.int32)[None, :]).astype(
-        jnp.int32
-    )
-    earlier = jnp.cumsum(one_hot, 0) - one_hot
-    slot = jnp.sum(earlier * one_hot, 1)
-    target = flat_experts * capacity + slot
-    source = jnp.arange(count_of_tokens * TOPK, dtype=jnp.int32) // TOPK
-    outgoing = jnp.zeros((experts_all * capacity, D), jnp.bfloat16).at[target].set(normed[source])
-    outgoing = outgoing.reshape(exp_devices, w_in.shape[0], capacity, D)
-    both = jnp.einsum(
-        "secd,edf->secf",
-        lax.all_to_all(outgoing, "exp", split_axis=0, concat_axis=0, tiled=True),
-        w_in,
-        preferred_element_type=jnp.float32,
-    )
+    local_experts = w_in.shape[0]
+    first_expert = lax.axis_index("exp") * local_experts
+    gathered = lax.all_gather(normed, "exp", axis=0, tiled=True)
+    gathered_routes = lax.all_gather(routes, "exp", axis=0, tiled=True)
+    gathered_weights = lax.all_gather(route_weight, "exp", axis=0, tiled=True)
+    expert_ids = first_expert + jnp.arange(local_experts, dtype=jnp.int32)
+    gate = jnp.sum(
+        jnp.where(
+            gathered_routes[None, :, :] == expert_ids[:, None, None],
+            gathered_weights[None, :, :],
+            jnp.float32(0.0),
+        ),
+        -1,
+    )
+    both = jnp.einsum("td,edf->etf", gathered, w_in, preferred_element_type=jnp.float32)
     act = (jax.nn.silu(both[..., :FF]) * both[..., FF:]).astype(jnp.bfloat16)
-    result = jnp.einsum("secf,efd->secd", act, w_down, preferred_element_type=jnp.float32).astype(
+    result = jnp.einsum("etf,efd->etd", act, w_down, preferred_element_type=jnp.float32).astype(
         jnp.bfloat16
     )
-    returned = lax.all_to_all(result, "exp", split_axis=0, concat_axis=0, tiled=True)
-    per_choice = returned.reshape(experts_all * capacity, D)[target].reshape(
-        count_of_tokens, TOPK, D
-    )
-    blended = jnp.sum(route_weight[..., None] * per_choice.astype(jnp.float32), 1)
+    partial = jnp.sum(gate[..., None] * result.astype(jnp.float32), 0)
+    blended = lax.psum_scatter(
+        partial.astype(jnp.bfloat16), "exp", scatter_dimension=0, tiled=True
+    ).astype(jnp.float32)
     return (mixed + blended).astype(jnp.bfloat16)
 
 

time: 601 us -> 412 us (0.69)
  the two profiles are of different devices: /device:TPU:0 before, /device:TPU:12 now
where the time goes in v1:
time: 412 us; the launch traced here: 408 us
  local copies, waits for them, and re-layouts  130 us (32%)
  waiting for transfers between devices  116 us (28%)
  matrix products  92.4 us (22%)
  other arithmetic  38.5 us (9%)
  blocking collectives  17.5 us (4%)
  between operations  13.3 us (3%)
    reduce_scatter x1, waiting for transfers between devices, per_device(): lax.psum_scatter(partial.astype(jnp.bfloat16), 'exp', scatter_dimension=0...  62 us
    slice x8, local copies, waits for them, and re-layouts, prompt_scores(): selected_entries[..., key_value_width:]  33.9 us
    all_gather x1, waiting for transfers between devices, per_device(): gathered = lax.all_gather(normed, 'exp', axis=0, tiled=True)  29 us
    all_gather x1, waiting for transfers between devices, per_device(): piece = lax.all_gather(prompt_key_value, 'req', axis=1, tiled=True)  24.5 us
    dot_general x4, matrix products, prompt_scores(): jnp.einsum('btkrd,bpkd->btkrp', queries_per_request, key_matrix, preferre...  22.7 us
    dot_general x1, matrix products, per_device(): jnp.einsum('td,edf->etf', gathered, w_in, preferred_element_type=jnp.floa...  19.4 us
    dot_general x4, matrix products, advance(): jnp.einsum('btkrp,bpkd->btkrd', expd.astype(jnp.bfloat16), value_matrix,...  17.1 us
    gather x4, local copies, waits for them, and re-layouts, prompt_scores(): selected_entries = piece[request_groups]  15.9 us
  transfers between devices with their start and end apart: 3, of which 3 were waited for; matrix products, arithmetic and copies ran while one was open for 14% of the time, Pallas kernels for 0%

profile of v1, /device:TPU:12, one launch (start us, length us, event | category | flops | bytes accessed | tf_op | source)
XLA Modules:
  0.0 408.5 jit_solution(1143790002661001322)
XLA Ops:
  8.3 7.7 %gather_fusion.1 = bf16[48,64,1024]{2,1,0:T(8,128)(2,1)} fusion(bf16[48,64,1024]{2,1,0:T(8,128)(2,1)} %param.21, s32[1024]{0:T(1024)S(1)} %pad_clamp_fusion.1), kind=kCustom, calls=%fused_computation.1 | custom fusion | bytes 12583104 | tf_op jit(solution)/shard_map/gather | solution.py:79
  16.0 8.8 %copy.79 = bf16[8,384,1024]{1,2,0:T(8,128)(2,1)} copy(bf16[8,384,1024]{2,1,0:T(8,128)(2,1)} %bitcast.141) | data formatting | bytes 12582912 | tf_op jit(solution)/shard_map/reshape | solution.py:79
  24.8 2.7 copy.80
  27.5 5.1 %reshape_reshape.12 = bf16[8,32,8,3,64]{4,3,2,1,0:T(4,128)(2,1)} reshape(bf16[256,1536]{1,0:T(8,128)(2,1)} %param.18) | data formatting | bytes 1572864 | tf_op jit(solution)/shard_map/reshape;reshape | solution.py:76
  32.6 2.8 copy.81
  37.0 3.6 pad_maximum_fusion
  40.6 6.4 %fusion.14 = (f32[8,32,8,3]{1,3,2,0:T(4,128)S(1)}, f32[8,8,416,32,3]{2,3,4,1,0:T(8,128)}) fusion(pred[8,32,416]{2,1,0:T(8,128)(4,1)S(1)} %pad_add_fusion, bf16[8,416,8,64,1]{1,3,4,2,0:T(8,128)(2,1)S(1)} %bitcast.142, bf16[8,32,8,3,64]{4,1,3,2,0:T(8,128)(2,1)S(1)} %copy.81), kind=kOutput, calls=%fused_computation.24 | convolution fusion | flops 334817280 | bytes 14548992 | tf_op jit(solution)/shard_map/btkrd,blkd->btkrl/dot_general | solution.py:92
  47.1 6.3 %fusion.26 = f32[8,32,8,3,64]{4,1,3,2,0:T(8,128)S(1)} fusion(bf16[8,416,8,64,1]{1,3,4,2,0:T(8,128)(2,1)S(1)} %bitcast.144, f32[8,8,416,32,3]{2,3,4,1,0:T(8,128)} %get-tuple-element.96, f32[8,32,8,3]{1,3,2,0:T(4,128)S(1)} %get-tuple-element.95, pred[8,32,416]{2,1,0:T(8,128)(4,1)S(1)} %pad_add_fusion), kind=kOutput, calls=%fused_computation.40 | convolution fusion | flops 337379328 | bytes 15335424 | tf_op jit(solution)/shard_map/btkrl,blkd->btkrd/dot_general | solution.py:108
  53.4 3.4 copy.84
  56.8 6.8 %fusion.13 = f32[8,32,8,3]{1,3,2,0:T(4,128)S(1)} fusion(f32[8,8,416,32,3]{2,3,4,1,0:T(8,128)} %get-tuple-element.96, f32[8,32,8,3]{1,3,2,0:T(4,128)S(1)} %get-tuple-element.95, pred[8,32,416]{2,1,0:T(8,128)(4,1)S(1)} %pad_add_fusion), kind=kLoop, calls=%fused_computation.23 | loop fusion | flops 10217472 | bytes 10379264 | tf_op jit(solution)/shard_map/reduce_sum | solution.py:115
  63.9 24.5 %all-gather.3.cloned.1.call-done = bf16[2,1024,1024]{2,1,0:T(8,128)(2,1)} async-done(((bf16[2,256,1024]{2,1,0:T(8,128)(2,1)}), bf16[2,1024,1024]{2,1,0:T(8,128)(2,1)}) %all-gather.3.cloned.1.call-update) | async-done | bytes 4194320 | tf_op jit(solution)/shard_map/all_gather | solution.py:121
  88.4 156.6 %while.14 = (s32[]{:T(128)}, f32[256,8,3]{0,1,2:T(8,128)S(1)}, f32[256,8,3]{0,1,2:T(8,128)S(1)}, f32[256,8,3,64]{3,1,2,0:T(8,128)}, bf16[4,2,256,1024]{3,2,0,1:T...) while((s32[]{:T(128)}, f32[256,8,3]{0,1,2:T(8,128)S(1)}, ...), condition=%wide.region_5.6_spmd, body=%wide.region_2.5_spmd.sunk | while | flops 416035872 | bytes 73978160 | solution.py:158
  88.4 2.3 dynamic-slice_bitcast_fusion.2
  90.7 4.0 gather_fusion
  94.7 4.6 %fusion.71 = (bf16[8,256,512]{2,1,0:T(8,128)(2,1)}, bf16[8,256,512]{2,1,0:T(8,128)(2,1)}) fusion(bf16[8,256,1024]{2,1,0:T(8,128)(2,1)} %gather_fusion), kind=kLoop, calls=%fused_computation.69.clone.1 | loop fusion | bytes 8388608 | tf_op jit(solution)/shard_map/while/body/eval_jaxpr/slice | solution.py:40
  99.2 3.9 copy.101
  103.1 5.7 %bitcast_reduce_fusion.2 = (f32[8,32,8,3]{1,3,2,0:T(4,128)S(1)}, f32[8,8,256,32,3]{2,3,4,1,0:T(8,128)}) fusion(bf16[8,256,8,64,1]{1,3,4,2,0:T(8,128)(2,1)} %bitcast.138, bf16[8,32,8,3,64]{4,1,3,2,0:T(8,128)(2,1)} %get-tuple-element.176), kind=kOutput, calls=%fused_computation.3.clone.1 | convolution fusion | flops 204466176 | bytes 9199616 | tf_op jit(solution)/shard_map/while/body/eval_jaxpr/btkrd,bpkd->btkrp/dot_general | solution.py:44
  109.1 3.8 fusion.72
  114.2 3.9 copy.105
  118.1 4.3 %fusion.73 = f32[8,32,8,3,64]{4,1,3,2,0:T(8,128)S(1)} fusion(bf16[8,256,8,64,1]{1,3,4,2,0:T(8,128)(2,1)} %bitcast.139, f32[8,8,256,32,3]{2,3,4,1,0:T(8,128)} %get-tuple-element.150, f32[8,32,8,3]{1,3,2,0:T(4,128)S(1)} %copy.103), kind=kOutput, calls=%fused_computation.11.clone.1 | convolution fusion | flops 206045184 | bytes 9986048 | tf_op jit(solution)/shard_map/while/body/eval_jaxpr/btkrp,bpkd->btkrd/dot_general | solution.py:144
  122.4 1.8 copy.106
  124.3 1.5 bitcast_add_fusion.2
  125.9 1.6 copy-done.2
  127.5 2.3 dynamic-slice_bitcast_fusion.2
  129.8 4.0 gather_fusion
  133.8 4.6 %fusion.71 = (bf16[8,256,512]{2,1,0:T(8,128)(2,1)}, bf16[8,256,512]{2,1,0:T(8,128)(2,1)}) fusion(bf16[8,256,1024]{2,1,0:T(8,128)(2,1)} %gather_fusion), kind=kLoop, calls=%fused_computation.69.clone.1 | loop fusion | bytes 8388608 | tf_op jit(solution)/shard_map/while/body/eval_jaxpr/slice | solution.py:40
  138.4 3.9 copy.101
  142.3 5.7 %bitcast_reduce_fusion.2 = (f32[8,32,8,3]{1,3,2,0:T(4,128)S(1)}, f32[8,8,256,32,3]{2,3,4,1,0:T(8,128)}) fusion(bf16[8,256,8,64,1]{1,3,4,2,0:T(8,128)(2,1)} %bitcast.138, bf16[8,32,8,3,64]{4,1,3,2,0:T(8,128)(2,1)} %get-tuple-element.176), kind=kOutput, calls=%fused_computation.3.clone.1 | convolution fusion | flops 204466176 | bytes 9199616 | tf_op jit(solution)/shard_map/while/body/eval_jaxpr/btkrd,bpkd->btkrp/dot_general | solution.py:44
  148.3 3.8 fusion.72
  153.3 3.9 copy.105
  157.2 4.3 %fusion.73 = f32[8,32,8,3,64]{4,1,3,2,0:T(8,128)S(1)} fusion(bf16[8,256,8,64,1]{1,3,4,2,0:T(8,128)(2,1)} %bitcast.139, f32[8,8,256,32,3]{2,3,4,1,0:T(8,128)} %get-tuple-element.150, f32[8,32,8,3]{1,3,2,0:T(4,128)S(1)} %copy.103), kind=kOutput, calls=%fused_computation.11.clone.1 | convolution fusion | flops 206045184 | bytes 9986048 | tf_op jit(solution)/shard_map/while/body/eval_jaxpr/btkrp,bpkd->btkrd/dot_general | solution.py:144
  161.5 1.8 copy.106
  163.5 1.5 bitcast_add_fusion.2
  165.0 1.6 copy-done.2
  166.7 2.3 dynamic-slice_bitcast_fusion.2
  169.0 4.0 gather_fusion
  172.9 4.6 %fusion.71 = (bf16[8,256,512]{2,1,0:T(8,128)(2,1)}, bf16[8,256,512]{2,1,0:T(8,128)(2,1)}) fusion(bf16[8,256,1024]{2,1,0:T(8,128)(2,1)} %gather_fusion), kind=kLoop, calls=%fused_computation.69.clone.1 | loop fusion | bytes 8388608 | tf_op jit(solution)/shard_map/while/body/eval_jaxpr/slice | solution.py:40
  177.5 3.9 copy.101
  181.4 5.7 %bitcast_reduce_fusion.2 = (f32[8,32,8,3]{1,3,2,0:T(4,128)S(1)}, f32[8,8,256,32,3]{2,3,4,1,0:T(8,128)}) fusion(bf16[8,256,8,64,1]{1,3,4,2,0:T(8,128)(2,1)} %bitcast.138, bf16[8,32,8,3,64]{4,1,3,2,0:T(8,128)(2,1)} %get-tuple-element.176), kind=kOutput, calls=%fused_computation.3.clone.1 | convolution fusion | flops 204466176 | bytes 9199616 | tf_op jit(solution)/shard_map/while/body/eval_jaxpr/btkrd,bpkd->btkrp/dot_general | solution.py:44
  187.4 3.8 fusion.72
  192.4 3.9 copy.105
  196.3 4.3 %fusion.73 = f32[8,32,8,3,64]{4,1,3,2,0:T(8,128)S(1)} fusion(bf16[8,256,8,64,1]{1,3,4,2,0:T(8,128)(2,1)} %bitcast.139, f32[8,8,256,32,3]{2,3,4,1,0:T(8,128)} %get-tuple-element.150, f32[8,32,8,3]{1,3,2,0:T(4,128)S(1)} %copy.103), kind=kOutput, calls=%fused_computation.11.clone.1 | convolution fusion | flops 206045184 | bytes 9986048 | tf_op jit(solution)/shard_map/while/body/eval_jaxpr/btkrp,bpkd->btkrd/dot_general | solution.py:144
  200.6 1.8 copy.106
  202.6 1.5 bitcast_add_fusion.2
  204.2 1.6 copy-done.2
  205.8 2.3 dynamic-slice_bitcast_fusion.2
  208.1 4.0 gather_fusion
  212.1 4.6 %fusion.71 = (bf16[8,256,512]{2,1,0:T(8,128)(2,1)}, bf16[8,256,512]{2,1,0:T(8,128)(2,1)}) fusion(bf16[8,256,1024]{2,1,0:T(8,128)(2,1)} %gather_fusion), kind=kLoop, calls=%fused_computation.69.clone.1 | loop fusion | bytes 8388608 | tf_op jit(solution)/shard_map/while/body/eval_jaxpr/slice | solution.py:40
  216.7 3.9 copy.101
  220.6 5.7 %bitcast_reduce_fusion.2 = (f32[8,32,8,3]{1,3,2,0:T(4,128)S(1)}, f32[8,8,256,32,3]{2,3,4,1,0:T(8,128)}) fusion(bf16[8,256,8,64,1]{1,3,4,2,0:T(8,128)(2,1)} %bitcast.138, bf16[8,32,8,3,64]{4,1,3,2,0:T(8,128)(2,1)} %get-tuple-element.176), kind=kOutput, calls=%fused_computation.3.clone.1 | convolution fusion | flops 204466176 | bytes 9199616 | tf_op jit(solution)/shard_map/while/body/eval_jaxpr/btkrd,bpkd->btkrp/dot_general | solution.py:44
  226.6 3.8 fusion.72
  231.6 3.9 copy.105
  235.5 4.3 %fusion.73 = f32[8,32,8,3,64]{4,1,3,2,0:T(8,128)S(1)} fusion(bf16[8,256,8,64,1]{1,3,4,2,0:T(8,128)(2,1)} %bitcast.139, f32[8,8,256,32,3]{2,3,4,1,0:T(8,128)} %get-tuple-element.150, f32[8,32,8,3]{1,3,2,0:T(4,128)S(1)} %copy.103), kind=kOutput, calls=%fused_computation.11.clone.1 | convolution fusion | flops 206045184 | bytes 9986048 | tf_op jit(solution)/shard_map/while/body/eval_jaxpr/btkrp,bpkd->btkrd/dot_general | solution.py:144
  239.8 1.8 copy.106
  243.3 1.6 copy-done.2
  245.0 3.2 copy.87
  249.8 4.0 multiply_reduce_fusion.1
  256.2 9.2 %all_gather.13 = s32[2048,8]{0,1:T(8,128)S(1)} all-gather(s32[256,8]{0,1:T(8,128)S(1)} %copy-done.8), channel_id=1, replica_groups=mesh['req'=4,'exp'=8] {'exp'}, dimensions={0}, use_global_device_ids=true | all-gather | bytes 73728 | tf_op jit(solution)/shard_map/all_gather | solution.py:173
  265.4 8.3 %all_gather.14 = f32[2048,8]{0,1:T(8,128)S(1)} all-gather(f32[256,8]{0,1:T(8,128)S(1)} %copy-done.9), channel_id=1, replica_groups=mesh['req'=4,'exp'=8] {'exp'}, dimensions={0}, use_global_device_ids=true | all-gather | bytes 73728 | tf_op jit(solution)/shard_map/all_gather | solution.py:174
  273.8 29.0 %all-gather.5.cloned.1.call-done = bf16[2048,1536]{1,0:T(8,128)(2,1)} async-done(((bf16[256,1536]{1,0:T(8,128)(2,1)}), bf16[2048,1536]{1,0:T(8,128)(2,1)}) %all-gather.5.cloned.1.call-update) | async-done | bytes 6291472 | tf_op jit(solution)/shard_map/all_gather | solution.py:172
  302.8 19.4 %convolution_bitcast_fusion = f32[2,2048,1024]{2,1,0:T(8,128)} fusion(bf16[2,1536,1024]{2,1,0:T(8,128)(2,1)} %param.30, bf16[2048,1536]{1,0:T(8,128)(2,1)} %all-gather.5.cloned.1.call-done), kind=kOutput, calls=%fused_computation.29 | convolution fusion | flops 12884901888 | bytes 29360128 | tf_op jit(solution)/shard_map/td,edf->etf/dot_general | solution.py:184
  322.2 15.1 %multiply_reduce_fusion = bf16[2048,1536]{1,0:T(8,128)(2,1)} fusion(f32[2,2048]{1,0:T(2,128)S(1)} %select_reduce_fusion, bf16[2,512,1536]{2,1,0:T(8,128)(2,1)S(1)} %copy-done, f32[2,2048,1024]{2,1,0:T(8,128)} %convolution_bitcast_fusion), kind=kOutput, calls=%fused_computation.19 | convolution fusion | flops 6477053952 | bytes 26230784 | tf_op jit(solution)/shard_map/etf,efd->etd/dot_general | solution.py:186
  337.3 62.0 %reduce-scatter.2.cloned.1.call-done = bf16[256,1536]{1,0:T(8,128)(2,1)} async-done(((bf16[2048,1536]{1,0:T(8,128)(2,1)}), bf16[256,1536]{1,0:T(8,128)(2,1)}) %reduce-scatter.2.cloned.1.call-update) | async-done | bytes 786448 | tf_op jit(solution)/shard_map/reduce_scatter | solution.py:190
  399.3 2.7 add_convert_fusion
  (118 shorter events, 15.8 us)
Async XLA Ops:
  6.5 315.6 %copy-start = (bf16[2,512,1536]{2,1,0:T(8,128)(2,1)S(1)}, bf16[2,512,1536]{2,1,0:T(8,128)(2,1)}, u32[]{:S(2)}) copy-start(bf16[2,512,1536]{2,1,0:T(8,128)(2,1)} %param.31) | copy-start | bytes 9437188
  6.5 81.9 %all-gather.3.cloned.1.call-start = ((), (), s32[]{:S(2)}) async-start(), calls=%async_computation.1 | async-start | bytes 5242880 | tf_op jit(solution)/shard_map/all_gather | solution.py:121
  7.3 295.5 %all-gather.5.cloned.1.call-start = ((), (), s32[]{:S(2)}) async-start(), calls=%async_computation.2 | async-start | bytes 7077888 | tf_op jit(solution)/shard_map/all_gather | solution.py:172
  24.8 10.6 %copy-start.11 = (s32[8]{0:T(128)S(1)}, s32[8]{0:T(128)}, u32[]{:S(2)}) copy-start(s32[8]{0:T(128)} %param.23) | copy-start | bytes 100
  24.8 10.7 %copy-start.10 = (s32[8,32]{1,0:T(8,128)S(1)}, s32[8,32]{1,0:T(8,128)}, u32[]{:S(2)}) copy-start(s32[8,32]{1,0:T(8,128)} %param.24) | copy-start | bytes 3076
  32.6 4.4 %copy-start.6 = (bf16[8,32,1024]{1,2,0:T(8,128)(2,1)S(1)}, bf16[8,32,1024]{1,2,0:T(8,128)(2,1)}, u32[]{:S(2)}) copy-start(bf16[8,32,1024]{1,2,0:T(8,128)(2,1)} %copy.80) | copy-start | bytes 1572868
  35.4 5.2 %copy-start.3 = (bf16[8,32,8,3,64]{4,1,3,2,0:T(8,128)(2,1)}, bf16[8,32,8,3,64]{4,1,3,2,0:T(8,128)(2,1)S(1)}, u32[]{:S(2)}) copy-start(bf16[8,32,8,3,64]{4,1,3,2,0:T(8,128)(2,1)S(1)} %copy.81) | copy-start | bytes 2359300
  56.8 31.6 %copy-start.12 = (s32[8]{0:T(128)S(1)}, s32[8]{0:T(128)}, u32[]{:S(2)}) copy-start(s32[8]{0:T(128)} %param.25) | copy-start | bytes 100
  122.3 1.9 copy-start.1
  122.3 2.0 copy-start.4
  125.9 1.7 copy-start.2
  161.5 1.9 copy-start.1
  161.5 2.0 copy-start.4
  165.0 1.7 copy-start.2
  200.6 1.9 copy-start.1
  200.6 2.0 copy-start.4
  204.2 1.7 copy-start.2
  239.8 1.9 copy-start.1
  239.8 2.0 copy-start.4
  243.3 1.7 copy-start.2
  249.8 5.2 %copy-start.7 = (f32[1536]{0:T(1024)S(1)}, f32[1536]{0:T(1024)}, u32[]{:S(2)}) copy-start(f32[1536]{0:T(1024)} %param.27) | copy-start | bytes 18436
  249.8 6.4 %copy-start.8 = (s32[256,8]{0,1:T(8,128)S(1)}, s32[256,8]{0,1:T(8,128)}, u32[]{:S(2)}) copy-start(s32[256,8]{0,1:T(8,128)} %param.28) | copy-start | bytes 24580
  249.8 15.6 %copy-start.9 = (f32[256,8]{0,1:T(8,128)S(1)}, f32[256,8]{0,1:T(8,128)}, u32[]{:S(2)}) copy-start(f32[256,8]{0,1:T(8,128)} %param.29) | copy-start | bytes 24580
  253.9 1.2 copy-start.5
  256.1 143.2 %reduce-scatter.2.cloned.1.call-start = ((), (), s32[]{:S(2)}) async-start(), calls=%async_computation.3 | async-start | bytes 7077888 | tf_op jit(solution)/shard_map/reduce_scatter | solution.py:190
Sparse Core Ops, SparseCore 0:
  8.9 79.4 all-gather.2
  256.2 46.5 all-gather.4
  337.4 61.8 reduce-scatter.1

commit v2 on v1

v2 whole, which is shorter than its diff:
```python
import math

import jax
import jax.numpy as jnp
from jax import lax
from jax.experimental import pallas as pl
from jax.experimental.pallas import tpu as pltpu
from jax.sharding import PartitionSpec as P

D = 1536
QUERY_HEADS = 24
KEY_VALUE_HEADS = 8
HEAD_WIDTH = 64
FF = 512
TOPK = 8
TREE_TOKENS = 32
GROUPS_PER_COLUMN = 2
PAGE_POSITIONS = 64
MAXP = 6


def ancestry(parent_rows):
    tree_size = parent_rows.shape[1]
    positions = jnp.arange(tree_size, dtype=jnp.int32)
    linked = (parent_rows[:, :, None] == positions[None, None, :]).astype(jnp.float32)
    reach = jnp.eye(tree_size, dtype=jnp.float32)[None] + linked
    for sweep in range((tree_size - 1).bit_length()):
        reach = jnp.minimum(
            jnp.einsum("bij,bjk->bik", reach, reach, precision=lax.Precision.HIGHEST),
            jnp.float32(1.0),
        )
    return reach > 0.5


def attention_kernel(groups_ref, pages_ref, lengths_ref, queries_ref, tree_ref, visible_ref, prompt_ref, *rest):
    page_refs = rest[:MAXP]
    out_ref = rest[MAXP]
    request = pl.program_id(0)
    key_value_width = KEY_VALUE_HEADS * HEAD_WIDTH
    heads_repeated = QUERY_HEADS // KEY_VALUE_HEADS
    rows = heads_repeated * TREE_TOKENS
    scale_factor = HEAD_WIDTH ** (-0.5)
    tree_visible = jnp.concatenate([visible_ref[0]] * heads_repeated, 0) > 0.5
    positions = lax.broadcasted_iota(jnp.int32, (rows, MAXP * PAGE_POSITIONS), 1)
    cache_visible = positions < lengths_ref[request]
    contract = (((1,), (1,)), ((), ()))

    for kv in range(KEY_VALUE_HEADS):
        key_at = kv * HEAD_WIDTH
        value_at = key_value_width + kv * HEAD_WIDTH
        query_rows = jnp.concatenate(
            [
                queries_ref[:, (kv * heads_repeated + j) * HEAD_WIDTH : (kv * heads_repeated + j + 1) * HEAD_WIDTH]
                for j in range(heads_repeated)
            ],
            0,
        )
        prompt_keys = prompt_ref[0, :, key_at : key_at + HEAD_WIDTH]
        prompt_values = prompt_ref[0, :, value_at : value_at + HEAD_WIDTH]
        cache_keys = jnp.concatenate([p[0, :, key_at : key_at + HEAD_WIDTH] for p in page_refs], 0)
        cache_values = jnp.concatenate([p[0, :, value_at : value_at + HEAD_WIDTH] for p in page_refs], 0)
        tree_keys = tree_ref[:, key_at : key_at + HEAD_WIDTH]
        tree_values = tree_ref[:, value_at : value_at + HEAD_WIDTH]
        prompt_scores = lax.dot_general(query_rows, prompt_keys, contract, preferred_element_type=jnp.float32) * scale_factor
        cache_scores = lax.dot_general(query_rows, cache_keys, contract, preferred_element_type=jnp.float32) * scale_factor
        tree_scores = lax.dot_general(query_rows, tree_keys, contract, preferred_element_type=jnp.float32) * scale_factor
        cache_scores = jnp.where(cache_visible, cache_scores, -jnp.inf)
        tree_scores = jnp.where(tree_visible, tree_scores, -jnp.inf)
        peak = jnp.maximum(
            jnp.maximum(jnp.max(prompt_scores, -1, keepdims=True), jnp.max(cache_scores, -1, keepdims=True)),
            jnp.max(tree_scores, -1, keepdims=True),
        )
        prompt_exp = jnp.exp(prompt_scores - peak)
        cache_exp = jnp.exp(cache_scores - peak)
        tree_exp = jnp.exp(tree_scores - peak)
        denom = (
            jnp.sum(prompt_exp, -1, keepdims=True)
            + jnp.sum(cache_exp, -1, keepdims=True)
            + jnp.sum(tree_exp, -1, keepdims=True)
        )
        numer = (
            jnp.dot(prompt_exp.astype(jnp.bfloat16), prompt_values, preferred_element_type=jnp.float32)
            + jnp.dot(cache_exp.astype(jnp.bfloat16), cache_values, preferred_element_type=jnp.float32)
            + jnp.dot(tree_exp.astype(jnp.bfloat16), tree_values, preferred_element_type=jnp.float32)
        )
        result = (numer / denom).astype(jnp.bfloat16)
        for j in range(heads_repeated):
            head = kv * heads_repeated + j
            out_ref[:, head * HEAD_WIDTH : (head + 1) * HEAD_WIDTH] = result[j * TREE_TOKENS : (j + 1) * TREE_TOKENS]


def attend(queries, draft_kv, piece, cache_page_store, page_table, cache_len, parents, groups):
    count_of_tokens, width = queries.shape
    count_of_requests = page_table.shape[0]
    row_width = draft_kv.shape[1]
    store_pages = cache_page_store.shape[0]
    visible = ancestry(parents).astype(jnp.float32)
    flat_pages = jnp.clip(page_table.reshape(-1), 0, store_pages - 1).astype(jnp.int32)
    prompt_groups = jnp.clip(groups, 0, piece.shape[0] - 1).astype(jnp.int32)

    def page_spec(slot):
        return pl.BlockSpec(
            (1, PAGE_POSITIONS, row_width), lambda r, g, p, c: (p[r * MAXP + slot], 0, 0)
        )

    grid_spec = pltpu.PrefetchScalarGridSpec(
        num_scalar_prefetch=3,
        grid=(count_of_requests,),
        in_specs=[
            pl.BlockSpec((TREE_TOKENS, width), lambda r, g, p, c: (r, 0)),
            pl.BlockSpec((TREE_TOKENS, row_width), lambda r, g, p, c: (r, 0)),
            pl.BlockSpec((1, TREE_TOKENS, TREE_TOKENS), lambda r, g, p, c: (r, 0, 0)),
            pl.BlockSpec((1, piece.shape[1], row_width), lambda r, g, p, c: (g[r], 0, 0)),
        ]
        + [page_spec(slot) for slot in range(MAXP)],
        out_specs=pl.BlockSpec((TREE_TOKENS, width), lambda r, g, p, c: (r, 0)),
    )
    return pl.pallas_call(
        attention_kernel,
        grid_spec=grid_spec,
        out_shape=jax.ShapeDtypeStruct((count_of_tokens, width), jnp.bfloat16),
    )(prompt_groups, flat_pages, cache_len.astype(jnp.int32), queries, draft_kv, visible, piece, *([cache_page_store] * MAXP))


def per_device(
    resid,
    queries,
    draft_kv,
    prompt_key_value,
    cache_page_store,
    page_table,
    cache_len,
    parents,
    groups,
    w_out,
    norm_gain,
    routes,
    route_weight,
    w_in,
    w_down,
):
    piece = lax.all_gather(prompt_key_value, "req", axis=1, tiled=True)
    attended = attend(queries, draft_kv, piece, cache_page_store, page_table, cache_len, parents, groups)
    mixed = resid.astype(jnp.float32) + jnp.dot(attended, w_out, preferred_element_type=jnp.float32)
    spread = jnp.mean(mixed * mixed, -1, keepdims=True)
    normed = (mixed * lax.rsqrt(spread + 1e-05) * norm_gain).astype(jnp.bfloat16)
    local_experts = w_in.shape[0]
    first_expert = lax.axis_index("exp") * local_experts
    gathered = lax.all_gather(normed, "exp", axis=0, tiled=True)
    gathered_routes = lax.all_gather(routes, "exp", axis=0, tiled=True)
    gathered_weights = lax.all_gather(route_weight, "exp", axis=0, tiled=True)
    expert_ids = first_expert + jnp.arange(local_experts, dtype=jnp.int32)
    gate = jnp.sum(
        jnp.where(
            gathered_routes[None, :, :] == expert_ids[:, None, None],
            gathered_weights[None, :, :],
            jnp.float32(0.0),
        ),
        -1,
    )
    both = jnp.einsum("td,edf->etf", gathered, w_in, preferred_element_type=jnp.float32)
    act = (jax.nn.silu(both[..., :FF]) * both[..., FF:]).astype(jnp.bfloat16)
    result = jnp.einsum("etf,efd->etd", act, w_down, preferred_element_type=jnp.float32).astype(
        jnp.bfloat16
    )
    partial = jnp.sum(gate[..., None] * result.astype(jnp.float32), 0)
    blended = lax.psum_scatter(
        partial.astype(jnp.bfloat16), "exp", scatter_dimension=0, tiled=True
    ).astype(jnp.float32)
    return (mixed + blended).astype(jnp.bfloat16)


def solution(mesh):
    in_specs = (
        P(("req", "exp"), None),
        P(("req", "exp"), None),
        P(("req", "exp"), None),
        P("exp", "req", None),
        P(("req", "exp"), None, None),
        P(("req", "exp"), None),
        P(("req", "exp")),
        P(("req", "exp"), None),
        P(("req", "exp")),
        P(),
        P(),
        P(("req", "exp"), None),
        P(("req", "exp"), None),
        P("exp", None, None),
        P("exp", None, None),
    )
    out_specs = P(("req", "exp"), None)
    return jax.shard_map(
        per_device, mesh=mesh, in_specs=in_specs, out_specs=out_specs, check_vma=False
    )
```

time: 412 us -> 285 us (0.69)
  local copies, waits for them, and re-layouts: 130 us -> 1.82 us
  matrix products: 92.4 us -> 41.4 us
  waiting for transfers between devices: 116 us -> 167 us
  Pallas kernels: 0 us -> 35.7 us
  other arithmetic: 38.5 us -> 5.92 us
    dot_general x10 -> x0, matrix products: 52.5 us -> none  [the longest x4 22.7 us: prompt_scores(): jnp.einsum('btkrd,bpkd->btkrp', queries_per_request, key_matrix, preferre...]
    all_gather x1, waiting for transfers between devices: 24.5 us -> 75.5 us  [per_device(): piece = lax.all_gather(prompt_key_value, 'req', axis=1, tiled=True)]
    slice x12 -> x0, local copies, waits for them, and re-layouts: 49.5 us -> none  [the longest x8 33.9 us: prompt_scores(): selected_entries[..., key_value_width:]]
    pallas_call x0 -> x1, Pallas kernels: none -> 35.7 us  [attend(): pl.pallas_call(attention_kernel, grid_spec=grid_spec, out_shape=jax.Shape...]
    gather x5 -> x0, local copies, waits for them, and re-layouts: 23.6 us -> none  [the longest x4 15.9 us: prompt_scores(): selected_entries = piece[request_groups]]
    reduce_sum x5 -> x0, other arithmetic: 22.1 us -> none  [the longest x4 15.3 us: advance(): jnp.sum(expd, -1).reshape(count_of_tokens, KEY_VALUE_HEADS, heads_repeated)]
    reshape x11 -> x0, local copies, waits for them, and re-layouts: 12.2 us -> none  [the longest x1 8.76 us: per_device(): cache_page_store[page_table]]
    transpose x5 -> x0, local copies, waits for them, and re-layouts: 10.6 us -> none  [the longest x4 7.15 us: advance(): jnp.einsum('btkrp,bpkd->btkrd', expd.astype(jnp.bfloat16), value_matrix,...]
  transfers between devices with their start and end apart: 3 -> 3, of which waited for: 3 -> 3; matrix products, arithmetic and copies ran while one was open for 14% -> 2% of each run, Pallas kernels for 0% -> 0%
where the time goes in v2:
time: 285 us; the launch traced here: 283 us
  waiting for transfers between devices  167 us (59%)
  matrix products  41.4 us (15%)
  Pallas kernels  35.7 us (13%)
  blocking collectives  17.7 us (6%)
  between operations  13.2 us (5%)
  other arithmetic  5.92 us (2%)
    all_gather x1, waiting for transfers between devices, per_device(): piece = lax.all_gather(prompt_key_value, 'req', axis=1, tiled=True)  75.5 us
    reduce_scatter x1, waiting for transfers between devices, per_device(): lax.psum_scatter(partial.astype(jnp.bfloat16), 'exp', scatter_dimension=0...  62.1 us
    pallas_call x1, Pallas kernels, attend(): pl.pallas_call(attention_kernel, grid_spec=grid_spec, out_shape=jax.Shape...  35.7 us
    all_gather x1, waiting for transfers between devices, per_device(): gathered = lax.all_gather(normed, 'exp', axis=0, tiled=True)  28.8 us
    dot_general x1, matrix products, per_device(): jnp.einsum('td,edf->etf', gathered, w_in, preferred_element_type=jnp.floa...  19.4 us
    dot_general x1, matrix products, per_device(): jnp.einsum('etf,efd->etd', act, w_down, preferred_element_type=jnp.float32)  15 us
    all_gather x1, blocking collectives, per_device(): gathered_routes = lax.all_gather(routes, 'exp', axis=0, tiled=True)  9.19 us
    all_gather x1, blocking collectives, per_device(): gathered_weights = lax.all_gather(route_weight, 'exp', axis=0, tiled=True)  8.46 us
  transfers between devices with their start and end apart: 3, of which 3 were waited for; matrix products, arithmetic and copies ran while one was open for 2% of the time, Pallas kernels for 0%

profile of v2, /device:TPU:12, one launch (start us, length us, event | category | flops | bytes accessed | tf_op | source)
XLA Modules:
  0.0 283.0 jit_solution(9934508662630071719)
XLA Ops:
  6.5 0.0 copy-start
  6.5 0.0 all-gather.3.cloned.1.call-start
  6.5 0.7 all-gather.3.cloned.1.call-update
  7.3 0.0 all-gather.5.cloned.1.call-start
  7.3 0.9 broadcast_clamp_fusion
  8.2 0.7 min.37.pages_ref
  8.9 1.2 broadcast_clamp_fusion.1.groups_ref
  10.0 1.1 convolution_minimum_fusion.4
  11.2 0.3 convolution_minimum_fusion.3
  11.4 0.3 convolution_minimum_fusion.2
  11.7 0.3 convolution_minimum_fusion.1
  11.9 0.9 fusion.5.visible_ref
  12.8 75.5 %all-gather.3.cloned.1.call-done.prompt_ref = bf16[2,1024,1024]{2,1,0:T(8,128)(2,1)} async-done(((bf16[2,256,1024]{2,1,0:T(8,128)(2,1)}), bf16[2,1024,1024]{2,1,0:T(8,128)(2,1)}) %all-gather.3.cloned.1.call-update) | async-done | bytes 4194320 | tf_op jit(solution)/shard_map/all_gather | solution.py:142
  88.4 35.7 %shard_map.145 = bf16[256,1536]{1,0:T(8,128)(2,1)} custom-call(s32[8]{0:T(128)} %broadcast_clamp_fusion.1.groups_ref, s32[48]{0:T(128)} %min.37.pages_ref, s32[8]{0:T(128)} %lengths_ref.1, bf16[256,1536]{1,0:T(8,128)(2,1)} %queries_ref.1, bf16[256,1024]{1,0:T(8,128)(2,1)} %tree_ref.1, f32[8,32,32]{2,1,0:T(8,128)} %fusion.5.visible_ref, ...), custom_call_target="tpu_custom_call" | custom-call | tf_op jit(solution)/shard_map/pallas_call | solution.py:118
  124.1 0.0 copy-start.2
  124.1 0.0 copy-start.3
  124.1 0.0 copy-start.4
  124.1 4.3 %multiply_reduce_fusion.1 = (f32[256]{0:T(256)S(1)}, f32[256,1536]{1,0:T(8,128)S(1)}) fusion(bf16[256,1536]{1,0:T(8,128)(2,1)} %shard_map.145, bf16[1536,1536]{1,0:T(8,128)(2,1)} %param.24, bf16[256,1536]{1,0:T(8,128)(2,1)} %param.15), kind=kOutput, calls=%fused_computation.9 | convolution fusion | flops 1209532160 | bytes 7865344 | tf_op jit(solution)/shard_map/dot_general | solution.py:144
  128.4 0.0 copy-start.1
  128.4 1.1 copy-done.1
  129.5 0.0 copy-done.2
  129.5 1.1 multiply_convert_fusion
  130.6 0.0 all-gather.5.cloned.1.call-update
  130.6 0.0 reduce-scatter.2.cloned.1.call-start
  130.7 0.0 copy-done.3
  130.7 9.2 %all_gather.13 = s32[2048,8]{0,1:T(8,128)S(1)} all-gather(s32[256,8]{0,1:T(8,128)S(1)} %copy-done.3), channel_id=1, replica_groups=mesh['req'=4,'exp'=8] {'exp'}, dimensions={0}, use_global_device_ids=true | all-gather | bytes 73728 | tf_op jit(solution)/shard_map/all_gather | solution.py:150
  139.9 0.0 copy-done.4
  139.9 8.5 %all_gather.14 = f32[2048,8]{0,1:T(8,128)S(1)} all-gather(f32[256,8]{0,1:T(8,128)S(1)} %copy-done.4), channel_id=1, replica_groups=mesh['req'=4,'exp'=8] {'exp'}, dimensions={0}, use_global_device_ids=true | all-gather | bytes 73728 | tf_op jit(solution)/shard_map/all_gather | solution.py:151
  148.3 0.1 select_reduce_fusion
  148.5 28.8 %all-gather.5.cloned.1.call-done = bf16[2048,1536]{1,0:T(8,128)(2,1)} async-done(((bf16[256,1536]{1,0:T(8,128)(2,1)}), bf16[2048,1536]{1,0:T(8,128)(2,1)}) %all-gather.5.cloned.1.call-update) | async-done | bytes 6291472 | tf_op jit(solution)/shard_map/all_gather | solution.py:149
  177.3 19.4 %convolution_bitcast_fusion = f32[2,2048,1024]{2,1,0:T(8,128)} fusion(bf16[2,1536,1024]{2,1,0:T(8,128)(2,1)} %param.28, bf16[2048,1536]{1,0:T(8,128)(2,1)} %all-gather.5.cloned.1.call-done), kind=kOutput, calls=%fused_computation.3 | convolution fusion | flops 12884901888 | bytes 29360128 | tf_op jit(solution)/shard_map/td,edf->etf/dot_general | solution.py:161
  196.7 0.0 copy-done
  196.7 15.0 %multiply_reduce_fusion = bf16[2048,1536]{1,0:T(8,128)(2,1)} fusion(f32[2,2048]{1,0:T(2,128)S(1)} %select_reduce_fusion, bf16[2,512,1536]{2,1,0:T(8,128)(2,1)S(1)} %copy-done, f32[2,2048,1024]{2,1,0:T(8,128)} %convolution_bitcast_fusion), kind=kOutput, calls=%fused_computation | convolution fusion | flops 6477053952 | bytes 26230784 | tf_op jit(solution)/shard_map/etf,efd->etd/dot_general | solution.py:163
  211.7 0.0 reduce-scatter.2.cloned.1.call-update
  211.7 62.1 %reduce-scatter.2.cloned.1.call-done = bf16[256,1536]{1,0:T(8,128)(2,1)} async-done(((bf16[2048,1536]{1,0:T(8,128)(2,1)}), bf16[256,1536]{1,0:T(8,128)(2,1)}) %reduce-scatter.2.cloned.1.call-update) | async-done | bytes 786448 | tf_op jit(solution)/shard_map/reduce_scatter | solution.py:167
  273.8 2.7 add_convert_fusion
  (3 shorter events, 0.0 us)
Async XLA Ops:
  6.5 190.1 %copy-start = (bf16[2,512,1536]{2,1,0:T(8,128)(2,1)S(1)}, bf16[2,512,1536]{2,1,0:T(8,128)(2,1)}, u32[]{:S(2)}) copy-start(bf16[2,512,1536]{2,1,0:T(8,128)(2,1)} %param.29) | copy-start | bytes 9437188
  6.5 81.9 %all-gather.3.cloned.1.call-start = ((), (), s32[]{:S(2)}) async-start(), calls=%async_computation.1 | async-start | bytes 5242880 | tf_op jit(solution)/shard_map/all_gather | solution.py:142
  7.3 170.0 %all-gather.5.cloned.1.call-start = ((), (), s32[]{:S(2)}) async-start(), calls=%async_computation.2 | async-start | bytes 7077888 | tf_op jit(solution)/shard_map/all_gather | solution.py:149
  124.1 5.4 %copy-start.2 = (f32[1536]{0:T(1024)S(1)}, f32[1536]{0:T(1024)}, u32[]{:S(2)}) copy-start(f32[1536]{0:T(1024)} %param.25) | copy-start | bytes 18436
  124.1 6.6 %copy-start.3 = (s32[256,8]{0,1:T(8,128)S(1)}, s32[256,8]{0,1:T(8,128)}, u32[]{:S(2)}) copy-start(s32[256,8]{0,1:T(8,128)} %param.26) | copy-start | bytes 24580
  124.1 15.8 %copy-start.4 = (f32[256,8]{0,1:T(8,128)S(1)}, f32[256,8]{0,1:T(8,128)}, u32[]{:S(2)}) copy-start(f32[256,8]{0,1:T(8,128)} %param.27) | copy-start | bytes 24580
  128.4 1.1 copy-start.1
  130.6 143.2 %reduce-scatter.2.cloned.1.call-start = ((), (), s32[]{:S(2)}) async-start(), calls=%async_computation.3 | async-start | bytes 7077888 | tf_op jit(solution)/shard_map/reduce_scatter | solution.py:167
Sparse Core Ops, SparseCore 0:
  8.9 79.4 all-gather.2
  130.7 46.5 all-gather.4
  211.8 61.9 reduce-scatter.1

commit v3 on v2

--- a/solution.py
+++ b/solution.py
@@ -139,34 +139,41 @@
     w_in,
     w_down,
 ):
+    local_experts = w_in.shape[0]
+    exp_devices = lax.axis_size("exp")
+    experts_all = local_experts * exp_devices
+    count_of_tokens = routes.shape[0]
+    every_expert = jnp.arange(experts_all, dtype=jnp.int32)
+    gate_local = jnp.sum(
+        jnp.where(routes[:, :, None] == every_expert[None, None, :], route_weight[:, :, None], jnp.float32(0.0)),
+        1,
+    )
+    gate_gathered = lax.all_gather(gate_local, "exp", axis=0, tiled=True)
+    gate = lax.dynamic_slice_in_dim(gate_gathered, lax.axis_index("exp") * local_experts, local_experts, 1)
+    gate = gate.reshape(exp_devices, count_of_tokens, local_experts)
     piece = lax.all_gather(prompt_key_value, "req", axis=1, tiled=True)
+    gate, piece = lax.optimization_barrier((gate, piece))
     attended = attend(queries, draft_kv, piece, cache_page_store, page_table, cache_len, parents, groups)
     mixed = resid.astype(jnp.float32) + jnp.dot(attended, w_out, preferred_element_type=jnp.float32)
     spread = jnp.mean(mixed * mixed, -1, keepdims=True)
     normed = (mixed * lax.rsqrt(spread + 1e-05) * norm_gain).astype(jnp.bfloat16)
-    local_experts = w_in.shape[0]
-    first_expert = lax.axis_index("exp") * local_experts
-    gathered = lax.all_gather(normed, "exp", axis=0, tiled=True)
-    gathered_routes = lax.all_gather(routes, "exp", axis=0, tiled=True)
-    gathered_weights = lax.all_gather(route_weight, "exp", axis=0, tiled=True)
-    expert_ids = first_expert + jnp.arange(local_experts, dtype=jnp.int32)
-    gate = jnp.sum(
-        jnp.where(
-            gathered_routes[None, :, :] == expert_ids[:, None, None],
-            gathered_weights[None, :, :],
-            jnp.float32(0.0),
-        ),
-        -1,
-    )
-    both = jnp.einsum("td,edf->etf", gathered, w_in, preferred_element_type=jnp.float32)
-    act = (jax.nn.silu(both[..., :FF]) * both[..., FF:]).astype(jnp.bfloat16)
-    result = jnp.einsum("etf,efd->etd", act, w_down, preferred_element_type=jnp.float32).astype(
-        jnp.bfloat16
-    )
-    partial = jnp.sum(gate[..., None] * result.astype(jnp.float32), 0)
-    blended = lax.psum_scatter(
-        partial.astype(jnp.bfloat16), "exp", scatter_dimension=0, tiled=True
-    ).astype(jnp.float32)
+    chunks = 2 if count_of_tokens % 16 == 0 else 1
+    span = count_of_tokens // chunks
+    pieces = []
+    for chunk in range(chunks):
+        rows = normed[chunk * span : (chunk + 1) * span]
+        gathered = lax.all_gather(rows, "exp", axis=0, tiled=True)
+        chunk_gate = gate[:, chunk * span : (chunk + 1) * span].reshape(exp_devices * span, local_experts)
+        both = jnp.einsum("td,edf->etf", gathered, w_in, preferred_element_type=jnp.float32)
+        act = (jax.nn.silu(both[..., :FF]) * both[..., FF:]).astype(jnp.bfloat16)
+        result = jnp.einsum("etf,efd->etd", act, w_down, preferred_element_type=jnp.float32).astype(
+            jnp.bfloat16
+        )
+        partial = jnp.sum(jnp.transpose(chunk_gate)[..., None] * result.astype(jnp.float32), 0)
+        pieces.append(
+            lax.psum_scatter(partial.astype(jnp.bfloat16), "exp", scatter_dimension=0, tiled=True)
+        )
+    blended = jnp.concatenate(pieces, 0).astype(jnp.float32)
     return (mixed + blended).astype(jnp.bfloat16)
 
 

time: 285 us -> 309 us (1.084)
  waiting for transfers between devices: 167 us -> 189 us
  matrix products: 41.4 us -> 50.5 us
  blocking collectives: 17.7 us -> 9.22 us
    all_gather x1 -> x2, waiting for transfers between devices: 28.8 us -> 45.1 us  [per_device(): gathered = lax.all_gather(rows, 'exp', axis=0, tiled=True)]
    reduce_scatter x1 -> x2, waiting for transfers between devices: 62.1 us -> 77.4 us  [per_device(): lax.psum_scatter(partial.astype(jnp.bfloat16), 'exp', scatter_dimension=0...]
    all_gather x1, waiting for transfers between devices: 75.5 us -> 65.6 us  [per_device(): piece = lax.all_gather(prompt_key_value, 'req', axis=1, tiled=True)]
    all_gather x2 -> x1, blocking collectives: 17.7 us -> 9.22 us  [per_device(): gate_gathered = lax.all_gather(gate_local, 'exp', axis=0, tiled=True)]
    dot_general x1 -> x2, matrix products: 15 us -> 19.9 us  [per_device(): jnp.einsum('etf,efd->etd', act, w_down, preferred_element_type=jnp.float32)]
    dot_general x1 -> x2, matrix products: 19.4 us -> 23.5 us  [per_device(): jnp.einsum('td,edf->etf', gathered, w_in, preferred_element_type=jnp.floa...]
  transfers between devices with their start and end apart: 3 -> 5, of which waited for: 3 -> 5; matrix products, arithmetic and copies ran while one was open for 2% -> 16% of each run, Pallas kernels for 0% -> 0%
where the time goes in v3:
time: 309 us; the launch traced here: 307 us
  waiting for transfers between devices  189 us (61%)
  matrix products  50.5 us (16%)
  Pallas kernels  35.7 us (12%)
  between operations  13.2 us (4%)
  blocking collectives  9.22 us (3%)
  other arithmetic  5.63 us (2%)
    reduce_scatter x2, waiting for transfers between devices, per_device(): lax.psum_scatter(partial.astype(jnp.bfloat16), 'exp', scatter_dimension=0...  77.4 us
    all_gather x1, waiting for transfers between devices, per_device(): piece = lax.all_gather(prompt_key_value, 'req', axis=1, tiled=True)  65.6 us
    all_gather x2, waiting for transfers between devices, per_device(): gathered = lax.all_gather(rows, 'exp', axis=0, tiled=True)  45.1 us
    pallas_call x1, Pallas kernels, attend(): pl.pallas_call(attention_kernel, grid_spec=grid_spec, out_shape=jax.Shape...  35.7 us
    dot_general x2, matrix products, per_device(): jnp.einsum('td,edf->etf', gathered, w_in, preferred_element_type=jnp.floa...  23.5 us
    dot_general x2, matrix products, per_device(): jnp.einsum('etf,efd->etd', act, w_down, preferred_element_type=jnp.float32)  19.9 us
    all_gather x1, blocking collectives, per_device(): gate_gathered = lax.all_gather(gate_local, 'exp', axis=0, tiled=True)  9.22 us
  transfers between devices with their start and end apart: 5, of which 5 were waited for; matrix products, arithmetic and copies ran while one was open for 16% of the time, Pallas kernels for 0%

profile of v3, /device:TPU:12, one launch (start us, length us, event | category | flops | bytes accessed | tf_op | source)
XLA Modules:
  0.0 306.9 jit_solution(8917135854961957662)
XLA Ops:
  6.5 0.0 copy-start
  6.5 0.0 all-gather.4.cloned.1.call-start
  6.5 0.7 all-gather.4.cloned.1.call-update
  7.3 0.0 all-gather.6.cloned.1.call-start
  7.3 0.9 select_reduce_fusion
  8.2 9.2 %all_gather.12 = f32[2048,16]{0,1:T(8,128)S(1)} all-gather(f32[256,16]{0,1:T(8,128)S(1)} %select_reduce_fusion), channel_id=1, replica_groups=mesh['req'=4,'exp'=8] {'exp'}, dimensions={0}, use_global_device_ids=true | all-gather | bytes 147456 | tf_op jit(solution)/shard_map/all_gather | solution.py:151
  17.5 0.7 broadcast_clamp_fusion
  18.2 0.7 min.37.pages_ref
  18.8 1.2 broadcast_clamp_fusion.1.groups_ref
  20.0 1.1 convolution_minimum_fusion.4
  21.2 0.3 convolution_minimum_fusion.3
  21.4 0.3 convolution_minimum_fusion.2
  21.7 0.3 convolution_minimum_fusion.1
  21.9 0.9 fusion.9.visible_ref
  22.8 65.6 %all-gather.4.cloned.1.call-done.prompt_ref = bf16[2,1024,1024]{2,1,0:T(8,128)(2,1)} async-done(((bf16[2,256,1024]{2,1,0:T(8,128)(2,1)}), bf16[2,1024,1024]{2,1,0:T(8,128)(2,1)}) %all-gather.4.cloned.1.call-update) | async-done | bytes 4194320 | tf_op jit(solution)/shard_map/all_gather | solution.py:154
  88.4 35.7 %shard_map.145 = bf16[256,1536]{1,0:T(8,128)(2,1)} custom-call(s32[8]{0:T(128)} %broadcast_clamp_fusion.1.groups_ref, s32[48]{0:T(128)} %min.37.pages_ref, s32[8]{0:T(128)} %lengths_ref.1, bf16[256,1536]{1,0:T(8,128)(2,1)} %queries_ref.1, bf16[256,1024]{1,0:T(8,128)(2,1)} %tree_ref.1, f32[8,32,32]{2,1,0:T(8,128)} %fusion.9.visible_ref, ...), custom_call_target="tpu_custom_call" | custom-call | tf_op jit(solution)/shard_map/pallas_call | solution.py:118
  124.1 0.0 copy-start.2
  124.1 4.3 %multiply_reduce_fusion.2 = (f32[256]{0:T(256)S(1)}, f32[256,1536]{1,0:T(8,128)S(1)}) fusion(bf16[256,1536]{1,0:T(8,128)(2,1)} %shard_map.145, bf16[1536,1536]{1,0:T(8,128)(2,1)} %param.24, bf16[256,1536]{1,0:T(8,128)(2,1)} %param.15), kind=kOutput, calls=%fused_computation.15 | convolution fusion | flops 1209532160 | bytes 7865344 | tf_op jit(solution)/shard_map/dot_general | solution.py:157
  128.3 0.0 copy-start.1
  128.4 1.1 copy-done.1
  129.5 0.0 copy-done.2
  129.5 0.2 multiply_convert_fusion
  129.7 0.9 fusion.17
  130.6 0.0 all-gather.6.cloned.1.call-update
  130.7 0.0 all-gather.8.cloned.1.call-start
  130.7 0.7 all-gather.8.cloned.1.call-update
  131.4 0.2 reduce-scatter.3.cloned.1.call-start
  131.7 32.3 %all-gather.6.cloned.1.call-done = bf16[1024,1536]{1,0:T(8,128)(2,1)} async-done(((bf16[128,1536]{1,0:T(8,128)(2,1)}), bf16[1024,1536]{1,0:T(8,128)(2,1)}) %all-gather.6.cloned.1.call-update) | async-done | bytes 3145744 | tf_op jit(solution)/shard_map/all_gather | solution.py:165
  164.0 11.8 %convolution_bitcast_fusion.1 = f32[2,1024,1024]{2,1,0:T(8,128)} fusion(bf16[2,1536,1024]{2,1,0:T(8,128)(2,1)} %param.28, bf16[1024,1536]{1,0:T(8,128)(2,1)} %all-gather.6.cloned.1.call-done), kind=kOutput, calls=%fused_computation.7 | convolution fusion | flops 6442450944 | bytes 17825792 | tf_op jit(solution)/shard_map/td,edf->etf/dot_general | solution.py:167
  175.8 0.0 copy-done
  175.8 9.7 %multiply_reduce_fusion.1 = bf16[1024,1536]{1,0:T(8,128)(2,1)} fusion(f32[2,1024]{1,0:T(2,128)S(1)} %bitcast.52, bf16[2,512,1536]{2,1,0:T(8,128)(2,1)S(1)} %copy-done, f32[2,1024,1024]{2,1,0:T(8,128)} %convolution_bitcast_fusion.1), kind=kOutput, calls=%fused_computation.1 | convolution fusion | flops 3238526976 | bytes 14688256 | tf_op jit(solution)/shard_map/etf,efd->etd/dot_general | solution.py:169
  185.4 0.0 reduce-scatter.3.cloned.1.call-update
  185.5 0.0 reduce-scatter.5.cloned.1.call-start
  185.5 12.7 %all-gather.8.cloned.1.call-done = bf16[1024,1536]{1,0:T(8,128)(2,1)} async-done(((bf16[128,1536]{1,0:T(8,128)(2,1)}), bf16[1024,1536]{1,0:T(8,128)(2,1)}) %all-gather.8.cloned.1.call-update) | async-done | bytes 3145744 | tf_op jit(solution)/shard_map/all_gather | solution.py:165
  198.2 11.8 %convolution_bitcast_fusion = f32[2,1024,1024]{2,1,0:T(8,128)} fusion(bf16[2,1536,1024]{2,1,0:T(8,128)(2,1)} %param.28, bf16[1024,1536]{1,0:T(8,128)(2,1)} %all-gather.8.cloned.1.call-done), kind=kOutput, calls=%fused_computation.6 | convolution fusion | flops 6442450944 | bytes 17825792 | tf_op jit(solution)/shard_map/td,edf->etf/dot_general | solution.py:167
  210.0 10.3 %multiply_reduce_fusion = bf16[1024,1536]{1,0:T(8,128)(2,1)} fusion(f32[2,1024]{1,0:T(2,128)S(1)} %bitcast.53, bf16[2,512,1536]{2,1,0:T(8,128)(2,1)S(1)} %copy-done, f32[2,1024,1024]{2,1,0:T(8,128)} %convolution_bitcast_fusion), kind=kOutput, calls=%fused_computation | convolution fusion | flops 3238526976 | bytes 14688256 | tf_op jit(solution)/shard_map/etf,efd->etd/dot_general | solution.py:169
  220.3 0.0 reduce-scatter.5.cloned.1.call-update
  220.3 27.5 %reduce-scatter.3.cloned.1.call-done = bf16[128,1536]{1,0:T(8,128)(2,1)} async-done(((bf16[1024,1536]{1,0:T(8,128)(2,1)}), bf16[128,1536]{1,0:T(8,128)(2,1)}) %reduce-scatter.3.cloned.1.call-update) | async-done | bytes 393232 | tf_op jit(solution)/shard_map/reduce_scatter | solution.py:174
  247.8 49.9 %reduce-scatter.5.cloned.1.call-done = bf16[128,1536]{1,0:T(8,128)(2,1)} async-done(((bf16[1024,1536]{1,0:T(8,128)(2,1)}), bf16[128,1536]{1,0:T(8,128)(2,1)}) %reduce-scatter.5.cloned.1.call-update) | async-done | bytes 393232 | tf_op jit(solution)/shard_map/reduce_scatter | solution.py:174
  297.7 2.6 add_convert_fusion
  (7 shorter events, 0.0 us)
Async XLA Ops:
  6.5 169.2 %copy-start = (bf16[2,512,1536]{2,1,0:T(8,128)(2,1)S(1)}, bf16[2,512,1536]{2,1,0:T(8,128)(2,1)}, u32[]{:S(2)}) copy-start(bf16[2,512,1536]{2,1,0:T(8,128)(2,1)} %param.29) | copy-start | bytes 9437188
  6.5 81.9 %all-gather.4.cloned.1.call-start = ((), (), s32[]{:S(2)}) async-start(), calls=%async_computation.2 | async-start | bytes 5242880 | tf_op jit(solution)/shard_map/all_gather | solution.py:154
  7.3 156.7 %all-gather.6.cloned.1.call-start = ((), (), s32[]{:S(2)}) async-start(), calls=%async_computation.3 | async-start | bytes 3538944 | tf_op jit(solution)/shard_map/all_gather | solution.py:165
  124.1 5.4 %copy-start.2 = (f32[1536]{0:T(1024)S(1)}, f32[1536]{0:T(1024)}, u32[]{:S(2)}) copy-start(f32[1536]{0:T(1024)} %param.25) | copy-start | bytes 18436
  128.3 1.2 copy-start.1
  130.7 67.6 %all-gather.8.cloned.1.call-start = ((), (), s32[]{:S(2)}) async-start(), calls=%async_computation.5 | async-start | bytes 3538944 | tf_op jit(solution)/shard_map/all_gather | solution.py:165
  131.4 116.4 %reduce-scatter.3.cloned.1.call-start = ((), (), s32[]{:S(2)}) async-start(), calls=%async_computation.4 | async-start | bytes 3538944 | tf_op jit(solution)/shard_map/reduce_scatter | solution.py:174
  185.5 112.2 %reduce-scatter.5.cloned.1.call-start = ((), (), s32[]{:S(2)}) async-start(), calls=%async_computation.6 | async-start | bytes 3538944 | tf_op jit(solution)/shard_map/reduce_scatter | solution.py:174
Sparse Core Ops, SparseCore 0:
  8.9 79.4 all-gather.3
  130.8 33.1 all-gather.5
  165.9 32.3 all-gather.7
  201.5 46.3 reduce-scatter.2
  251.4 46.2 reduce-scatter.4

commit v4 on v3

--- a/solution.py
+++ b/solution.py
@@ -157,7 +157,7 @@
     mixed = resid.astype(jnp.float32) + jnp.dot(attended, w_out, preferred_element_type=jnp.float32)
     spread = jnp.mean(mixed * mixed, -1, keepdims=True)
     normed = (mixed * lax.rsqrt(spread + 1e-05) * norm_gain).astype(jnp.bfloat16)
-    chunks = 2 if count_of_tokens % 16 == 0 else 1
+    chunks = 1
     span = count_of_tokens // chunks
     pieces = []
     for chunk in range(chunks):

time: 309 us -> 285 us (0.922)
  waiting for transfers between devices: 189 us -> 175 us
  matrix products: 50.5 us -> 41.5 us
    reduce_scatter x2 -> x1, waiting for transfers between devices: 77.4 us -> 62.1 us  [per_device(): lax.psum_scatter(partial.astype(jnp.bfloat16), 'exp', scatter_dimension=0...]
    dot_general x2 -> x1, matrix products: 19.9 us -> 15 us  [per_device(): jnp.einsum('etf,efd->etd', act, w_down, preferred_element_type=jnp.float32)]
    dot_general x2 -> x1, matrix products: 23.5 us -> 19.4 us  [per_device(): jnp.einsum('td,edf->etf', gathered, w_in, preferred_element_type=jnp.floa...]
    all_gather x2 -> x1, waiting for transfers between devices: 45.1 us -> 46.2 us  [per_device(): gathered = lax.all_gather(rows, 'exp', axis=0, tiled=True)]
  transfers between devices with their start and end apart: 5 -> 3, of which waited for: 5 -> 3; matrix products, arithmetic and copies ran while one was open for 16% -> 2% of each run, Pallas kernels for 0% -> 0%
where the time goes in v4:
time: 285 us; the launch traced here: 283 us
  waiting for transfers between devices  175 us (61%)
  matrix products  41.5 us (15%)
  Pallas kernels  35.7 us (13%)
  between operations  13.2 us (5%)
  blocking collectives  9.22 us (3%)
  other arithmetic  6.52 us (2%)
    all_gather x1, waiting for transfers between devices, per_device(): piece = lax.all_gather(prompt_key_value, 'req', axis=1, tiled=True)  65.6 us
    reduce_scatter x1, waiting for transfers between devices, per_device(): lax.psum_scatter(partial.astype(jnp.bfloat16), 'exp', scatter_dimension=0...  62.1 us
    all_gather x1, waiting for transfers between devices, per_device(): gathered = lax.all_gather(rows, 'exp', axis=0, tiled=True)  46.2 us
    pallas_call x1, Pallas kernels, attend(): pl.pallas_call(attention_kernel, grid_spec=grid_spec, out_shape=jax.Shape...  35.7 us
    dot_general x1, matrix products, per_device(): jnp.einsum('td,edf->etf', gathered, w_in, preferred_element_type=jnp.floa...  19.4 us
    dot_general x1, matrix products, per_device(): jnp.einsum('etf,efd->etd', act, w_down, preferred_element_type=jnp.float32)  15 us
    all_gather x1, blocking collectives, per_device(): gate_gathered = lax.all_gather(gate_local, 'exp', axis=0, tiled=True)  9.22 us
  transfers between devices with their start and end apart: 3, of which 3 were waited for; matrix products, arithmetic and copies ran while one was open for 2% of the time, Pallas kernels for 0%

profile of v4, /device:TPU:12, one launch (start us, length us, event | category | flops | bytes accessed | tf_op | source)
XLA Modules:
  0.0 282.7 jit_solution(8322116891396178342)
XLA Ops:
  6.5 0.0 copy-start
  6.5 0.0 all-gather.3.cloned.1.call-start
  6.5 0.7 all-gather.3.cloned.1.call-update
  7.3 0.0 all-gather.5.cloned.1.call-start
  7.3 0.9 broadcast_clamp_fusion
  8.2 0.7 min.37.pages_ref
  8.8 0.7 select_reduce_fusion
  9.6 9.2 %all_gather.9 = f32[2048,16]{0,1:T(8,128)S(1)} all-gather(f32[256,16]{0,1:T(8,128)S(1)} %select_reduce_fusion), channel_id=1, replica_groups=mesh['req'=4,'exp'=8] {'exp'}, dimensions={0}, use_global_device_ids=true | all-gather | bytes 147456 | tf_op jit(solution)/shard_map/all_gather | solution.py:151
  18.8 1.2 broadcast_clamp_fusion.1.groups_ref
  20.0 1.1 convolution_minimum_fusion.4
  21.1 0.3 convolution_minimum_fusion.3
  21.4 0.3 convolution_minimum_fusion.2
  21.6 0.3 convolution_minimum_fusion.1
  21.9 0.9 fusion.5.visible_ref
  22.8 65.6 %all-gather.3.cloned.1.call-done.prompt_ref = bf16[2,1024,1024]{2,1,0:T(8,128)(2,1)} async-done(((bf16[2,256,1024]{2,1,0:T(8,128)(2,1)}), bf16[2,1024,1024]{2,1,0:T(8,128)(2,1)}) %all-gather.3.cloned.1.call-update) | async-done | bytes 4194320 | tf_op jit(solution)/shard_map/all_gather | solution.py:154
  88.4 35.7 %shard_map.145 = bf16[256,1536]{1,0:T(8,128)(2,1)} custom-call(s32[8]{0:T(128)} %broadcast_clamp_fusion.1.groups_ref, s32[48]{0:T(128)} %min.37.pages_ref, s32[8]{0:T(128)} %lengths_ref.1, bf16[256,1536]{1,0:T(8,128)(2,1)} %queries_ref.1, bf16[256,1024]{1,0:T(8,128)(2,1)} %tree_ref.1, f32[8,32,32]{2,1,0:T(8,128)} %fusion.5.visible_ref, ...), custom_call_target="tpu_custom_call" | custom-call | tf_op jit(solution)/shard_map/pallas_call | solution.py:118
  124.1 0.0 copy-start.2
  124.1 4.3 %multiply_reduce_fusion.1 = (f32[256]{0:T(256)S(1)}, f32[256,1536]{1,0:T(8,128)S(1)}) fusion(bf16[256,1536]{1,0:T(8,128)(2,1)} %shard_map.145, bf16[1536,1536]{1,0:T(8,128)(2,1)} %param.24, bf16[256,1536]{1,0:T(8,128)(2,1)} %param.15), kind=kOutput, calls=%fused_computation.9 | convolution fusion | flops 1209532160 | bytes 7865344 | tf_op jit(solution)/shard_map/dot_general | solution.py:157
  128.4 0.0 copy-start.1
  128.4 1.1 copy-done.1
  129.5 0.0 copy-done.2
  129.5 1.1 multiply_convert_fusion
  130.6 0.0 all-gather.5.cloned.1.call-update
  130.6 0.2 reduce-scatter.2.cloned.1.call-start
  130.9 46.2 %all-gather.5.cloned.1.call-done = bf16[2048,1536]{1,0:T(8,128)(2,1)} async-done(((bf16[256,1536]{1,0:T(8,128)(2,1)}), bf16[2048,1536]{1,0:T(8,128)(2,1)}) %all-gather.5.cloned.1.call-update) | async-done | bytes 6291472 | tf_op jit(solution)/shard_map/all_gather | solution.py:165
  177.0 19.4 %convolution_bitcast_fusion = f32[2,2048,1024]{2,1,0:T(8,128)} fusion(bf16[2,1536,1024]{2,1,0:T(8,128)(2,1)} %param.28, bf16[2048,1536]{1,0:T(8,128)(2,1)} %all-gather.5.cloned.1.call-done), kind=kOutput, calls=%fused_computation.3 | convolution fusion | flops 12884901888 | bytes 29360128 | tf_op jit(solution)/shard_map/td,edf->etf/dot_general | solution.py:167
  196.4 0.0 copy-done
  196.4 15.0 %multiply_reduce_fusion = bf16[2048,1536]{1,0:T(8,128)(2,1)} fusion(f32[2,2048]{1,0:T(2,128)S(1)} %bitcast.30, bf16[2,512,1536]{2,1,0:T(8,128)(2,1)S(1)} %copy-done, f32[2,2048,1024]{2,1,0:T(8,128)} %convolution_bitcast_fusion), kind=kOutput, calls=%fused_computation | convolution fusion | flops 6477053952 | bytes 26230784 | tf_op jit(solution)/shard_map/etf,efd->etd/dot_general | solution.py:169
  211.4 0.0 reduce-scatter.2.cloned.1.call-update
  211.5 62.1 %reduce-scatter.2.cloned.1.call-done = bf16[256,1536]{1,0:T(8,128)(2,1)} async-done(((bf16[2048,1536]{1,0:T(8,128)(2,1)}), bf16[256,1536]{1,0:T(8,128)(2,1)}) %reduce-scatter.2.cloned.1.call-update) | async-done | bytes 786448 | tf_op jit(solution)/shard_map/reduce_scatter | solution.py:174
  273.5 2.7 add_convert_fusion
  (5 shorter events, 0.0 us)
Async XLA Ops:
  6.5 189.9 %copy-start = (bf16[2,512,1536]{2,1,0:T(8,128)(2,1)S(1)}, bf16[2,512,1536]{2,1,0:T(8,128)(2,1)}, u32[]{:S(2)}) copy-start(bf16[2,512,1536]{2,1,0:T(8,128)(2,1)} %param.29) | copy-start | bytes 9437188
  6.5 81.9 %all-gather.3.cloned.1.call-start = ((), (), s32[]{:S(2)}) async-start(), calls=%async_computation.1 | async-start | bytes 5242880 | tf_op jit(solution)/shard_map/all_gather | solution.py:154
  7.3 169.8 %all-gather.5.cloned.1.call-start = ((), (), s32[]{:S(2)}) async-start(), calls=%async_computation.2 | async-start | bytes 7077888 | tf_op jit(solution)/shard_map/all_gather | solution.py:165
  124.1 5.4 %copy-start.2 = (f32[1536]{0:T(1024)S(1)}, f32[1536]{0:T(1024)}, u32[]{:S(2)}) copy-start(f32[1536]{0:T(1024)} %param.25) | copy-start | bytes 18436
  128.4 1.2 copy-start.1
  130.6 142.9 %reduce-scatter.2.cloned.1.call-start = ((), (), s32[]{:S(2)}) async-start(), calls=%async_computation.3 | async-start | bytes 7077888 | tf_op jit(solution)/shard_map/reduce_scatter | solution.py:174
Sparse Core Ops, SparseCore 0:
  8.9 79.4 all-gather.2
  130.7 46.2 all-gather.4
  211.6 61.9 reduce-scatter.1

commit v5 on v4

--- a/solution.py
+++ b/solution.py
@@ -120,6 +120,48 @@
         grid_spec=grid_spec,
         out_shape=jax.ShapeDtypeStruct((count_of_tokens, width), jnp.bfloat16),
     )(prompt_groups, flat_pages, cache_len.astype(jnp.int32), queries, draft_kv, visible, piece, *([cache_page_store] * MAXP))
+
+
+def run_experts(rows, row_gate, w_in, w_down):
+    both = jnp.einsum("td,edf->etf", rows, w_in, preferred_element_type=jnp.float32)
+    act = (jax.nn.silu(both[..., :FF]) * both[..., FF:]).astype(jnp.bfloat16)
+    result = jnp.einsum("etf,efd->etd", act, w_down, preferred_element_type=jnp.float32).astype(jnp.bfloat16)
+    return jnp.sum(jnp.transpose(row_gate)[..., None] * result.astype(jnp.float32), 0)
+
+
+def exchange_experts(normed, gate, w_in, w_down):
+    devices = lax.axis_size("exp")
+    count_of_tokens, width = normed.shape
+    if devices % 2 != 0:
+        rows = lax.all_gather(normed, "exp", axis=0, tiled=True)
+        partial = run_experts(rows, gate, w_in, w_down)
+        return lax.psum_scatter(partial.astype(jnp.bfloat16), "exp", scatter_dimension=0, tiled=True).astype(jnp.float32)
+    half = devices // 2
+    me = lax.axis_index("exp")
+    core = me % 2
+    chip = me // 2
+
+    def chip_shift(x, shift):
+        pairs = [(2 * c + b, 2 * ((c + shift) % half) + b) for c in range(half) for b in range(2)]
+        return lax.ppermute(x, "exp", pairs)
+
+    def sibling(x):
+        return lax.ppermute(x, "exp", [(i, i ^ 1) for i in range(devices)])
+
+    same_core = jnp.stack([normed] + [chip_shift(normed, d) for d in range(1, half)], 0)
+    other_core = sibling(same_core)
+    rows = jnp.concatenate([same_core, other_core], 0).reshape(devices * count_of_tokens, width)
+    chip_of = (chip - jnp.arange(half, dtype=jnp.int32)) % half
+    device_of = jnp.concatenate([2 * chip_of + core, 2 * chip_of + (1 - core)])
+    row_gate = jnp.take(gate.reshape(devices, count_of_tokens, -1), device_of, axis=0).reshape(
+        devices * count_of_tokens, -1
+    )
+    partial = run_experts(rows, row_gate, w_in, w_down).reshape(2, half, count_of_tokens, width)
+    merged = partial[0] + sibling(partial[1].astype(jnp.bfloat16)).astype(jnp.float32)
+    total = merged[0]
+    for d in range(1, half):
+        total = total + chip_shift(merged[d].astype(jnp.bfloat16), -d).astype(jnp.float32)
+    return total
 
 
 def per_device(
@@ -150,30 +192,13 @@
     )
     gate_gathered = lax.all_gather(gate_local, "exp", axis=0, tiled=True)
     gate = lax.dynamic_slice_in_dim(gate_gathered, lax.axis_index("exp") * local_experts, local_experts, 1)
-    gate = gate.reshape(exp_devices, count_of_tokens, local_experts)
     piece = lax.all_gather(prompt_key_value, "req", axis=1, tiled=True)
     gate, piece = lax.optimization_barrier((gate, piece))
     attended = attend(queries, draft_kv, piece, cache_page_store, page_table, cache_len, parents, groups)
     mixed = resid.astype(jnp.float32) + jnp.dot(attended, w_out, preferred_element_type=jnp.float32)
     spread = jnp.mean(mixed * mixed, -1, keepdims=True)
     normed = (mixed * lax.rsqrt(spread + 1e-05) * norm_gain).astype(jnp.bfloat16)
-    chunks = 1
-    span = count_of_tokens // chunks
-    pieces = []
-    for chunk in range(chunks):
-        rows = normed[chunk * span : (chunk + 1) * span]
-        gathered = lax.all_gather(rows, "exp", axis=0, tiled=True)
-        chunk_gate = gate[:, chunk * span : (chunk + 1) * span].reshape(exp_devices * span, local_experts)
-        both = jnp.einsum("td,edf->etf", gathered, w_in, preferred_element_type=jnp.float32)
-        act = (jax.nn.silu(both[..., :FF]) * both[..., FF:]).astype(jnp.bfloat16)
-        result = jnp.einsum("etf,efd->etd", act, w_down, preferred_element_type=jnp.float32).astype(
-            jnp.bfloat16
-        )
-        partial = jnp.sum(jnp.transpose(chunk_gate)[..., None] * result.astype(jnp.float32), 0)
-        pieces.append(
-            lax.psum_scatter(partial.astype(jnp.bfloat16), "exp", scatter_dimension=0, tiled=True)
-        )
-    blended = jnp.concatenate(pieces, 0).astype(jnp.float32)
+    blended = exchange_experts(normed, gate, w_in, w_down)
     return (mixed + blended).astype(jnp.bfloat16)
 
 

time: 285 us -> 284 us (level); the launches traced: 283 us -> 279 us
  waiting for transfers between devices: 175 us -> 141 us
  local copies, waits for them, and re-layouts: 1.83 us -> 17.6 us
  starting transfers between devices: 0.26 us -> 7.07 us
  other arithmetic: 6.52 us -> 12.4 us
    ppermute x0 -> x8, waiting for transfers between devices: none -> 74.3 us  [the longest x6 69 us: chip_shift(): return lax.ppermute(x, 'exp', pairs)]
    reduce_scatter x1 -> x0, waiting for transfers between devices: 62.1 us -> none  [per_device(): lax.psum_scatter(partial.astype(jnp.bfloat16), 'exp', scatter_dimension=0...]
    all_gather x1 -> x0, waiting for transfers between devices: 46.2 us -> none  [per_device(): gathered = lax.all_gather(rows, 'exp', axis=0, tiled=True)]
    unnamed x8 -> x17, local copies, waits for them, and re-layouts: 1.16 us -> 9.19 us
    ppermute x0 -> x8, starting transfers between devices: none -> 7.07 us  [the longest x6 6.51 us: chip_shift(): return lax.ppermute(x, 'exp', pairs)]
    another operation x0 -> x2, other arithmetic: none -> 5.21 us
    concatenate x0 -> x1, local copies, waits for them, and re-layouts: none -> 3.77 us  [exchange_experts(): jnp.concatenate([same_core, other_core], 0)]
    slice x0 -> x3, local copies, waits for them, and re-layouts: none -> 3.17 us  [the longest x1 3.16 us: exchange_experts(): partial[1].astype(jnp.bfloat16)]
  transfers between devices with their start and end apart: 3 -> 9, of which waited for: 3 -> 7; matrix products, arithmetic and copies ran while one was open for 2% -> 5% of each run, Pallas kernels for 0% -> 0%
where the time goes in v5:
time: 284 us; the launch traced here: 279 us
  waiting for transfers between devices  141 us (50%)
  matrix products  42.7 us (15%)
  Pallas kernels  35.7 us (13%)
  local copies, waits for them, and re-layouts  17.6 us (6%)
  between operations  13.5 us (5%)
  other arithmetic  12.4 us (4%)
  blocking collectives  9.22 us (3%)
  starting transfers between devices  7.07 us (2%)
    ppermute x6, waiting for transfers between devices, chip_shift(): return lax.ppermute(x, 'exp', pairs)  69 us
    all_gather x1, waiting for transfers between devices, per_device(): piece = lax.all_gather(prompt_key_value, 'req', axis=1, tiled=True)  65.6 us
    pallas_call x1, Pallas kernels, attend(): pl.pallas_call(attention_kernel, grid_spec=grid_spec, out_shape=jax.Shape...  35.7 us
    dot_general x1, matrix products, run_experts(): jnp.einsum('td,edf->etf', rows, w_in, preferred_element_type=jnp.float32)  19.4 us
    dot_general x1, matrix products, run_experts(): jnp.einsum('etf,efd->etd', act, w_down, preferred_element_type=jnp.float32)  16.3 us
    all_gather x1, blocking collectives, per_device(): gate_gathered = lax.all_gather(gate_local, 'exp', axis=0, tiled=True)  9.22 us
    unnamed x17, local copies, waits for them, and re-layouts  9.19 us
    ppermute x6, starting transfers between devices, chip_shift(): return lax.ppermute(x, 'exp', pairs)  6.51 us
  transfers between devices with their start and end apart: 9, of which 7 were waited for; matrix products, arithmetic and copies ran while one was open for 5% of the time, Pallas kernels for 0%

profile of v5, /device:TPU:12, one launch (start us, length us, event | category | flops | bytes accessed | tf_op | source)
XLA Modules:
  0.0 278.8 jit_solution(970145627981944896)
XLA Ops:
  6.5 0.0 copy-start
  6.5 0.0 all-gather.2.cloned.1.call-start
  6.5 0.7 all-gather.2.cloned.1.call-update
  7.3 0.9 broadcast_clamp_fusion
  8.2 0.6 min.37.pages_ref
  8.8 0.7 select_reduce_fusion
  9.5 9.2 %all_gather.6 = f32[2048,16]{0,1:T(8,128)S(1)} all-gather(f32[256,16]{0,1:T(8,128)S(1)} %select_reduce_fusion), channel_id=1, replica_groups=mesh['req'=4,'exp'=8] {'exp'}, dimensions={0}, use_global_device_ids=true | all-gather | bytes 147456 | tf_op jit(solution)/shard_map/all_gather | solution.py:193
  18.7 1.2 broadcast_clamp_fusion.1.groups_ref
  20.0 1.1 convolution_minimum_fusion.4
  21.1 0.3 convolution_minimum_fusion.3
  21.4 0.3 convolution_minimum_fusion.2
  21.6 0.3 convolution_minimum_fusion.1
  21.9 0.9 fusion.9.visible_ref
  22.8 65.6 %all-gather.2.cloned.1.call-done.prompt_ref = bf16[2,1024,1024]{2,1,0:T(8,128)(2,1)} async-done(((bf16[2,256,1024]{2,1,0:T(8,128)(2,1)}), bf16[2,1024,1024]{2,1,0:T(8,128)(2,1)}) %all-gather.2.cloned.1.call-update) | async-done | bytes 4194320 | tf_op jit(solution)/shard_map/all_gather | solution.py:195
  88.4 35.7 %shard_map.145 = bf16[256,1536]{1,0:T(8,128)(2,1)} custom-call(s32[8]{0:T(128)} %broadcast_clamp_fusion.1.groups_ref, s32[48]{0:T(128)} %min.37.pages_ref, s32[8]{0:T(128)} %lengths_ref.1, bf16[256,1536]{1,0:T(8,128)(2,1)} %queries_ref.1, bf16[256,1024]{1,0:T(8,128)(2,1)} %tree_ref.1, f32[8,32,32]{2,1,0:T(8,128)} %fusion.9.visible_ref, ...), custom_call_target="tpu_custom_call" | custom-call | tf_op jit(solution)/shard_map/pallas_call | solution.py:118
  124.1 0.0 copy-start.6
  124.1 4.3 %multiply_reduce_fusion.1 = (f32[256]{0:T(256)S(1)}, f32[256,1536]{1,0:T(8,128)S(1)}) fusion(bf16[256,1536]{1,0:T(8,128)(2,1)} %shard_map.145, bf16[1536,1536]{1,0:T(8,128)(2,1)} %param.24, bf16[256,1536]{1,0:T(8,128)(2,1)} %param.15), kind=kOutput, calls=%fused_computation.17 | convolution fusion | flops 1209532160 | bytes 7865344 | tf_op jit(solution)/shard_map/dot_general | solution.py:198
  128.4 0.0 copy-start.1
  128.4 1.2 copy-done.1
  129.6 0.0 copy-done.6
  129.6 1.1 constant_dynamic-update-slice_fusion.4
  130.7 1.5 collective-permute-start.2
  132.1 1.5 collective-permute-start.1
  133.6 0.0 collective-permute-start
  133.6 17.5 %collective-permute-done.2 = bf16[256,1536]{1,0:T(8,128)(2,1)S(1)} collective-permute-done((bf16[256,1536]{1,0:T(8,128)(2,1)S(1)}, bf16[256,1536]{1,0:T(8,128)(2,1)S(1)}, u32[]{:S(2)}, u32[]{:S(2)}) %collective-permute-start.2) | collective-permute-done | bytes 786464 | tf_op jit(solution)/shard_map/ppermute | solution.py:146
  151.1 0.0 copy-start.3
  151.1 16.9 %collective-permute-done.1 = bf16[256,1536]{1,0:T(8,128)(2,1)S(1)} collective-permute-done((bf16[256,1536]{1,0:T(8,128)(2,1)S(1)}, bf16[256,1536]{1,0:T(8,128)(2,1)S(1)}, u32[]{:S(2)}, u32[]{:S(2)}) %collective-permute-start.1) | collective-permute-done | bytes 786464 | tf_op jit(solution)/shard_map/ppermute | solution.py:146
  168.0 0.0 copy-start.4
  168.0 0.0 collective-permute-done
  168.0 0.0 copy-start.5
  168.0 0.0 copy-done.3
  168.0 2.1 pad_maximum_fusion
  170.1 0.0 copy-done.4
  170.1 0.1 copy-done.5
  170.2 0.0 collective-permute-start.3
  170.2 0.1 compare_and_fusion
  170.3 0.1 broadcast_in_dim.37
  170.4 0.1 fusion.17
  170.4 0.6 gather_fusion
  171.0 2.1 constant_dynamic-update-slice_fusion.3
  173.1 2.1 constant_dynamic-update-slice_fusion.2
  175.2 2.1 constant_dynamic-update-slice_fusion.1
  177.3 0.0 collective-permute-done.3
  177.3 3.8 %constant_dynamic-update-slice_fusion = bf16[8,256,1536]{2,1,0:T(8,128)(2,1)} fusion(bf16[8,256,1536]{2,1,0:T(8,128)(2,1)} %constant_dynamic-update-slice_fusion.1, bf16[4,256,1536]{2,1,0:T(8,128)(2,1)} %collective-permute-done.3), kind=kLoop, calls=%fused_computation.38 | loop fusion | bytes 6291456 | tf_op jit(solution)/shard_map/concatenate | solution.py:153
  181.1 19.4 %convolution_bitcast_fusion = f32[2,2048,1024]{2,1,0:T(8,128)} fusion(bf16[2048,1536,1]{1,0,2:T(8,128)(2,1)} %bitcast.62, bf16[2,1536,1024]{2,1,0:T(8,128)(2,1)} %param.28), kind=kOutput, calls=%fused_computation.4 | convolution fusion | flops 12884901888 | bytes 29360128 | tf_op jit(solution)/shard_map/td,edf->etf/dot_general | solution.py:126
  200.4 0.0 copy-done
  200.4 16.3 %multiply_reduce_fusion = f32[2048,1536]{1,0:T(8,128)} fusion(f32[2,2048]{1,0:T(2,128)S(1)} %select_bitcast_fusion, bf16[2,512,1536]{2,1,0:T(8,128)(2,1)S(1)} %copy-done, f32[2,2048,1024]{2,1,0:T(8,128)} %convolution_bitcast_fusion), kind=kOutput, calls=%fused_computation.1 | convolution fusion | flops 6477053952 | bytes 32522240 | tf_op jit(solution)/shard_map/etf,efd->etd/dot_general | solution.py:128
  216.7 3.2 %slice.69 = bf16[1024,1536]{1,0:T(8,128)(2,1)S(1)} slice(f32[2048,1536]{1,0:T(8,128)} %multiply_reduce_fusion), slice={[1024:2048], [0:1536]} | slice | bytes 6291456 | tf_op jit(solution)/shard_map/slice | solution.py:160
  219.9 0.0 slice-start
  219.9 0.6 collective-permute-start.4
  220.5 5.3 %collective-permute-done.4 = bf16[4,256,1536]{2,1,0:T(8,128)(2,1)S(1)} collective-permute-done((bf16[4,256,1536]{2,1,0:T(8,128)(2,1)S(1)}, bf16[4,256,1536]{2,1,0:T(8,128)(2,1)S(1)}, u32[]{:S(2)}, u32[]{:S(2)}) %collective-permute-start.4) | collective-permute-done | bytes 3145760 | tf_op jit(solution)/shard_map/ppermute | solution.py:149
  225.8 0.0 copy-start.2
  225.8 1.7 copy-done.2
  227.4 0.0 slice-done
  227.4 3.1 %fusion.19 = (bf16[4,256,1536]{2,1,0:T(8,128)(2,1)S(1)}, f32[4,256,1536]{2,1,0:T(8,128)S(1)}) fusion(f32[4,256,1536]{2,1,0:T(8,128)S(1)} %bitcast.56, bf16[4,256,1536]{2,1,0:T(8,128)(2,1)} %copy-done.2), kind=kLoop, calls=%fused_computation.60 | loop fusion | flops 4718592 | bytes 18874368 | tf_op jit(solution)/shard_map/convert.2
  230.6 0.2 slice_bitcast_fusion.3
  230.8 1.1 collective-permute-start.5
  231.8 1.0 collective-permute-start.7
  232.8 1.5 collective-permute-start.6
  234.3 16.9 %collective-permute-done.5 = bf16[256,1536]{1,0:T(8,128)(2,1)S(1)} collective-permute-done((bf16[256,1536]{1,0:T(8,128)(2,1)S(1)}, bf16[256,1536]{1,0:T(8,128)(2,1)S(1)}, u32[]{:S(2)}, u32[]{:S(2)}) %collective-permute-start.5) | collective-permute-done | bytes 786464 | tf_op jit(solution)/shard_map/ppermute | solution.py:146
  251.2 17.3 %collective-permute-done.7 = bf16[256,1536]{1,0:T(8,128)(2,1)S(1)} collective-permute-done((bf16[256,1536]{1,0:T(8,128)(2,1)S(1)}, bf16[256,1536]{1,0:T(8,128)(2,1)S(1)}, u32[]{:S(2)}, u32[]{:S(2)}) %collective-permute-start.7) | collective-permute-done | bytes 786464 | tf_op jit(solution)/shard_map/ppermute | solution.py:146
  268.5 0.4 collective-permute-done.6
  268.9 3.0 %fusion.7 = bf16[256,1536]{1,0:T(8,128)(2,1)} fusion(f32[256,1536]{1,0:T(8,128)} %copy-done.1, f32[4,256,1536]{2,1,0:T(8,128)S(1)} %get-tuple-element.10, bf16[256,1536]{1,0:T(8,128)(2,1)S(1)} %collective-permute-done.7, bf16[256,1536]{1,0:T(8,128)(2,1)S(1)} %collective-permute-done.6, bf16[256,1536]{1,0:T(8,128)(2,1)S(1)} %collective-permute-done.5), kind=kLoop, calls=%fused_computation.15 | loop fusion | flops 3145728 | bytes 6291456 | tf_op jit(solution)/shard_map/convert_element_type | solution.py:202
  (7 shorter events, 0.1 us)
Async XLA Ops:
  6.5 193.9 %copy-start = (bf16[2,512,1536]{2,1,0:T(8,128)(2,1)S(1)}, bf16[2,512,1536]{2,1,0:T(8,128)(2,1)}, u32[]{:S(2)}) copy-start(bf16[2,512,1536]{2,1,0:T(8,128)(2,1)} %param.29) | copy-start | bytes 9437188
  6.5 81.9 %all-gather.2.cloned.1.call-start = ((), (), s32[]{:S(2)}) async-start(), calls=%async_computation | async-start | bytes 5242880 | tf_op jit(solution)/shard_map/all_gather | solution.py:195
  124.1 5.5 %copy-start.6 = (f32[1536]{0:T(1024)S(1)}, f32[1536]{0:T(1024)}, u32[]{:S(2)}) copy-start(f32[1536]{0:T(1024)} %param.25) | copy-start | bytes 18436
  128.4 1.2 copy-start.1
  130.7 20.4 %collective-permute-start.2 = (bf16[256,1536]{1,0:T(8,128)(2,1)S(1)}, bf16[256,1536]{1,0:T(8,128)(2,1)S(1)}, u32[]{:S(2)}, u32[]{:S(2)}) collective-permute-start(bf16[256,1536]{1,0:T(8,128)(2,1)S(1)} %get-tuple-element.12), channel_id=1, source_target_pairs={{0,6},{1,7},{2,0},{3,1},{4,2},{5,3},{6,4},{7,5},{8,14},{9,15},{10,... | collective-permute-start | bytes 2359304 | tf_op jit(solution)/shard_map/ppermute | solution.py:146
  132.1 35.8 %collective-permute-start.1 = (bf16[256,1536]{1,0:T(8,128)(2,1)S(1)}, bf16[256,1536]{1,0:T(8,128)(2,1)S(1)}, u32[]{:S(2)}, u32[]{:S(2)}) collective-permute-start(bf16[256,1536]{1,0:T(8,128)(2,1)S(1)} %get-tuple-element.12), channel_id=1, source_target_pairs={{0,4},{1,5},{2,6},{3,7},{4,0},{5,1},{6,2},{7,3},{8,12},{9,13},{10,... | collective-permute-start | bytes 2359304 | tf_op jit(solution)/shard_map/ppermute | solution.py:146
  133.6 34.4 %collective-permute-start = (bf16[256,1536]{1,0:T(8,128)(2,1)S(1)}, bf16[256,1536]{1,0:T(8,128)(2,1)S(1)}, u32[]{:S(2)}, u32[]{:S(2)}) collective-permute-start(bf16[256,1536]{1,0:T(8,128)(2,1)S(1)} %get-tuple-element.12), channel_id=1, source_target_pairs={{0,2},{1,3},{2,4},{3,5},{4,6},{5,7},{6,0},{7,1},{8,10},{9,11},{10,... | collective-permute-start | bytes 2359304 | tf_op jit(solution)/shard_map/ppermute | solution.py:146
  151.1 16.9 %copy-start.3 = (bf16[256,1536]{1,0:T(8,128)(2,1)}, bf16[256,1536]{1,0:T(8,128)(2,1)S(1)}, u32[]{:S(2)}) copy-start(bf16[256,1536]{1,0:T(8,128)(2,1)S(1)} %collective-permute-done.2) | copy-start | bytes 2359300
  168.0 2.1 copy-start.4
  168.0 2.2 copy-start.5
  170.2 7.1 %collective-permute-start.3 = (bf16[4,256,1536]{2,1,0:T(8,128)(2,1)}, bf16[4,256,1536]{2,1,0:T(8,128)(2,1)}, u32[]{:S(2)}, u32[]{:S(2)}) collective-permute-start(bf16[4,256,1536]{2,1,0:T(8,128)(2,1)} %pad_maximum_fusion), channel_id=1, source_target_pairs={{0,1},{1,0},{2,3},{3,2},{4,5},{5,4},{6,7},{7,6},{8,9},{9,8},{10,11... | collective-permute-start | bytes 9437192 | tf_op jit(solution)/shard_map/ppermute | solution.py:149
  219.9 7.5 %slice-start = ((f32[2048,1536]{1,0:T(8,128)}), f32[1024,1536]{1,0:T(8,128)S(1)}, s32[]{:S(2)}) async-start(f32[2048,1536]{1,0:T(8,128)} %multiply_reduce_fusion), calls=%async_computation.1 | async-start | bytes 12582912 | tf_op jit(solution)/shard_map/slice | solution.py:160
  219.9 5.8 %collective-permute-start.4 = (bf16[4,256,1536]{2,1,0:T(8,128)(2,1)S(1)}, bf16[4,256,1536]{2,1,0:T(8,128)(2,1)S(1)}, u32[]{:S(2)}, u32[]{:S(2)}) collective-permute-start(bf16[4,256,1536]{2,1,0:T(8,128)(2,1)S(1)} %bitcast.60), channel_id=1, source_target_pairs={{0,1},{1,0},{2,3},{3,2},{4,5},{5,4},{6,7},{7,6},{8,9},{9,8},{10,11... | collective-permute-start | bytes 9437192 | tf_op jit(solution)/shard_map/ppermute | solution.py:149
  225.8 1.7 copy-start.2
  230.8 20.4 %collective-permute-start.5 = (bf16[256,1536]{1,0:T(8,128)(2,1)S(1)}, bf16[256,1536]{1,0:T(8,128)(2,1)S(1)}, u32[]{:S(2)}, u32[]{:S(2)}) collective-permute-start(bf16[256,1536]{1,0:T(8,128)(2,1)S(1)} %get-tuple-element.13), channel_id=1, source_target_pairs={{0,6},{1,7},{2,0},{3,1},{4,2},{5,3},{6,4},{7,5},{8,14},{9,15},{10,... | collective-permute-start | bytes 2359304 | tf_op jit(solution)/shard_map/ppermute | solution.py:146
  231.8 36.6 %collective-permute-start.7 = (bf16[256,1536]{1,0:T(8,128)(2,1)S(1)}, bf16[256,1536]{1,0:T(8,128)(2,1)S(1)}, u32[]{:S(2)}, u32[]{:S(2)}) collective-permute-start(bf16[256,1536]{1,0:T(8,128)(2,1)S(1)} %get-tuple-element.14), channel_id=1, source_target_pairs={{0,2},{1,3},{2,4},{3,5},{4,6},{5,7},{6,0},{7,1},{8,10},{9,11},{10,... | collective-permute-start | bytes 2359304 | tf_op jit(solution)/shard_map/ppermute | solution.py:146
  232.8 36.1 %collective-permute-start.6 = (bf16[256,1536]{1,0:T(8,128)(2,1)S(1)}, bf16[256,1536]{1,0:T(8,128)(2,1)S(1)}, u32[]{:S(2)}, u32[]{:S(2)}) collective-permute-start(bf16[256,1536]{1,0:T(8,128)(2,1)S(1)} %get-tuple-element.15), channel_id=1, source_target_pairs={{0,4},{1,5},{2,6},{3,7},{4,0},{5,1},{6,2},{7,3},{8,12},{9,13},{10,... | collective-permute-start | bytes 2359304 | tf_op jit(solution)/shard_map/ppermute | solution.py:146
Sparse Core Ops, SparseCore 0:
  8.9 79.4 all-gather.1

commit v6 on v5

--- a/solution.py
+++ b/solution.py
@@ -148,19 +148,24 @@
     def sibling(x):
         return lax.ppermute(x, "exp", [(i, i ^ 1) for i in range(devices)])
 
-    same_core = jnp.stack([normed] + [chip_shift(normed, d) for d in range(1, half)], 0)
-    other_core = sibling(same_core)
-    rows = jnp.concatenate([same_core, other_core], 0).reshape(devices * count_of_tokens, width)
-    chip_of = (chip - jnp.arange(half, dtype=jnp.int32)) % half
-    device_of = jnp.concatenate([2 * chip_of + core, 2 * chip_of + (1 - core)])
-    row_gate = jnp.take(gate.reshape(devices, count_of_tokens, -1), device_of, axis=0).reshape(
-        devices * count_of_tokens, -1
-    )
-    partial = run_experts(rows, row_gate, w_in, w_down).reshape(2, half, count_of_tokens, width)
-    merged = partial[0] + sibling(partial[1].astype(jnp.bfloat16)).astype(jnp.float32)
-    total = merged[0]
-    for d in range(1, half):
-        total = total + chip_shift(merged[d].astype(jnp.bfloat16), -d).astype(jnp.float32)
+    gate_blocks = gate.reshape(devices, count_of_tokens, -1)
+
+    def block_gate(device):
+        return lax.dynamic_index_in_dim(gate_blocks, device, 0, keepdims=False)
+
+    same_core = [normed] + [chip_shift(normed, d) for d in range(1, half)]
+    other_core = [sibling(rows) for rows in same_core]
+    total = None
+    for d in range(half):
+        source_chip = (chip - d) % half
+        other_partial = run_experts(other_core[d], block_gate(2 * source_chip + 1 - core), w_in, w_down)
+        same_partial = run_experts(same_core[d], block_gate(2 * source_chip + core), w_in, w_down)
+        merged = same_partial + sibling(other_partial.astype(jnp.bfloat16)).astype(jnp.float32)
+        if d == 0:
+            total = merged if total is None else total + merged
+        else:
+            arrived = chip_shift(merged.astype(jnp.bfloat16), -d).astype(jnp.float32)
+            total = arrived if total is None else total + arrived
     return total
 
 

time: 284 us -> 236 us (0.83)
  waiting for transfers between devices: 141 us -> 121 us
  local copies, waits for them, and re-layouts: 17.6 us -> 1.83 us
  other arithmetic: 12.4 us -> 6.04 us
  matrix products: 42.7 us -> 37.4 us
    ppermute x6, waiting for transfers between devices: 69 us -> 54.2 us  [chip_shift(): return lax.ppermute(x, 'exp', pairs)]
    unnamed x17 -> x21, local copies, waits for them, and re-layouts: 9.19 us -> 1.19 us
    dot_general x1 -> x8, matrix products: 16.3 us -> 8.66 us  [run_experts(): jnp.einsum('etf,efd->etd', act, w_down, preferred_element_type=jnp.float32)]
    ppermute x2 -> x8, waiting for transfers between devices: 5.29 us -> 0.02 us  [sibling(): return lax.ppermute(x, 'exp', [(i, i ^ 1) for i in range(devices)])]
    another operation x2 -> x0, other arithmetic: 5.21 us -> none
    concatenate x1 -> x0, local copies, waits for them, and re-layouts: 3.77 us -> none  [exchange_experts(): jnp.concatenate([same_core, other_core], 0)]
    slice x3 -> x0, local copies, waits for them, and re-layouts: 3.17 us -> none  [the longest x1 3.16 us: exchange_experts(): partial[1].astype(jnp.bfloat16)]
    dot_general x1 -> x8, matrix products: 19.4 us -> 21.7 us  [run_experts(): jnp.einsum('td,edf->etf', rows, w_in, preferred_element_type=jnp.float32)]
  transfers between devices with their start and end apart: 9 -> 15, of which waited for: 7 -> 5; matrix products, arithmetic and copies ran while one was open for 5% -> 16% of each run, Pallas kernels for 0% -> 0%
where the time goes in v6:
time: 236 us; the launch traced here: 232 us
  waiting for transfers between devices  121 us (51%)
  matrix products  37.4 us (16%)
  Pallas kernels  35.7 us (15%)
  between operations  13.8 us (6%)
  blocking collectives  9.22 us (4%)
  starting transfers between devices  7.21 us (3%)
  other arithmetic  6.04 us (3%)
    all_gather x1, waiting for transfers between devices, per_device(): piece = lax.all_gather(prompt_key_value, 'req', axis=1, tiled=True)  65.6 us
    ppermute x6, waiting for transfers between devices, chip_shift(): return lax.ppermute(x, 'exp', pairs)  54.2 us
    pallas_call x1, Pallas kernels, attend(): pl.pallas_call(attention_kernel, grid_spec=grid_spec, out_shape=jax.Shape...  35.7 us
    dot_general x8, matrix products, run_experts(): jnp.einsum('td,edf->etf', rows, w_in, preferred_element_type=jnp.float32)  21.7 us
    all_gather x1, blocking collectives, per_device(): gate_gathered = lax.all_gather(gate_local, 'exp', axis=0, tiled=True)  9.22 us
    dot_general x8, matrix products, run_experts(): jnp.einsum('etf,efd->etd', act, w_down, preferred_element_type=jnp.float32)  8.66 us
    ppermute x6, starting transfers between devices, chip_shift(): return lax.ppermute(x, 'exp', pairs)  5.73 us
  transfers between devices with their start and end apart: 15, of which 5 were waited for; matrix products, arithmetic and copies ran while one was open for 16% of the time, Pallas kernels for 0%

profile of v6, /device:TPU:12, one launch (start us, length us, event | category | flops | bytes accessed | tf_op | source)
XLA Modules:
  0.0 231.7 jit_solution(17134739498341760617)
XLA Ops:
  6.5 0.7 all-gather.2.cloned.1.call-update
  7.3 0.9 broadcast_clamp_fusion
  8.2 0.6 min.37.pages_ref
  8.8 0.7 select_reduce_fusion
  9.5 9.2 %all_gather.6 = f32[2048,16]{0,1:T(8,128)S(1)} all-gather(f32[256,16]{0,1:T(8,128)S(1)} %select_reduce_fusion), channel_id=1, replica_groups=mesh['req'=4,'exp'=8] {'exp'}, dimensions={0}, use_global_device_ids=true | all-gather | bytes 147456 | tf_op jit(solution)/shard_map/all_gather | solution.py:198
  18.7 1.2 broadcast_clamp_fusion.1.groups_ref
  20.0 1.1 convolution_minimum_fusion.4
  21.1 0.3 convolution_minimum_fusion.3
  21.4 0.3 convolution_minimum_fusion.2
  21.6 0.3 convolution_minimum_fusion.1
  21.9 0.9 fusion.1.visible_ref
  22.8 65.6 %all-gather.2.cloned.1.call-done.prompt_ref = bf16[2,1024,1024]{2,1,0:T(8,128)(2,1)} async-done(((bf16[2,256,1024]{2,1,0:T(8,128)(2,1)}), bf16[2,1024,1024]{2,1,0:T(8,128)(2,1)}) %all-gather.2.cloned.1.call-update) | async-done | bytes 4194320 | tf_op jit(solution)/shard_map/all_gather | solution.py:200
  88.4 35.7 %shard_map.145 = bf16[256,1536]{1,0:T(8,128)(2,1)} custom-call(s32[8]{0:T(128)} %broadcast_clamp_fusion.1.groups_ref, s32[48]{0:T(128)} %min.37.pages_ref, s32[8]{0:T(128)} %lengths_ref.1, bf16[256,1536]{1,0:T(8,128)(2,1)} %queries_ref.1, bf16[256,1024]{1,0:T(8,128)(2,1)} %tree_ref.1, f32[8,32,32]{2,1,0:T(8,128)} %fusion.1.visible_ref, ...), custom_call_target="tpu_custom_call" | custom-call | tf_op jit(solution)/shard_map/pallas_call | solution.py:118
  124.1 4.3 %multiply_reduce_fusion.8 = (f32[256]{0:T(256)S(1)}, f32[256,1536]{1,0:T(8,128)S(1)}) fusion(bf16[256,1536]{1,0:T(8,128)(2,1)} %shard_map.145, bf16[1536,1536]{1,0:T(8,128)(2,1)} %param.24, bf16[256,1536]{1,0:T(8,128)(2,1)} %param.15), kind=kOutput, calls=%fused_computation.30 | convolution fusion | flops 1209532160 | bytes 7865344 | tf_op jit(solution)/shard_map/dot_general | solution.py:203
  128.4 1.1 copy-done.1
  129.5 1.1 multiply_convert_fusion
  130.6 0.0 collective-permute-start
  130.6 1.5 collective-permute-start.2
  132.1 0.5 collective-permute-start.6
  132.6 1.2 collective-permute-start.10
  134.0 0.0 collective-permute-done
  134.0 4.8 %convolution_bitcast_fusion.6 = f32[2,256,1024]{2,1,0:T(8,128)S(1)} fusion(bf16[2,1536,1024]{2,1,0:T(8,128)(2,1)} %param.28, bf16[256,1536]{1,0:T(8,128)(2,1)} %collective-permute-done), kind=kOutput, calls=%fused_computation.23 | convolution fusion | flops 1610612736 | bytes 9175040 | tf_op jit(solution)/shard_map/td,edf->etf/dot_general | solution.py:126
  138.8 0.0 slice-start
  138.8 1.1 multiply_reduce_fusion.6
  139.9 0.0 slice-start.1
  139.9 0.1 collective-permute-start.1
  140.0 12.1 %collective-permute-done.2 = bf16[256,1536]{1,0:T(8,128)(2,1)S(1)} collective-permute-done((bf16[256,1536]{1,0:T(8,128)(2,1)}, bf16[256,1536]{1,0:T(8,128)(2,1)S(1)}, u32[]{:S(2)}, u32[]{:S(2)}) %collective-permute-start.2) | collective-permute-done | bytes 786464 | tf_op jit(solution)/shard_map/ppermute | solution.py:146
  152.1 4.7 %convolution_bitcast_fusion.5 = f32[2,256,1024]{2,1,0:T(8,128)S(1)} fusion(bf16[2,1536,1024]{2,1,0:T(8,128)(2,1)} %param.28, bf16[256,1536]{1,0:T(8,128)(2,1)S(1)} %collective-permute-done.2), kind=kOutput, calls=%fused_computation.22 | convolution fusion | flops 1610612736 | bytes 9175040 | tf_op jit(solution)/shard_map/td,edf->etf/dot_general | solution.py:126
  156.8 1.0 multiply_reduce_fusion.5
  157.8 0.1 collective-permute-start.3
  157.9 10.6 %collective-permute-done.6 = bf16[256,1536]{1,0:T(8,128)(2,1)S(1)} collective-permute-done((bf16[256,1536]{1,0:T(8,128)(2,1)}, bf16[256,1536]{1,0:T(8,128)(2,1)S(1)}, u32[]{:S(2)}, u32[]{:S(2)}) %collective-permute-start.6) | collective-permute-done | bytes 786464 | tf_op jit(solution)/shard_map/ppermute | solution.py:146
  168.5 0.0 collective-permute-start.7
  168.6 1.8 convolution_bitcast_fusion.3
  170.4 0.0 collective-permute-done.10
  170.4 0.5 collective-permute-start.11
  170.9 1.8 convolution_bitcast_fusion.1
  172.7 1.1 multiply_reduce_fusion.3
  173.8 1.1 multiply_reduce_fusion.1
  174.9 0.0 collective-permute-done.3
  174.9 1.8 convolution_bitcast_fusion.4
  176.7 1.1 multiply_reduce_fusion.4
  177.8 0.1 collective-permute-start.4
  177.9 0.0 collective-permute-done.7
  177.9 2.0 convolution_bitcast_fusion.2
  179.9 1.1 multiply_reduce_fusion.2
  181.0 0.5 collective-permute-start.8
  181.6 0.0 collective-permute-done.11
  181.6 1.8 convolution_bitcast_fusion
  183.4 1.1 multiply_reduce_fusion
  184.5 0.1 collective-permute-start.12
  184.6 0.2 add_convert_fusion.3
  184.8 1.8 collective-permute-start.5
  186.6 0.0 collective-permute-done.8
  186.6 0.2 add_convert_fusion.2
  186.8 0.1 collective-permute-start.9
  186.9 0.0 collective-permute-done.12
  186.9 0.2 add_convert_fusion.1
  187.1 0.6 collective-permute-start.13
  187.7 3.0 %convolution_bitcast_fusion.7 = f32[2,256,1024]{2,1,0:T(8,128)S(1)} fusion(bf16[2,1536,1024]{2,1,0:T(8,128)(2,1)S(1)} %bitcast.113, bf16[256,1536]{1,0:T(8,128)(2,1)} %multiply_convert_fusion), kind=kOutput, calls=%fused_computation.24 | convolution fusion | flops 1610612736 | bytes 9175040 | tf_op jit(solution)/shard_map/td,edf->etf/dot_general | solution.py:126
  190.8 1.1 multiply_reduce_fusion.7
  191.9 13.3 %collective-permute-done.5 = bf16[256,1536]{1,0:T(8,128)(2,1)S(1)} collective-permute-done((bf16[256,1536]{1,0:T(8,128)(2,1)S(1)}, bf16[256,1536]{1,0:T(8,128)(2,1)S(1)}, u32[]{:S(2)}, u32[]{:S(2)}) %collective-permute-start.5) | collective-permute-done | bytes 786464 | tf_op jit(solution)/shard_map/ppermute | solution.py:146
  205.2 18.2 %collective-permute-done.9 = bf16[256,1536]{1,0:T(8,128)(2,1)S(1)} collective-permute-done((bf16[256,1536]{1,0:T(8,128)(2,1)S(1)}, bf16[256,1536]{1,0:T(8,128)(2,1)S(1)}, u32[]{:S(2)}, u32[]{:S(2)}) %collective-permute-start.9) | collective-permute-done | bytes 786464 | tf_op jit(solution)/shard_map/ppermute | solution.py:146
  223.4 0.0 collective-permute-done.13
  223.4 1.5 add_convert_fusion
  (26 shorter events, 0.1 us)
Async XLA Ops:
  6.5 132.3 %copy-start = (bf16[2,512,1536]{2,1,0:T(8,128)(2,1)S(1)}, bf16[2,512,1536]{2,1,0:T(8,128)(2,1)}, u32[]{:S(2)}) copy-start(bf16[2,512,1536]{2,1,0:T(8,128)(2,1)} %param.29) | copy-start | bytes 9437188
  6.5 81.9 %all-gather.2.cloned.1.call-start = ((), (), s32[]{:S(2)}) async-start(), calls=%async_computation | async-start | bytes 5242880 | tf_op jit(solution)/shard_map/all_gather | solution.py:200
  124.1 5.4 %copy-start.3 = (f32[1536]{0:T(1024)S(1)}, f32[1536]{0:T(1024)}, u32[]{:S(2)}) copy-start(f32[1536]{0:T(1024)} %param.25) | copy-start | bytes 18436
  128.4 1.2 copy-start.1
  130.6 3.4 %collective-permute-start = (bf16[256,1536]{1,0:T(8,128)(2,1)}, bf16[256,1536]{1,0:T(8,128)(2,1)}, u32[]{:S(2)}, u32[]{:S(2)}) collective-permute-start(bf16[256,1536]{1,0:T(8,128)(2,1)} %multiply_convert_fusion), channel_id=1, source_target_pairs={{0,1},{1,0},{2,3},{3,2},{4,5},{5,4},{6,7},{7,6},{8,9},{9,8},{10,11... | collective-permute-start | bytes 2359304 | tf_op jit(solution)/shard_map/ppermute | solution.py:149
  130.6 21.5 %collective-permute-start.2 = (bf16[256,1536]{1,0:T(8,128)(2,1)}, bf16[256,1536]{1,0:T(8,128)(2,1)S(1)}, u32[]{:S(2)}, u32[]{:S(2)}) collective-permute-start(bf16[256,1536]{1,0:T(8,128)(2,1)} %multiply_convert_fusion), channel_id=1, source_target_pairs={{0,2},{1,3},{2,4},{3,5},{4,6},{5,7},{6,0},{7,1},{8,10},{9,11},{10,... | collective-permute-start | bytes 2359304 | tf_op jit(solution)/shard_map/ppermute | solution.py:146
  132.1 36.4 %collective-permute-start.6 = (bf16[256,1536]{1,0:T(8,128)(2,1)}, bf16[256,1536]{1,0:T(8,128)(2,1)S(1)}, u32[]{:S(2)}, u32[]{:S(2)}) collective-permute-start(bf16[256,1536]{1,0:T(8,128)(2,1)} %multiply_convert_fusion), channel_id=1, source_target_pairs={{0,4},{1,5},{2,6},{3,7},{4,0},{5,1},{6,2},{7,3},{8,12},{9,13},{10,... | collective-permute-start | bytes 2359304 | tf_op jit(solution)/shard_map/ppermute | solution.py:146
  132.6 37.8 %collective-permute-start.10 = (bf16[256,1536]{1,0:T(8,128)(2,1)}, bf16[256,1536]{1,0:T(8,128)(2,1)S(1)}, u32[]{:S(2)}, u32[]{:S(2)}) collective-permute-start(bf16[256,1536]{1,0:T(8,128)(2,1)} %multiply_convert_fusion), channel_id=1, source_target_pairs={{0,6},{1,7},{2,0},{3,1},{4,2},{5,3},{6,4},{7,5},{8,14},{9,15},{10,... | collective-permute-start | bytes 2359304 | tf_op jit(solution)/shard_map/ppermute | solution.py:146
  138.8 29.7 %slice-start = ((s8[6291456]{0:T(1024)(128)(4,1)}), s8[4194304]{0:T(1024)(128)(4,1)S(1)}, s32[]{:S(2)}) async-start(s8[6291456]{0:T(1024)(128)(4,1)} %bitcast.112), calls=%async_computation.1 | async-start | bytes 8388608
  139.9 28.6 %slice-start.1 = ((s8[6291456]{0:T(1024)(128)(4,1)}), s8[2097152]{0:T(1024)(128)(4,1)S(1)}, s32[]{:S(2)}) async-start(s8[6291456]{0:T(1024)(128)(4,1)} %bitcast.112), calls=%async_computation.2 | async-start | bytes 4194304
  139.9 51.9 %collective-permute-start.1 = (bf16[256,1536]{1,0:T(8,128)(2,1)S(1)}, bf16[256,1536]{1,0:T(8,128)(2,1)S(1)}, u32[]{:S(2)}, u32[]{:S(2)}) collective-permute-start(bf16[256,1536]{1,0:T(8,128)(2,1)S(1)} %multiply_reduce_fusion.6), channel_id=1, source_target_pairs={{0,1},{1,0},{2,3},{3,2},{4,5},{5,4},{6,7},{7,6},{8,9},{9,8},{10,11... | collective-permute-start | bytes 2359304 | tf_op jit(solution)/shard_map/ppermute | solution.py:149
  157.8 17.1 %collective-permute-start.3 = (bf16[256,1536]{1,0:T(8,128)(2,1)S(1)}, bf16[256,1536]{1,0:T(8,128)(2,1)S(1)}, u32[]{:S(2)}, u32[]{:S(2)}) collective-permute-start(bf16[256,1536]{1,0:T(8,128)(2,1)S(1)} %collective-permute-done.2), channel_id=1, source_target_pairs={{0,1},{1,0},{2,3},{3,2},{4,5},{5,4},{6,7},{7,6},{8,9},{9,8},{10,11... | collective-permute-start | bytes 2359304 | tf_op jit(solution)/shard_map/ppermute | solution.py:149
  168.5 9.4 %collective-permute-start.7 = (bf16[256,1536]{1,0:T(8,128)(2,1)S(1)}, bf16[256,1536]{1,0:T(8,128)(2,1)S(1)}, u32[]{:S(2)}, u32[]{:S(2)}) collective-permute-start(bf16[256,1536]{1,0:T(8,128)(2,1)S(1)} %collective-permute-done.6), channel_id=1, source_target_pairs={{0,1},{1,0},{2,3},{3,2},{4,5},{5,4},{6,7},{7,6},{8,9},{9,8},{10,11... | collective-permute-start | bytes 2359304 | tf_op jit(solution)/shard_map/ppermute | solution.py:149
  170.4 11.2 %collective-permute-start.11 = (bf16[256,1536]{1,0:T(8,128)(2,1)S(1)}, bf16[256,1536]{1,0:T(8,128)(2,1)S(1)}, u32[]{:S(2)}, u32[]{:S(2)}) collective-permute-start(bf16[256,1536]{1,0:T(8,128)(2,1)S(1)} %collective-permute-done.10), channel_id=1, source_target_pairs={{0,1},{1,0},{2,3},{3,2},{4,5},{5,4},{6,7},{7,6},{8,9},{9,8},{10,11... | collective-permute-start | bytes 2359304 | tf_op jit(solution)/shard_map/ppermute | solution.py:149
  177.8 6.8 %collective-permute-start.4 = (bf16[256,1536]{1,0:T(8,128)(2,1)S(1)}, bf16[256,1536]{1,0:T(8,128)(2,1)S(1)}, u32[]{:S(2)}, u32[]{:S(2)}) collective-permute-start(bf16[256,1536]{1,0:T(8,128)(2,1)S(1)} %multiply_reduce_fusion.4), channel_id=1, source_target_pairs={{0,1},{1,0},{2,3},{3,2},{4,5},{5,4},{6,7},{7,6},{8,9},{9,8},{10,11... | collective-permute-start | bytes 2359304 | tf_op jit(solution)/shard_map/ppermute | solution.py:149
  181.0 5.5 %collective-permute-start.8 = (bf16[256,1536]{1,0:T(8,128)(2,1)S(1)}, bf16[256,1536]{1,0:T(8,128)(2,1)S(1)}, u32[]{:S(2)}, u32[]{:S(2)}) collective-permute-start(bf16[256,1536]{1,0:T(8,128)(2,1)S(1)} %multiply_reduce_fusion.2), channel_id=1, source_target_pairs={{0,1},{1,0},{2,3},{3,2},{4,5},{5,4},{6,7},{7,6},{8,9},{9,8},{10,11... | collective-permute-start | bytes 2359304 | tf_op jit(solution)/shard_map/ppermute | solution.py:149
  184.5 2.4 %collective-permute-start.12 = (bf16[256,1536]{1,0:T(8,128)(2,1)S(1)}, bf16[256,1536]{1,0:T(8,128)(2,1)S(1)}, u32[]{:S(2)}, u32[]{:S(2)}) collective-permute-start(bf16[256,1536]{1,0:T(8,128)(2,1)S(1)} %multiply_reduce_fusion), channel_id=1, source_target_pairs={{0,1},{1,0},{2,3},{3,2},{4,5},{5,4},{6,7},{7,6},{8,9},{9,8},{10,11... | collective-permute-start | bytes 2359304 | tf_op jit(solution)/shard_map/ppermute | solution.py:149
  184.8 20.4 %collective-permute-start.5 = (bf16[256,1536]{1,0:T(8,128)(2,1)S(1)}, bf16[256,1536]{1,0:T(8,128)(2,1)S(1)}, u32[]{:S(2)}, u32[]{:S(2)}) collective-permute-start(bf16[256,1536]{1,0:T(8,128)(2,1)S(1)} %add_convert_fusion.3), channel_id=1, source_target_pairs={{0,6},{1,7},{2,0},{3,1},{4,2},{5,3},{6,4},{7,5},{8,14},{9,15},{10,... | collective-permute-start | bytes 2359304 | tf_op jit(solution)/shard_map/ppermute | solution.py:146
  186.8 36.6 %collective-permute-start.9 = (bf16[256,1536]{1,0:T(8,128)(2,1)S(1)}, bf16[256,1536]{1,0:T(8,128)(2,1)S(1)}, u32[]{:S(2)}, u32[]{:S(2)}) collective-permute-start(bf16[256,1536]{1,0:T(8,128)(2,1)S(1)} %add_convert_fusion.2), channel_id=1, source_target_pairs={{0,4},{1,5},{2,6},{3,7},{4,0},{5,1},{6,2},{7,3},{8,12},{9,13},{10,... | collective-permute-start | bytes 2359304 | tf_op jit(solution)/shard_map/ppermute | solution.py:146
  187.1 36.3 %collective-permute-start.13 = (bf16[256,1536]{1,0:T(8,128)(2,1)S(1)}, bf16[256,1536]{1,0:T(8,128)(2,1)S(1)}, u32[]{:S(2)}, u32[]{:S(2)}) collective-permute-start(bf16[256,1536]{1,0:T(8,128)(2,1)S(1)} %add_convert_fusion.1), channel_id=1, source_target_pairs={{0,2},{1,3},{2,4},{3,5},{4,6},{5,7},{6,0},{7,1},{8,10},{9,11},{10,... | collective-permute-start | bytes 2359304 | tf_op jit(solution)/shard_map/ppermute | solution.py:146
  190.8 32.6 %copy-start.2 = (f32[256,1536]{1,0:T(8,128)S(1)}, f32[256,1536]{1,0:T(8,128)}, u32[]{:S(2)}) copy-start(f32[256,1536]{1,0:T(8,128)} %copy-done.1) | copy-start | bytes 4718596
Sparse Core Ops, SparseCore 0:
  8.9 79.4 all-gather.1

commit v7 on v6

--- a/solution.py
+++ b/solution.py
@@ -32,56 +32,69 @@
     return reach > 0.5
 
 
-def attention_kernel(groups_ref, pages_ref, lengths_ref, queries_ref, tree_ref, visible_ref, prompt_ref, *rest):
+def stacked_queries(queries_ref, kv):
+    heads_repeated = QUERY_HEADS // KEY_VALUE_HEADS
+    return jnp.concatenate(
+        [
+            queries_ref[:, (kv * heads_repeated + j) * HEAD_WIDTH : (kv * heads_repeated + j + 1) * HEAD_WIDTH]
+            for j in range(heads_repeated)
+        ],
+        0,
+    )
+
+
+def scores_of(query_rows, keys):
+    contract = (((1,), (1,)), ((), ()))
+    return lax.dot_general(query_rows, keys, contract, preferred_element_type=jnp.float32) * (HEAD_WIDTH ** (-0.5))
+
+
+def local_kernel(lengths_ref, pages_ref, queries_ref, tree_ref, visible_ref, *rest):
     page_refs = rest[:MAXP]
-    out_ref = rest[MAXP]
+    peak_ref, denom_ref, numer_ref = rest[MAXP:]
     request = pl.program_id(0)
     key_value_width = KEY_VALUE_HEADS * HEAD_WIDTH
     heads_repeated = QUERY_HEADS // KEY_VALUE_HEADS
     rows = heads_repeated * TREE_TOKENS
-    scale_factor = HEAD_WIDTH ** (-0.5)
     tree_visible = jnp.concatenate([visible_ref[0]] * heads_repeated, 0) > 0.5
     positions = lax.broadcasted_iota(jnp.int32, (rows, MAXP * PAGE_POSITIONS), 1)
     cache_visible = positions < lengths_ref[request]
-    contract = (((1,), (1,)), ((), ()))
-
     for kv in range(KEY_VALUE_HEADS):
         key_at = kv * HEAD_WIDTH
         value_at = key_value_width + kv * HEAD_WIDTH
-        query_rows = jnp.concatenate(
-            [
-                queries_ref[:, (kv * heads_repeated + j) * HEAD_WIDTH : (kv * heads_repeated + j + 1) * HEAD_WIDTH]
-                for j in range(heads_repeated)
-            ],
-            0,
-        )
-        prompt_keys = prompt_ref[0, :, key_at : key_at + HEAD_WIDTH]
-        prompt_values = prompt_ref[0, :, value_at : value_at + HEAD_WIDTH]
+        query_rows = stacked_queries(queries_ref, kv)
         cache_keys = jnp.concatenate([p[0, :, key_at : key_at + HEAD_WIDTH] for p in page_refs], 0)
         cache_values = jnp.concatenate([p[0, :, value_at : value_at + HEAD_WIDTH] for p in page_refs], 0)
         tree_keys = tree_ref[:, key_at : key_at + HEAD_WIDTH]
         tree_values = tree_ref[:, value_at : value_at + HEAD_WIDTH]
-        prompt_scores = lax.dot_general(query_rows, prompt_keys, contract, preferred_element_type=jnp.float32) * scale_factor
-        cache_scores = lax.dot_general(query_rows, cache_keys, contract, preferred_element_type=jnp.float32) * scale_factor
-        tree_scores = lax.dot_general(query_rows, tree_keys, contract, preferred_element_type=jnp.float32) * scale_factor
-        cache_scores = jnp.where(cache_visible, cache_scores, -jnp.inf)
-        tree_scores = jnp.where(tree_visible, tree_scores, -jnp.inf)
-        peak = jnp.maximum(
-            jnp.maximum(jnp.max(prompt_scores, -1, keepdims=True), jnp.max(cache_scores, -1, keepdims=True)),
-            jnp.max(tree_scores, -1, keepdims=True),
-        )
-        prompt_exp = jnp.exp(prompt_scores - peak)
+        cache_scores = jnp.where(cache_visible, scores_of(query_rows, cache_keys), -jnp.inf)
+        tree_scores = jnp.where(tree_visible, scores_of(query_rows, tree_keys), -jnp.inf)
+        peak = jnp.maximum(jnp.max(cache_scores, -1, keepdims=True), jnp.max(tree_scores, -1, keepdims=True))
         cache_exp = jnp.exp(cache_scores - peak)
         tree_exp = jnp.exp(tree_scores - peak)
-        denom = (
-            jnp.sum(prompt_exp, -1, keepdims=True)
-            + jnp.sum(cache_exp, -1, keepdims=True)
-            + jnp.sum(tree_exp, -1, keepdims=True)
-        )
-        numer = (
-            jnp.dot(prompt_exp.astype(jnp.bfloat16), prompt_values, preferred_element_type=jnp.float32)
-            + jnp.dot(cache_exp.astype(jnp.bfloat16), cache_values, preferred_element_type=jnp.float32)
-            + jnp.dot(tree_exp.astype(jnp.bfloat16), tree_values, preferred_element_type=jnp.float32)
+        peak_ref[0, kv] = peak
+        denom_ref[0, kv] = jnp.sum(cache_exp, -1, keepdims=True) + jnp.sum(tree_exp, -1, keepdims=True)
+        numer_ref[0, kv] = jnp.dot(
+            cache_exp.astype(jnp.bfloat16), cache_values, preferred_element_type=jnp.float32
+        ) + jnp.dot(tree_exp.astype(jnp.bfloat16), tree_values, preferred_element_type=jnp.float32)
+
+
+def prompt_kernel(groups_ref, queries_ref, prompt_ref, peak_ref, denom_ref, numer_ref, out_ref):
+    key_value_width = KEY_VALUE_HEADS * HEAD_WIDTH
+    heads_repeated = QUERY_HEADS // KEY_VALUE_HEADS
+    for kv in range(KEY_VALUE_HEADS):
+        key_at = kv * HEAD_WIDTH
+        value_at = key_value_width + kv * HEAD_WIDTH
+        query_rows = stacked_queries(queries_ref, kv)
+        prompt_scores = scores_of(query_rows, prompt_ref[0, :, key_at : key_at + HEAD_WIDTH])
+        local_peak = peak_ref[0, kv]
+        peak = jnp.maximum(local_peak, jnp.max(prompt_scores, -1, keepdims=True))
+        prompt_exp = jnp.exp(prompt_scores - peak)
+        decay = jnp.exp(local_peak - peak)
+        denom = denom_ref[0, kv] * decay + jnp.sum(prompt_exp, -1, keepdims=True)
+        numer = numer_ref[0, kv] * decay + jnp.dot(
+            prompt_exp.astype(jnp.bfloat16),
+            prompt_ref[0, :, value_at : value_at + HEAD_WIDTH],
+            preferred_element_type=jnp.float32,
         )
         result = (numer / denom).astype(jnp.bfloat16)
         for j in range(heads_repeated):
@@ -89,37 +102,76 @@
             out_ref[:, head * HEAD_WIDTH : (head + 1) * HEAD_WIDTH] = result[j * TREE_TOKENS : (j + 1) * TREE_TOKENS]
 
 
-def attend(queries, draft_kv, piece, cache_page_store, page_table, cache_len, parents, groups):
+def attend_local(queries, draft_kv, cache_page_store, page_table, cache_len, parents):
     count_of_tokens, width = queries.shape
     count_of_requests = page_table.shape[0]
     row_width = draft_kv.shape[1]
     store_pages = cache_page_store.shape[0]
+    rows = (QUERY_HEADS // KEY_VALUE_HEADS) * TREE_TOKENS
     visible = ancestry(parents).astype(jnp.float32)
     flat_pages = jnp.clip(page_table.reshape(-1), 0, store_pages - 1).astype(jnp.int32)
-    prompt_groups = jnp.clip(groups, 0, piece.shape[0] - 1).astype(jnp.int32)
 
     def page_spec(slot):
-        return pl.BlockSpec(
-            (1, PAGE_POSITIONS, row_width), lambda r, g, p, c: (p[r * MAXP + slot], 0, 0)
-        )
+        return pl.BlockSpec((1, PAGE_POSITIONS, row_width), lambda r, c, p: (p[r * MAXP + slot], 0, 0))
+
+    def stat_spec(last):
+        return pl.BlockSpec((1, KEY_VALUE_HEADS, rows, last), lambda r, c, p: (r, 0, 0, 0))
 
     grid_spec = pltpu.PrefetchScalarGridSpec(
-        num_scalar_prefetch=3,
+        num_scalar_prefetch=2,
         grid=(count_of_requests,),
         in_specs=[
-            pl.BlockSpec((TREE_TOKENS, width), lambda r, g, p, c: (r, 0)),
-            pl.BlockSpec((TREE_TOKENS, row_width), lambda r, g, p, c: (r, 0)),
-            pl.BlockSpec((1, TREE_TOKENS, TREE_TOKENS), lambda r, g, p, c: (r, 0, 0)),
-            pl.BlockSpec((1, piece.shape[1], row_width), lambda r, g, p, c: (g[r], 0, 0)),
+            pl.BlockSpec((TREE_TOKENS, width), lambda r, c, p: (r, 0)),
+            pl.BlockSpec((TREE_TOKENS, row_width), lambda r, c, p: (r, 0)),
+            pl.BlockSpec((1, TREE_TOKENS, TREE_TOKENS), lambda r, c, p: (r, 0, 0)),
         ]
         + [page_spec(slot) for slot in range(MAXP)],
-        out_specs=pl.BlockSpec((TREE_TOKENS, width), lambda r, g, p, c: (r, 0)),
-    )
+        out_specs=[stat_spec(1), stat_spec(1), stat_spec(HEAD_WIDTH)],
+    )
+    stat_shape = (count_of_requests, KEY_VALUE_HEADS, rows)
     return pl.pallas_call(
-        attention_kernel,
+        local_kernel,
+        grid_spec=grid_spec,
+        out_shape=[
+            jax.ShapeDtypeStruct(stat_shape + (1,), jnp.float32),
+            jax.ShapeDtypeStruct(stat_shape + (1,), jnp.float32),
+            jax.ShapeDtypeStruct(stat_shape + (HEAD_WIDTH,), jnp.float32),
+        ],
+    )(cache_len.astype(jnp.int32), flat_pages, queries, draft_kv, visible, *([cache_page_store] * MAXP))
+
+
+def attend_prompt(queries, piece, groups, peak, denom, numer):
+    count_of_tokens, width = queries.shape
+    count_of_requests = peak.shape[0]
+    rows = peak.shape[2]
+    row_width = piece.shape[2]
+    prompt_groups = jnp.clip(groups, 0, piece.shape[0] - 1).astype(jnp.int32)
+
+    def stat_spec(last):
+        return pl.BlockSpec((1, KEY_VALUE_HEADS, rows, last), lambda r, g: (r, 0, 0, 0))
+
+    grid_spec = pltpu.PrefetchScalarGridSpec(
+        num_scalar_prefetch=1,
+        grid=(count_of_requests,),
+        in_specs=[
+            pl.BlockSpec((TREE_TOKENS, width), lambda r, g: (r, 0)),
+            pl.BlockSpec((1, piece.shape[1], row_width), lambda r, g: (g[r], 0, 0)),
+            stat_spec(1),
+            stat_spec(1),
+            stat_spec(HEAD_WIDTH),
+        ],
+        out_specs=pl.BlockSpec((TREE_TOKENS, width), lambda r, g: (r, 0)),
+    )
+    return pl.pallas_call(
+        prompt_kernel,
         grid_spec=grid_spec,
         out_shape=jax.ShapeDtypeStruct((count_of_tokens, width), jnp.bfloat16),
-    )(prompt_groups, flat_pages, cache_len.astype(jnp.int32), queries, draft_kv, visible, piece, *([cache_page_store] * MAXP))
+    )(prompt_groups, queries, piece, peak, denom, numer)
+
+
+def attend(queries, draft_kv, piece, cache_page_store, page_table, cache_len, parents, groups):
+    peak, denom, numer = attend_local(queries, draft_kv, cache_page_store, page_table, cache_len, parents)
+    return attend_prompt(queries, piece, groups, peak, denom, numer)
 
 
 def run_experts(rows, row_gate, w_in, w_down):

time: 236 us -> 243 us (1.030)
  Pallas kernels: 35.7 us -> 61.7 us
  waiting for transfers between devices: 121 us -> 101 us
    pallas_call x1 -> x2, Pallas kernels: 35.7 us -> 61.7 us  [the longest x1 36.8 us: attend_prompt(): pl.pallas_call(prompt_kernel, grid_spec=grid_spec, out_shape=jax.ShapeDty...]
    all_gather x1, waiting for transfers between devices: 65.6 us -> 42.1 us  [per_device(): piece = lax.all_gather(prompt_key_value, 'req', axis=1, tiled=True)]
    ppermute x6, waiting for transfers between devices: 54.2 us -> 58.3 us  [chip_shift(): return lax.ppermute(x, 'exp', pairs)]
  transfers between devices with their start and end apart: 15 -> 15, of which waited for: 5 -> 4; matrix products, arithmetic and copies ran while one was open for 16% -> 15% of each run, Pallas kernels for 0% -> 10%
where the time goes in v7:
time: 243 us; the launch traced here: 238 us
  waiting for transfers between devices  101 us (42%)
  Pallas kernels  61.7 us (25%)
  matrix products  37.4 us (15%)
  between operations  13.8 us (6%)
  blocking collectives  9.22 us (4%)
  starting transfers between devices  8.72 us (4%)
  other arithmetic  4.66 us (2%)
    ppermute x6, waiting for transfers between devices, chip_shift(): return lax.ppermute(x, 'exp', pairs)  58.3 us
    all_gather x1, waiting for transfers between devices, per_device(): piece = lax.all_gather(prompt_key_value, 'req', axis=1, tiled=True)  42.1 us
    pallas_call x1, Pallas kernels, attend_prompt(): pl.pallas_call(prompt_kernel, grid_spec=grid_spec, out_shape=jax.ShapeDty...  36.8 us
    pallas_call x1, Pallas kernels, attend_local(): pl.pallas_call(local_kernel, grid_spec=grid_spec, out_shape=[jax.ShapeDty...  24.9 us
    dot_general x8, matrix products, run_experts(): jnp.einsum('td,edf->etf', rows, w_in, preferred_element_type=jnp.float32)  22.1 us
    all_gather x1, blocking collectives, per_device(): gate_gathered = lax.all_gather(gate_local, 'exp', axis=0, tiled=True)  9.22 us
    dot_general x8, matrix products, run_experts(): jnp.einsum('etf,efd->etd', act, w_down, preferred_element_type=jnp.float32)  8.24 us
    ppermute x6, starting transfers between devices, chip_shift(): return lax.ppermute(x, 'exp', pairs)  6.81 us
  transfers between devices with their start and end apart: 15, of which 4 were waited for; matrix products, arithmetic and copies ran while one was open for 15% of the time, Pallas kernels for 10%

profile of v7, /device:TPU:12, one launch (start us, length us, event | category | flops | bytes accessed | tf_op | source)
XLA Modules:
  0.0 238.4 jit_solution(14208356439131126559)
XLA Ops:
  6.5 0.7 all-gather.2.cloned.1.call-update
  7.3 0.9 broadcast_clamp_fusion
  8.2 0.6 min.37.pages_ref
  8.8 1.1 convolution_minimum_fusion.4
  9.9 0.3 convolution_minimum_fusion.3
  10.2 0.3 convolution_minimum_fusion.2
  10.4 0.3 convolution_minimum_fusion.1
  10.7 0.9 fusion.1.visible_ref
  11.6 24.9 %shard_map.145 = (f32[8,8,96,1]{3,2,1,0:T(8,128)}, f32[8,8,96,1]{3,2,1,0:T(8,128)}, f32[8,8,96,64]{3,2,1,0:T(8,128)}) custom-call(s32[8]{0:T(128)} %lengths_ref.1, s32[48]{0:T(128)} %min.37.pages_ref, bf16[256,1536]{1,0:T(8,128)(2,1)} %queries_ref.3, bf16[256,1024]{1,0:T(8,128)(2,1)} %tree_ref.1, f32[8,32,32]{2,1,0:T(8,128)} %fusion.1.visible_ref, ...), custom_call_target="tpu_custom_call" | custom-call | tf_op jit(solution)/shard_map/pallas_call | solution.py:132
  36.6 9.2 %all_gather.6 = f32[2048,16]{0,1:T(8,128)S(1)} all-gather(f32[256,16]{0,1:T(8,128)S(1)} %select_reduce_fusion), channel_id=1, replica_groups=mesh['req'=4,'exp'=8] {'exp'}, dimensions={0}, use_global_device_ids=true | all-gather | bytes 147456 | tf_op jit(solution)/shard_map/all_gather | solution.py:250
  45.8 0.5 broadcast_clamp_fusion.1.groups_ref
  46.3 42.1 %all-gather.2.cloned.1.call-done.prompt_ref = bf16[2,1024,1024]{2,1,0:T(8,128)(2,1)} async-done(((bf16[2,256,1024]{2,1,0:T(8,128)(2,1)}), bf16[2,1024,1024]{2,1,0:T(8,128)(2,1)}) %all-gather.2.cloned.1.call-update) | async-done | bytes 4194320 | tf_op jit(solution)/shard_map/all_gather | solution.py:252
  88.4 36.8 %shard_map.146 = bf16[256,1536]{1,0:T(8,128)(2,1)} custom-call(s32[8]{0:T(128)} %broadcast_clamp_fusion.1.groups_ref, bf16[256,1536]{1,0:T(8,128)(2,1)} %queries_ref.3, bf16[2,1024,1024]{2,1,0:T(8,128)(2,1)} %all-gather.2.cloned.1.call-done.prompt_ref, f32[8,8,96,1]{3,2,1,0:T(8,128)} %get-tuple-element.11.peak_ref, ...), custom_call_target="tpu_custom_call" | custom-call | tf_op jit(solution)/shard_map/pallas_call | solution.py:165
  125.2 4.3 %multiply_reduce_fusion.8 = (f32[256]{0:T(256)S(1)}, f32[256,1536]{1,0:T(8,128)S(1)}) fusion(bf16[256,1536]{1,0:T(8,128)(2,1)} %shard_map.146, bf16[1536,1536]{1,0:T(8,128)(2,1)} %param.24, bf16[256,1536]{1,0:T(8,128)(2,1)} %param.15), kind=kOutput, calls=%fused_computation.30 | convolution fusion | flops 1209532160 | bytes 7865344 | tf_op jit(solution)/shard_map/dot_general | solution.py:255
  129.4 1.1 copy-done.1
  130.6 1.1 multiply_convert_fusion
  131.7 0.0 collective-permute-start
  131.7 1.4 collective-permute-start.10
  133.1 1.5 collective-permute-start.6
  134.6 0.0 collective-permute-start.2
  134.7 0.0 collective-permute-done
  134.7 4.8 %convolution_bitcast_fusion.6 = f32[2,256,1024]{2,1,0:T(8,128)S(1)} fusion(bf16[2,1536,1024]{2,1,0:T(8,128)(2,1)} %param.28, bf16[256,1536]{1,0:T(8,128)(2,1)} %collective-permute-done), kind=kOutput, calls=%fused_computation.23 | convolution fusion | flops 1610612736 | bytes 9175040 | tf_op jit(solution)/shard_map/td,edf->etf/dot_general | solution.py:178
  139.6 0.0 slice-start
  139.6 1.1 multiply_reduce_fusion.6
  140.7 0.0 slice-start.1
  140.7 0.1 collective-permute-start.1
  140.8 27.8 %collective-permute-done.2 = bf16[256,1536]{1,0:T(8,128)(2,1)S(1)} collective-permute-done((bf16[256,1536]{1,0:T(8,128)(2,1)}, bf16[256,1536]{1,0:T(8,128)(2,1)S(1)}, u32[]{:S(2)}, u32[]{:S(2)}) %collective-permute-start.2) | collective-permute-done | bytes 786464 | tf_op jit(solution)/shard_map/ppermute | solution.py:198
  168.6 4.7 %convolution_bitcast_fusion.5 = f32[2,256,1024]{2,1,0:T(8,128)S(1)} fusion(bf16[2,1536,1024]{2,1,0:T(8,128)(2,1)} %param.28, bf16[256,1536]{1,0:T(8,128)(2,1)S(1)} %collective-permute-done.2), kind=kOutput, calls=%fused_computation.22 | convolution fusion | flops 1610612736 | bytes 9175040 | tf_op jit(solution)/shard_map/td,edf->etf/dot_general | solution.py:178
  173.3 1.0 multiply_reduce_fusion.5
  174.3 0.1 collective-permute-start.3
  174.4 0.0 collective-permute-done.6
  174.4 0.5 collective-permute-start.7
  174.9 1.8 convolution_bitcast_fusion.3
  176.7 0.0 collective-permute-done.10
  176.7 0.1 collective-permute-start.11
  176.8 1.8 convolution_bitcast_fusion.1
  178.6 1.0 multiply_reduce_fusion.3
  179.6 1.0 multiply_reduce_fusion.1
  180.7 0.0 collective-permute-done.3
  180.7 1.9 convolution_bitcast_fusion.4
  182.6 1.0 multiply_reduce_fusion.4
  183.6 0.5 collective-permute-start.4
  184.1 0.0 collective-permute-done.7
  184.1 2.1 convolution_bitcast_fusion.2
  186.3 1.0 multiply_reduce_fusion.2
  187.3 0.2 collective-permute-start.8
  187.5 0.0 collective-permute-done.11
  187.5 1.9 convolution_bitcast_fusion
  189.4 1.0 multiply_reduce_fusion
  190.4 0.5 collective-permute-start.12
  190.9 0.0 collective-permute-done.4
  190.9 0.2 add_convert_fusion.3
  191.1 2.6 %collective-permute-start.5 = (bf16[256,1536]{1,0:T(8,128)(2,1)S(1)}, bf16[256,1536]{1,0:T(8,128)(2,1)S(1)}, u32[]{:S(2)}, u32[]{:S(2)}) collective-permute-start(bf16[256,1536]{1,0:T(8,128)(2,1)S(1)} %add_convert_fusion.3), channel_id=1, source_target_pairs={{0,6},{1,7},{2,0},{3,1},{4,2},{5,3},{6,4},{7,5},{8,14},{9,15},{10,... | collective-permute-start | bytes 2359304 | tf_op jit(solution)/shard_map/ppermute | solution.py:198
  193.7 0.2 add_convert_fusion.2
  193.9 0.6 collective-permute-start.9
  194.5 0.0 collective-permute-done.12
  194.5 0.2 add_convert_fusion.1
  194.7 0.7 collective-permute-start.13
  195.4 3.0 %convolution_bitcast_fusion.7 = f32[2,256,1024]{2,1,0:T(8,128)S(1)} fusion(bf16[2,1536,1024]{2,1,0:T(8,128)(2,1)S(1)} %bitcast.113, bf16[256,1536]{1,0:T(8,128)(2,1)} %multiply_convert_fusion), kind=kOutput, calls=%fused_computation.24 | convolution fusion | flops 1610612736 | bytes 9175040 | tf_op jit(solution)/shard_map/td,edf->etf/dot_general | solution.py:178
  198.5 1.0 multiply_reduce_fusion.7
  199.5 0.0 collective-permute-done.1
  199.5 12.1 %collective-permute-done.5 = bf16[256,1536]{1,0:T(8,128)(2,1)S(1)} collective-permute-done((bf16[256,1536]{1,0:T(8,128)(2,1)S(1)}, bf16[256,1536]{1,0:T(8,128)(2,1)S(1)}, u32[]{:S(2)}, u32[]{:S(2)}) %collective-permute-start.5) | collective-permute-done | bytes 786464 | tf_op jit(solution)/shard_map/ppermute | solution.py:198
  211.6 18.4 %collective-permute-done.9 = bf16[256,1536]{1,0:T(8,128)(2,1)S(1)} collective-permute-done((bf16[256,1536]{1,0:T(8,128)(2,1)S(1)}, bf16[256,1536]{1,0:T(8,128)(2,1)S(1)}, u32[]{:S(2)}, u32[]{:S(2)}) %collective-permute-start.9) | collective-permute-done | bytes 786464 | tf_op jit(solution)/shard_map/ppermute | solution.py:198
  230.0 1.5 add_convert_fusion
  (33 shorter events, 0.1 us)
Async XLA Ops:
  6.5 133.0 %copy-start = (bf16[2,512,1536]{2,1,0:T(8,128)(2,1)S(1)}, bf16[2,512,1536]{2,1,0:T(8,128)(2,1)}, u32[]{:S(2)}) copy-start(bf16[2,512,1536]{2,1,0:T(8,128)(2,1)} %param.29) | copy-start | bytes 9437188
  6.5 81.9 %all-gather.2.cloned.1.call-start = ((), (), s32[]{:S(2)}) async-start(), calls=%async_computation | async-start | bytes 5242880 | tf_op jit(solution)/shard_map/all_gather | solution.py:252
  11.6 24.9 %copy-start.4 = (f32[256,8]{0,1:T(8,128)S(1)}, f32[256,8]{0,1:T(8,128)}, u32[]{:S(2)}) copy-start(f32[256,8]{0,1:T(8,128)} %param.27) | copy-start | bytes 24580
  11.6 24.9 %copy-start.5 = (s32[256,8]{0,1:T(8,128)S(1)}, s32[256,8]{0,1:T(8,128)}, u32[]{:S(2)}) copy-start(s32[256,8]{0,1:T(8,128)} %param.26) | copy-start | bytes 24580
  11.6 34.2 %copy-start.6 = (s32[8]{0:T(128)S(1)}, s32[8]{0:T(128)}, u32[]{:S(2)}) copy-start(s32[8]{0:T(128)} %param.23) | copy-start | bytes 100
  125.2 5.4 %copy-start.3 = (f32[1536]{0:T(1024)S(1)}, f32[1536]{0:T(1024)}, u32[]{:S(2)}) copy-start(f32[1536]{0:T(1024)} %param.25) | copy-start | bytes 18436
  129.4 1.2 copy-start.1
  131.7 3.0 %collective-permute-start = (bf16[256,1536]{1,0:T(8,128)(2,1)}, bf16[256,1536]{1,0:T(8,128)(2,1)}, u32[]{:S(2)}, u32[]{:S(2)}) collective-permute-start(bf16[256,1536]{1,0:T(8,128)(2,1)} %multiply_convert_fusion), channel_id=1, source_target_pairs={{0,1},{1,0},{2,3},{3,2},{4,5},{5,4},{6,7},{7,6},{8,9},{9,8},{10,11... | collective-permute-start | bytes 2359304 | tf_op jit(solution)/shard_map/ppermute | solution.py:201
  131.7 45.0 %collective-permute-start.10 = (bf16[256,1536]{1,0:T(8,128)(2,1)}, bf16[256,1536]{1,0:T(8,128)(2,1)S(1)}, u32[]{:S(2)}, u32[]{:S(2)}) collective-permute-start(bf16[256,1536]{1,0:T(8,128)(2,1)} %multiply_convert_fusion), channel_id=1, source_target_pairs={{0,6},{1,7},{2,0},{3,1},{4,2},{5,3},{6,4},{7,5},{8,14},{9,15},{10,... | collective-permute-start | bytes 2359304 | tf_op jit(solution)/shard_map/ppermute | solution.py:198
  133.1 41.2 %collective-permute-start.6 = (bf16[256,1536]{1,0:T(8,128)(2,1)}, bf16[256,1536]{1,0:T(8,128)(2,1)S(1)}, u32[]{:S(2)}, u32[]{:S(2)}) collective-permute-start(bf16[256,1536]{1,0:T(8,128)(2,1)} %multiply_convert_fusion), channel_id=1, source_target_pairs={{0,4},{1,5},{2,6},{3,7},{4,0},{5,1},{6,2},{7,3},{8,12},{9,13},{10,... | collective-permute-start | bytes 2359304 | tf_op jit(solution)/shard_map/ppermute | solution.py:198
  134.6 34.0 %collective-permute-start.2 = (bf16[256,1536]{1,0:T(8,128)(2,1)}, bf16[256,1536]{1,0:T(8,128)(2,1)S(1)}, u32[]{:S(2)}, u32[]{:S(2)}) collective-permute-start(bf16[256,1536]{1,0:T(8,128)(2,1)} %multiply_convert_fusion), channel_id=1, source_target_pairs={{0,2},{1,3},{2,4},{3,5},{4,6},{5,7},{6,0},{7,1},{8,10},{9,11},{10,... | collective-permute-start | bytes 2359304 | tf_op jit(solution)/shard_map/ppermute | solution.py:198
  139.6 35.3 %slice-start = ((s8[6291456]{0:T(1024)(128)(4,1)}), s8[4194304]{0:T(1024)(128)(4,1)S(1)}, s32[]{:S(2)}) async-start(s8[6291456]{0:T(1024)(128)(4,1)} %bitcast.112), calls=%async_computation.1 | async-start | bytes 8388608
  140.7 34.2 %slice-start.1 = ((s8[6291456]{0:T(1024)(128)(4,1)}), s8[2097152]{0:T(1024)(128)(4,1)S(1)}, s32[]{:S(2)}) async-start(s8[6291456]{0:T(1024)(128)(4,1)} %bitcast.112), calls=%async_computation.2 | async-start | bytes 4194304
  140.7 58.8 %collective-permute-start.1 = (bf16[256,1536]{1,0:T(8,128)(2,1)S(1)}, bf16[256,1536]{1,0:T(8,128)(2,1)S(1)}, u32[]{:S(2)}, u32[]{:S(2)}) collective-permute-start(bf16[256,1536]{1,0:T(8,128)(2,1)S(1)} %multiply_reduce_fusion.6), channel_id=1, source_target_pairs={{0,1},{1,0},{2,3},{3,2},{4,5},{5,4},{6,7},{7,6},{8,9},{9,8},{10,11... | collective-permute-start | bytes 2359304 | tf_op jit(solution)/shard_map/ppermute | solution.py:201
  174.3 6.4 %collective-permute-start.3 = (bf16[256,1536]{1,0:T(8,128)(2,1)S(1)}, bf16[256,1536]{1,0:T(8,128)(2,1)S(1)}, u32[]{:S(2)}, u32[]{:S(2)}) collective-permute-start(bf16[256,1536]{1,0:T(8,128)(2,1)S(1)} %collective-permute-done.2), channel_id=1, source_target_pairs={{0,1},{1,0},{2,3},{3,2},{4,5},{5,4},{6,7},{7,6},{8,9},{9,8},{10,11... | collective-permute-start | bytes 2359304 | tf_op jit(solution)/shard_map/ppermute | solution.py:201
  174.4 9.8 %collective-permute-start.7 = (bf16[256,1536]{1,0:T(8,128)(2,1)S(1)}, bf16[256,1536]{1,0:T(8,128)(2,1)S(1)}, u32[]{:S(2)}, u32[]{:S(2)}) collective-permute-start(bf16[256,1536]{1,0:T(8,128)(2,1)S(1)} %collective-permute-done.6), channel_id=1, source_target_pairs={{0,1},{1,0},{2,3},{3,2},{4,5},{5,4},{6,7},{7,6},{8,9},{9,8},{10,11... | collective-permute-start | bytes 2359304 | tf_op jit(solution)/shard_map/ppermute | solution.py:201
  176.7 10.8 %collective-permute-start.11 = (bf16[256,1536]{1,0:T(8,128)(2,1)S(1)}, bf16[256,1536]{1,0:T(8,128)(2,1)S(1)}, u32[]{:S(2)}, u32[]{:S(2)}) collective-permute-start(bf16[256,1536]{1,0:T(8,128)(2,1)S(1)} %collective-permute-done.10), channel_id=1, source_target_pairs={{0,1},{1,0},{2,3},{3,2},{4,5},{5,4},{6,7},{7,6},{8,9},{9,8},{10,11... | collective-permute-start | bytes 2359304 | tf_op jit(solution)/shard_map/ppermute | solution.py:201
  183.6 7.3 %collective-permute-start.4 = (bf16[256,1536]{1,0:T(8,128)(2,1)S(1)}, bf16[256,1536]{1,0:T(8,128)(2,1)S(1)}, u32[]{:S(2)}, u32[]{:S(2)}) collective-permute-start(bf16[256,1536]{1,0:T(8,128)(2,1)S(1)} %multiply_reduce_fusion.4), channel_id=1, source_target_pairs={{0,1},{1,0},{2,3},{3,2},{4,5},{5,4},{6,7},{7,6},{8,9},{9,8},{10,11... | collective-permute-start | bytes 2359304 | tf_op jit(solution)/shard_map/ppermute | solution.py:201
  187.3 6.4 %collective-permute-start.8 = (bf16[256,1536]{1,0:T(8,128)(2,1)S(1)}, bf16[256,1536]{1,0:T(8,128)(2,1)S(1)}, u32[]{:S(2)}, u32[]{:S(2)}) collective-permute-start(bf16[256,1536]{1,0:T(8,128)(2,1)S(1)} %multiply_reduce_fusion.2), channel_id=1, source_target_pairs={{0,1},{1,0},{2,3},{3,2},{4,5},{5,4},{6,7},{7,6},{8,9},{9,8},{10,11... | collective-permute-start | bytes 2359304 | tf_op jit(solution)/shard_map/ppermute | solution.py:201
  190.4 4.1 %collective-permute-start.12 = (bf16[256,1536]{1,0:T(8,128)(2,1)S(1)}, bf16[256,1536]{1,0:T(8,128)(2,1)S(1)}, u32[]{:S(2)}, u32[]{:S(2)}) collective-permute-start(bf16[256,1536]{1,0:T(8,128)(2,1)S(1)} %multiply_reduce_fusion), channel_id=1, source_target_pairs={{0,1},{1,0},{2,3},{3,2},{4,5},{5,4},{6,7},{7,6},{8,9},{9,8},{10,11... | collective-permute-start | bytes 2359304 | tf_op jit(solution)/shard_map/ppermute | solution.py:201
  191.1 20.5 %collective-permute-start.5 = (bf16[256,1536]{1,0:T(8,128)(2,1)S(1)}, bf16[256,1536]{1,0:T(8,128)(2,1)S(1)}, u32[]{:S(2)}, u32[]{:S(2)}) collective-permute-start(bf16[256,1536]{1,0:T(8,128)(2,1)S(1)} %add_convert_fusion.3), channel_id=1, source_target_pairs={{0,6},{1,7},{2,0},{3,1},{4,2},{5,3},{6,4},{7,5},{8,14},{9,15},{10,... | collective-permute-start | bytes 2359304 | tf_op jit(solution)/shard_map/ppermute | solution.py:198
  193.9 36.2 %collective-permute-start.9 = (bf16[256,1536]{1,0:T(8,128)(2,1)S(1)}, bf16[256,1536]{1,0:T(8,128)(2,1)S(1)}, u32[]{:S(2)}, u32[]{:S(2)}) collective-permute-start(bf16[256,1536]{1,0:T(8,128)(2,1)S(1)} %add_convert_fusion.2), channel_id=1, source_target_pairs={{0,4},{1,5},{2,6},{3,7},{4,0},{5,1},{6,2},{7,3},{8,12},{9,13},{10,... | collective-permute-start | bytes 2359304 | tf_op jit(solution)/shard_map/ppermute | solution.py:198
  194.7 35.3 %collective-permute-start.13 = (bf16[256,1536]{1,0:T(8,128)(2,1)S(1)}, bf16[256,1536]{1,0:T(8,128)(2,1)S(1)}, u32[]{:S(2)}, u32[]{:S(2)}) collective-permute-start(bf16[256,1536]{1,0:T(8,128)(2,1)S(1)} %add_convert_fusion.1), channel_id=1, source_target_pairs={{0,2},{1,3},{2,4},{3,5},{4,6},{5,7},{6,0},{7,1},{8,10},{9,11},{10,... | collective-permute-start | bytes 2359304 | tf_op jit(solution)/shard_map/ppermute | solution.py:198
  198.5 31.6 %copy-start.2 = (f32[256,1536]{1,0:T(8,128)S(1)}, f32[256,1536]{1,0:T(8,128)}, u32[]{:S(2)}) copy-start(f32[256,1536]{1,0:T(8,128)} %copy-done.1) | copy-start | bytes 4718596
Sparse Core Ops, SparseCore 0:
  8.9 79.4 all-gather.1

commit v8 on v6

--- a/solution.py
+++ b/solution.py
@@ -48,13 +48,7 @@
     for kv in range(KEY_VALUE_HEADS):
         key_at = kv * HEAD_WIDTH
         value_at = key_value_width + kv * HEAD_WIDTH
-        query_rows = jnp.concatenate(
-            [
-                queries_ref[:, (kv * heads_repeated + j) * HEAD_WIDTH : (kv * heads_repeated + j + 1) * HEAD_WIDTH]
-                for j in range(heads_repeated)
-            ],
-            0,
-        )
+        query_rows = queries_ref[0, kv]
         prompt_keys = prompt_ref[0, :, key_at : key_at + HEAD_WIDTH]
         prompt_values = prompt_ref[0, :, value_at : value_at + HEAD_WIDTH]
         cache_keys = jnp.concatenate([p[0, :, key_at : key_at + HEAD_WIDTH] for p in page_refs], 0)
@@ -83,10 +77,7 @@
             + jnp.dot(cache_exp.astype(jnp.bfloat16), cache_values, preferred_element_type=jnp.float32)
             + jnp.dot(tree_exp.astype(jnp.bfloat16), tree_values, preferred_element_type=jnp.float32)
         )
-        result = (numer / denom).astype(jnp.bfloat16)
-        for j in range(heads_repeated):
-            head = kv * heads_repeated + j
-            out_ref[:, head * HEAD_WIDTH : (head + 1) * HEAD_WIDTH] = result[j * TREE_TOKENS : (j + 1) * TREE_TOKENS]
+        out_ref[0, kv] = (numer / denom).astype(jnp.bfloat16)
 
 
 def attend(queries, draft_kv, piece, cache_page_store, page_table, cache_len, parents, groups):
@@ -96,6 +87,10 @@
     store_pages = cache_page_store.shape[0]
     visible = ancestry(parents).astype(jnp.float32)
     flat_pages = jnp.clip(page_table.reshape(-1), 0, store_pages - 1).astype(jnp.int32)
+    heads_repeated = QUERY_HEADS // KEY_VALUE_HEADS
+    rows = heads_repeated * TREE_TOKENS
+    head_queries = queries.reshape(count_of_requests, TREE_TOKENS, KEY_VALUE_HEADS, heads_repeated, HEAD_WIDTH)
+    head_queries = head_queries.transpose(0, 2, 3, 1, 4).reshape(count_of_requests, KEY_VALUE_HEADS, rows, HEAD_WIDTH)
     prompt_groups = jnp.clip(groups, 0, piece.shape[0] - 1).astype(jnp.int32)
 
     def page_spec(slot):
@@ -107,19 +102,21 @@
         num_scalar_prefetch=3,
         grid=(count_of_requests,),
         in_specs=[
-            pl.BlockSpec((TREE_TOKENS, width), lambda r, g, p, c: (r, 0)),
+            pl.BlockSpec((1, KEY_VALUE_HEADS, rows, HEAD_WIDTH), lambda r, g, p, c: (r, 0, 0, 0)),
             pl.BlockSpec((TREE_TOKENS, row_width), lambda r, g, p, c: (r, 0)),
             pl.BlockSpec((1, TREE_TOKENS, TREE_TOKENS), lambda r, g, p, c: (r, 0, 0)),
             pl.BlockSpec((1, piece.shape[1], row_width), lambda r, g, p, c: (g[r], 0, 0)),
         ]
         + [page_spec(slot) for slot in range(MAXP)],
-        out_specs=pl.BlockSpec((TREE_TOKENS, width), lambda r, g, p, c: (r, 0)),
-    )
-    return pl.pallas_call(
+        out_specs=pl.BlockSpec((1, KEY_VALUE_HEADS, rows, HEAD_WIDTH), lambda r, g, p, c: (r, 0, 0, 0)),
+    )
+    per_head = pl.pallas_call(
         attention_kernel,
         grid_spec=grid_spec,
-        out_shape=jax.ShapeDtypeStruct((count_of_tokens, width), jnp.bfloat16),
-    )(prompt_groups, flat_pages, cache_len.astype(jnp.int32), queries, draft_kv, visible, piece, *([cache_page_store] * MAXP))
+        out_shape=jax.ShapeDtypeStruct((count_of_requests, KEY_VALUE_HEADS, rows, HEAD_WIDTH), jnp.bfloat16),
+    )(prompt_groups, flat_pages, cache_len.astype(jnp.int32), head_queries, draft_kv, visible, piece, *([cache_page_store] * MAXP))
+    per_head = per_head.reshape(count_of_requests, KEY_VALUE_HEADS, heads_repeated, TREE_TOKENS, HEAD_WIDTH)
+    return per_head.transpose(0, 3, 1, 2, 4).reshape(count_of_tokens, width)
 
 
 def run_experts(rows, row_gate, w_in, w_down):

time: 236 us -> 244 us (1.034)
  local copies, waits for them, and re-layouts: 1.83 us -> 19.4 us
  waiting for transfers between devices: 121 us -> 112 us
    reshape x0 -> x3, local copies, waits for them, and re-layouts: none -> 13.8 us  [the longest x1 5.18 us: attend(): queries.reshape(count_of_requests, TREE_TOKENS, KEY_VALUE_HEADS, heads_re...]
    all_gather x1, waiting for transfers between devices: 65.6 us -> 58.8 us  [per_device(): piece = lax.all_gather(prompt_key_value, 'req', axis=1, tiled=True)]
    transpose x0 -> x1, local copies, waits for them, and re-layouts: none -> 3.76 us  [attend(): head_queries.transpose(0, 2, 3, 1, 4)]
  transfers between devices with their start and end apart: 15 -> 15, of which waited for: 5 -> 7; matrix products, arithmetic and copies ran while one was open for 16% -> 18% of each run, Pallas kernels for 0% -> 0%
where the time goes in v8:
time: 244 us; the launch traced here: 239 us
  waiting for transfers between devices  112 us (46%)
  matrix products  36.7 us (15%)
  Pallas kernels  34.8 us (14%)
  local copies, waits for them, and re-layouts  19.4 us (8%)
  between operations  13.8 us (6%)
  blocking collectives  9.22 us (4%)
  starting transfers between devices  8.67 us (4%)
  other arithmetic  4.65 us (2%)
    all_gather x1, waiting for transfers between devices, per_device(): piece = lax.all_gather(prompt_key_value, 'req', axis=1, tiled=True)  58.8 us
    ppermute x6, waiting for transfers between devices, chip_shift(): return lax.ppermute(x, 'exp', pairs)  51.9 us
    pallas_call x1, Pallas kernels, attend(): pl.pallas_call(attention_kernel, grid_spec=grid_spec, out_shape=jax.Shape...  34.8 us
    dot_general x8, matrix products, run_experts(): jnp.einsum('td,edf->etf', rows, w_in, preferred_element_type=jnp.float32)  21.7 us
    all_gather x1, blocking collectives, per_device(): gate_gathered = lax.all_gather(gate_local, 'exp', axis=0, tiled=True)  9.22 us
    dot_general x8, matrix products, run_experts(): jnp.einsum('etf,efd->etd', act, w_down, preferred_element_type=jnp.float32)  8.73 us
    ppermute x6, starting transfers between devices, chip_shift(): return lax.ppermute(x, 'exp', pairs)  7.24 us
    reshape x1, local copies, waits for them, and re-layouts, attend(): queries.reshape(count_of_requests, TREE_TOKENS, KEY_VALUE_HEADS, heads_re...  5.18 us
  transfers between devices with their start and end apart: 15, of which 7 were waited for; matrix products, arithmetic and copies ran while one was open for 18% of the time, Pallas kernels for 0%

profile of v8, /device:TPU:12, one launch (start us, length us, event | category | flops | bytes accessed | tf_op | source)
XLA Modules:
  0.0 239.0 jit_solution(11191021285796484805)
XLA Ops:
  6.5 0.7 all-gather.2.cloned.1.call-update
  7.3 0.9 broadcast_clamp_fusion
  8.2 0.6 min.37.pages_ref
  8.7 5.2 %reshape.47 = bf16[8,32,8,3,64]{4,3,2,1,0:T(4,128)(2,1)} reshape(bf16[256,1536]{1,0:T(8,128)(2,1)} %param.16) | data formatting | bytes 1572864 | tf_op jit(solution)/shard_map/reshape | solution.py:92
  13.9 3.8 %copy.23 = bf16[8,8,3,32,64]{4,3,2,1,0:T(8,128)(2,1)} copy(bf16[8,8,3,32,64]{4,2,1,3,0:T(4,128)(2,1)} %bitcast.121) | data formatting | bytes 1572864 | tf_op jit(solution)/shard_map/transpose | solution.py:93
  17.7 9.2 %all_gather.6 = f32[2048,16]{0,1:T(8,128)S(1)} all-gather(f32[256,16]{0,1:T(8,128)S(1)} %select_reduce_fusion), channel_id=1, replica_groups=mesh['req'=4,'exp'=8] {'exp'}, dimensions={0}, use_global_device_ids=true | all-gather | bytes 147456 | tf_op jit(solution)/shard_map/all_gather | solution.py:195
  26.9 0.6 broadcast_clamp_fusion.1.groups_ref
  27.5 0.4 convolution_minimum_fusion.4
  27.9 0.3 convolution_minimum_fusion.3
  28.2 0.3 convolution_minimum_fusion.2
  28.4 0.3 convolution_minimum_fusion.1
  28.7 0.9 fusion.1.visible_ref
  29.6 58.8 %all-gather.2.cloned.1.call-done.prompt_ref = bf16[2,1024,1024]{2,1,0:T(8,128)(2,1)} async-done(((bf16[2,256,1024]{2,1,0:T(8,128)(2,1)}), bf16[2,1024,1024]{2,1,0:T(8,128)(2,1)}) %all-gather.2.cloned.1.call-update) | async-done | bytes 4194320 | tf_op jit(solution)/shard_map/all_gather | solution.py:197
  88.4 34.8 %shard_map.145 = bf16[8,8,96,64]{3,2,1,0:T(8,128)(2,1)} custom-call(s32[8]{0:T(128)} %broadcast_clamp_fusion.1.groups_ref, s32[48]{0:T(128)} %min.37.pages_ref, s32[8]{0:T(128)} %lengths_ref.1, bf16[8,8,96,64]{3,2,1,0:T(8,128)(2,1)} %bitcast.122, bf16[256,1024]{1,0:T(8,128)(2,1)} %tree_ref.1, f32[8,32,32]{2,1,0:T(8,128)} %fusion.1.visible_ref, ...), custom_call_target="tpu_custom_call" | custom-call | tf_op jit(solution)/shard_map/pallas_call | solution.py:113
  123.2 3.8 %copy.44 = bf16[8,8,3,32,64]{4,2,1,3,0:T(4,128)(2,1)} copy(bf16[8,8,3,32,64]{4,3,2,1,0:T(8,128)(2,1)} %bitcast.123) | data formatting | bytes 1572864 | tf_op jit(solution)/shard_map/reshape | solution.py:118
  127.1 4.8 %reshape.50 = bf16[256,1536]{1,0:T(8,128)(2,1)} reshape(bf16[8,32,8,3,64]{4,3,2,1,0:T(4,128)(2,1)} %bitcast.120) | data formatting | bytes 1572864 | tf_op jit(solution)/shard_map/reshape | solution.py:119
  131.9 4.3 %multiply_reduce_fusion.8 = (f32[256]{0:T(256)S(1)}, f32[256,1536]{1,0:T(8,128)S(1)}) fusion(bf16[256,1536]{1,0:T(8,128)(2,1)} %reshape.50, bf16[1536,1536]{1,0:T(8,128)(2,1)} %param.24, bf16[256,1536]{1,0:T(8,128)(2,1)} %param.15), kind=kOutput, calls=%fused_computation.31 | convolution fusion | flops 1209532160 | bytes 7865344 | tf_op jit(solution)/shard_map/dot_general | solution.py:200
  136.2 1.1 copy-done.1
  137.3 1.1 multiply_convert_fusion
  138.4 0.0 collective-permute-start
  138.4 1.5 collective-permute-start.10
  139.8 1.5 collective-permute-start.6
  141.3 0.0 collective-permute-start.2
  141.4 0.0 collective-permute-done
  141.4 4.8 %convolution_bitcast_fusion.6 = f32[2,256,1024]{2,1,0:T(8,128)S(1)} fusion(bf16[2,1536,1024]{2,1,0:T(8,128)(2,1)} %param.28, bf16[256,1536]{1,0:T(8,128)(2,1)} %collective-permute-done), kind=kOutput, calls=%fused_computation.24 | convolution fusion | flops 1610612736 | bytes 9175040 | tf_op jit(solution)/shard_map/td,edf->etf/dot_general | solution.py:123
  146.3 0.0 slice-start
  146.3 1.1 multiply_reduce_fusion.6
  147.4 0.0 slice-start.1
  147.4 0.1 collective-permute-start.1
  147.5 11.4 %collective-permute-done.10 = bf16[256,1536]{1,0:T(8,128)(2,1)S(1)} collective-permute-done((bf16[256,1536]{1,0:T(8,128)(2,1)}, bf16[256,1536]{1,0:T(8,128)(2,1)S(1)}, u32[]{:S(2)}, u32[]{:S(2)}) %collective-permute-start.10) | collective-permute-done | bytes 786464 | tf_op jit(solution)/shard_map/ppermute | solution.py:143
  158.9 4.7 %convolution_bitcast_fusion.1 = f32[2,256,1024]{2,1,0:T(8,128)S(1)} fusion(bf16[2,1536,1024]{2,1,0:T(8,128)(2,1)} %param.28, bf16[256,1536]{1,0:T(8,128)(2,1)S(1)} %collective-permute-done.10), kind=kOutput, calls=%fused_computation.19 | convolution fusion | flops 1610612736 | bytes 9175040 | tf_op jit(solution)/shard_map/td,edf->etf/dot_general | solution.py:123
  163.6 1.1 multiply_reduce_fusion.1
  164.7 0.1 collective-permute-start.11
  164.8 11.8 %collective-permute-done.6 = bf16[256,1536]{1,0:T(8,128)(2,1)S(1)} collective-permute-done((bf16[256,1536]{1,0:T(8,128)(2,1)}, bf16[256,1536]{1,0:T(8,128)(2,1)S(1)}, u32[]{:S(2)}, u32[]{:S(2)}) %collective-permute-start.6) | collective-permute-done | bytes 786464 | tf_op jit(solution)/shard_map/ppermute | solution.py:143
  176.6 0.0 collective-permute-start.7
  176.6 1.8 convolution_bitcast_fusion.3
  178.4 1.8 convolution_bitcast_fusion.5
  180.2 0.6 collective-permute-start.3
  180.8 1.1 multiply_reduce_fusion.3
  181.9 1.1 multiply_reduce_fusion.5
  183.0 0.0 collective-permute-done.11
  183.0 1.8 convolution_bitcast_fusion
  184.8 1.1 multiply_reduce_fusion
  185.9 0.1 collective-permute-start.12
  186.0 2.0 convolution_bitcast_fusion.2
  188.0 1.1 multiply_reduce_fusion.2
  189.1 0.6 collective-permute-start.8
  189.6 1.8 convolution_bitcast_fusion.4
  191.4 1.1 multiply_reduce_fusion.4
  192.5 0.1 collective-permute-start.4
  192.6 0.2 add_convert_fusion.1
  192.8 0.6 collective-permute-start.13
  193.5 0.0 collective-permute-done.8
  193.5 0.2 add_convert_fusion.2
  193.7 1.0 collective-permute-start.9
  194.6 0.3 collective-permute-done.4
  194.9 0.2 add_convert_fusion.3
  195.1 2.7 %collective-permute-start.5 = (bf16[256,1536]{1,0:T(8,128)(2,1)S(1)}, bf16[256,1536]{1,0:T(8,128)(2,1)S(1)}, u32[]{:S(2)}, u32[]{:S(2)}) collective-permute-start(bf16[256,1536]{1,0:T(8,128)(2,1)S(1)} %add_convert_fusion.3), channel_id=1, source_target_pairs={{0,6},{1,7},{2,0},{3,1},{4,2},{5,3},{6,4},{7,5},{8,14},{9,15},{10,... | collective-permute-start | bytes 2359304 | tf_op jit(solution)/shard_map/ppermute | solution.py:143
  197.8 3.0 %convolution_bitcast_fusion.7 = f32[2,256,1024]{2,1,0:T(8,128)S(1)} fusion(bf16[2,1536,1024]{2,1,0:T(8,128)(2,1)S(1)} %bitcast.119, bf16[256,1536]{1,0:T(8,128)(2,1)} %multiply_convert_fusion), kind=kOutput, calls=%fused_computation.25 | convolution fusion | flops 1610612736 | bytes 9175040 | tf_op jit(solution)/shard_map/td,edf->etf/dot_general | solution.py:123
  200.8 1.1 multiply_reduce_fusion.7
  202.0 12.2 %collective-permute-done.13 = bf16[256,1536]{1,0:T(8,128)(2,1)S(1)} collective-permute-done((bf16[256,1536]{1,0:T(8,128)(2,1)S(1)}, bf16[256,1536]{1,0:T(8,128)(2,1)S(1)}, u32[]{:S(2)}, u32[]{:S(2)}) %collective-permute-start.13) | collective-permute-done | bytes 786464 | tf_op jit(solution)/shard_map/ppermute | solution.py:143
  214.2 16.1 %collective-permute-done.9 = bf16[256,1536]{1,0:T(8,128)(2,1)S(1)} collective-permute-done((bf16[256,1536]{1,0:T(8,128)(2,1)S(1)}, bf16[256,1536]{1,0:T(8,128)(2,1)S(1)}, u32[]{:S(2)}, u32[]{:S(2)}) %collective-permute-start.9) | collective-permute-done | bytes 786464 | tf_op jit(solution)/shard_map/ppermute | solution.py:143
  230.2 0.4 collective-permute-done.5
  230.6 1.5 add_convert_fusion
  (38 shorter events, 0.1 us)
Async XLA Ops:
  6.5 139.7 %copy-start = (bf16[2,512,1536]{2,1,0:T(8,128)(2,1)S(1)}, bf16[2,512,1536]{2,1,0:T(8,128)(2,1)}, u32[]{:S(2)}) copy-start(bf16[2,512,1536]{2,1,0:T(8,128)(2,1)} %param.29) | copy-start | bytes 9437188
  6.5 81.9 %all-gather.2.cloned.1.call-start = ((), (), s32[]{:S(2)}) async-start(), calls=%async_computation | async-start | bytes 5242880 | tf_op jit(solution)/shard_map/all_gather | solution.py:197
  8.7 9.0 %copy-start.4 = (f32[256,8]{0,1:T(8,128)S(1)}, f32[256,8]{0,1:T(8,128)}, u32[]{:S(2)}) copy-start(f32[256,8]{0,1:T(8,128)} %param.27) | copy-start | bytes 24580
  8.7 9.0 %copy-start.5 = (s32[256,8]{0,1:T(8,128)S(1)}, s32[256,8]{0,1:T(8,128)}, u32[]{:S(2)}) copy-start(s32[256,8]{0,1:T(8,128)} %param.26) | copy-start | bytes 24580
  8.7 18.2 %copy-start.7 = (s32[8]{0:T(128)S(1)}, s32[8]{0:T(128)}, u32[]{:S(2)}) copy-start(s32[8]{0:T(128)} %param.23) | copy-start | bytes 100
  8.7 18.8 %copy-start.6 = (s32[8,32]{1,0:T(8,128)S(1)}, s32[8,32]{1,0:T(8,128)}, u32[]{:S(2)}) copy-start(s32[8,32]{1,0:T(8,128)} %param.22) | copy-start | bytes 3076
  131.9 5.4 %copy-start.3 = (f32[1536]{0:T(1024)S(1)}, f32[1536]{0:T(1024)}, u32[]{:S(2)}) copy-start(f32[1536]{0:T(1024)} %param.25) | copy-start | bytes 18436
  136.1 1.2 copy-start.1
  138.4 3.0 %collective-permute-start = (bf16[256,1536]{1,0:T(8,128)(2,1)}, bf16[256,1536]{1,0:T(8,128)(2,1)}, u32[]{:S(2)}, u32[]{:S(2)}) collective-permute-start(bf16[256,1536]{1,0:T(8,128)(2,1)} %multiply_convert_fusion), channel_id=1, source_target_pairs={{0,1},{1,0},{2,3},{3,2},{4,5},{5,4},{6,7},{7,6},{8,9},{9,8},{10,11... | collective-permute-start | bytes 2359304 | tf_op jit(solution)/shard_map/ppermute | solution.py:146
  138.4 20.5 %collective-permute-start.10 = (bf16[256,1536]{1,0:T(8,128)(2,1)}, bf16[256,1536]{1,0:T(8,128)(2,1)S(1)}, u32[]{:S(2)}, u32[]{:S(2)}) collective-permute-start(bf16[256,1536]{1,0:T(8,128)(2,1)} %multiply_convert_fusion), channel_id=1, source_target_pairs={{0,6},{1,7},{2,0},{3,1},{4,2},{5,3},{6,4},{7,5},{8,14},{9,15},{10,... | collective-permute-start | bytes 2359304 | tf_op jit(solution)/shard_map/ppermute | solution.py:143
  139.8 36.7 %collective-permute-start.6 = (bf16[256,1536]{1,0:T(8,128)(2,1)}, bf16[256,1536]{1,0:T(8,128)(2,1)S(1)}, u32[]{:S(2)}, u32[]{:S(2)}) collective-permute-start(bf16[256,1536]{1,0:T(8,128)(2,1)} %multiply_convert_fusion), channel_id=1, source_target_pairs={{0,4},{1,5},{2,6},{3,7},{4,0},{5,1},{6,2},{7,3},{8,12},{9,13},{10,... | collective-permute-start | bytes 2359304 | tf_op jit(solution)/shard_map/ppermute | solution.py:143
  141.3 37.1 %collective-permute-start.2 = (bf16[256,1536]{1,0:T(8,128)(2,1)}, bf16[256,1536]{1,0:T(8,128)(2,1)S(1)}, u32[]{:S(2)}, u32[]{:S(2)}) collective-permute-start(bf16[256,1536]{1,0:T(8,128)(2,1)} %multiply_convert_fusion), channel_id=1, source_target_pairs={{0,2},{1,3},{2,4},{3,5},{4,6},{5,7},{6,0},{7,1},{8,10},{9,11},{10,... | collective-permute-start | bytes 2359304 | tf_op jit(solution)/shard_map/ppermute | solution.py:143
  146.3 30.3 %slice-start = ((s8[6291456]{0:T(1024)(128)(4,1)}), s8[4194304]{0:T(1024)(128)(4,1)S(1)}, s32[]{:S(2)}) async-start(s8[6291456]{0:T(1024)(128)(4,1)} %bitcast.118), calls=%async_computation.1 | async-start | bytes 8388608
  147.4 29.2 %slice-start.1 = ((s8[6291456]{0:T(1024)(128)(4,1)}), s8[2097152]{0:T(1024)(128)(4,1)S(1)}, s32[]{:S(2)}) async-start(s8[6291456]{0:T(1024)(128)(4,1)} %bitcast.118), calls=%async_computation.2 | async-start | bytes 4194304
  147.4 54.5 %collective-permute-start.1 = (bf16[256,1536]{1,0:T(8,128)(2,1)S(1)}, bf16[256,1536]{1,0:T(8,128)(2,1)S(1)}, u32[]{:S(2)}, u32[]{:S(2)}) collective-permute-start(bf16[256,1536]{1,0:T(8,128)(2,1)S(1)} %multiply_reduce_fusion.6), channel_id=1, source_target_pairs={{0,1},{1,0},{2,3},{3,2},{4,5},{5,4},{6,7},{7,6},{8,9},{9,8},{10,11... | collective-permute-start | bytes 2359304 | tf_op jit(solution)/shard_map/ppermute | solution.py:146
  164.7 18.2 %collective-permute-start.11 = (bf16[256,1536]{1,0:T(8,128)(2,1)S(1)}, bf16[256,1536]{1,0:T(8,128)(2,1)S(1)}, u32[]{:S(2)}, u32[]{:S(2)}) collective-permute-start(bf16[256,1536]{1,0:T(8,128)(2,1)S(1)} %collective-permute-done.10), channel_id=1, source_target_pairs={{0,1},{1,0},{2,3},{3,2},{4,5},{5,4},{6,7},{7,6},{8,9},{9,8},{10,11... | collective-permute-start | bytes 2359304 | tf_op jit(solution)/shard_map/ppermute | solution.py:146
  176.6 9.4 %collective-permute-start.7 = (bf16[256,1536]{1,0:T(8,128)(2,1)S(1)}, bf16[256,1536]{1,0:T(8,128)(2,1)S(1)}, u32[]{:S(2)}, u32[]{:S(2)}) collective-permute-start(bf16[256,1536]{1,0:T(8,128)(2,1)S(1)} %collective-permute-done.6), channel_id=1, source_target_pairs={{0,1},{1,0},{2,3},{3,2},{4,5},{5,4},{6,7},{7,6},{8,9},{9,8},{10,11... | collective-permute-start | bytes 2359304 | tf_op jit(solution)/shard_map/ppermute | solution.py:146
  180.2 9.4 %collective-permute-start.3 = (bf16[256,1536]{1,0:T(8,128)(2,1)S(1)}, bf16[256,1536]{1,0:T(8,128)(2,1)S(1)}, u32[]{:S(2)}, u32[]{:S(2)}) collective-permute-start(bf16[256,1536]{1,0:T(8,128)(2,1)S(1)} %collective-permute-done.2), channel_id=1, source_target_pairs={{0,1},{1,0},{2,3},{3,2},{4,5},{5,4},{6,7},{7,6},{8,9},{9,8},{10,11... | collective-permute-start | bytes 2359304 | tf_op jit(solution)/shard_map/ppermute | solution.py:146
  185.9 6.8 %collective-permute-start.12 = (bf16[256,1536]{1,0:T(8,128)(2,1)S(1)}, bf16[256,1536]{1,0:T(8,128)(2,1)S(1)}, u32[]{:S(2)}, u32[]{:S(2)}) collective-permute-start(bf16[256,1536]{1,0:T(8,128)(2,1)S(1)} %multiply_reduce_fusion), channel_id=1, source_target_pairs={{0,1},{1,0},{2,3},{3,2},{4,5},{5,4},{6,7},{7,6},{8,9},{9,8},{10,11... | collective-permute-start | bytes 2359304 | tf_op jit(solution)/shard_map/ppermute | solution.py:146
  189.1 4.4 %collective-permute-start.8 = (bf16[256,1536]{1,0:T(8,128)(2,1)S(1)}, bf16[256,1536]{1,0:T(8,128)(2,1)S(1)}, u32[]{:S(2)}, u32[]{:S(2)}) collective-permute-start(bf16[256,1536]{1,0:T(8,128)(2,1)S(1)} %multiply_reduce_fusion.2), channel_id=1, source_target_pairs={{0,1},{1,0},{2,3},{3,2},{4,5},{5,4},{6,7},{7,6},{8,9},{9,8},{10,11... | collective-permute-start | bytes 2359304 | tf_op jit(solution)/shard_map/ppermute | solution.py:146
  192.5 2.4 collective-permute-start.4
  192.8 21.3 %collective-permute-start.13 = (bf16[256,1536]{1,0:T(8,128)(2,1)S(1)}, bf16[256,1536]{1,0:T(8,128)(2,1)S(1)}, u32[]{:S(2)}, u32[]{:S(2)}) collective-permute-start(bf16[256,1536]{1,0:T(8,128)(2,1)S(1)} %add_convert_fusion.1), channel_id=1, source_target_pairs={{0,2},{1,3},{2,4},{3,5},{4,6},{5,7},{6,0},{7,1},{8,10},{9,11},{10,... | collective-permute-start | bytes 2359304 | tf_op jit(solution)/shard_map/ppermute | solution.py:143
  193.7 36.6 %collective-permute-start.9 = (bf16[256,1536]{1,0:T(8,128)(2,1)S(1)}, bf16[256,1536]{1,0:T(8,128)(2,1)S(1)}, u32[]{:S(2)}, u32[]{:S(2)}) collective-permute-start(bf16[256,1536]{1,0:T(8,128)(2,1)S(1)} %add_convert_fusion.2), channel_id=1, source_target_pairs={{0,4},{1,5},{2,6},{3,7},{4,0},{5,1},{6,2},{7,3},{8,12},{9,13},{10,... | collective-permute-start | bytes 2359304 | tf_op jit(solution)/shard_map/ppermute | solution.py:143
  195.1 35.5 %collective-permute-start.5 = (bf16[256,1536]{1,0:T(8,128)(2,1)S(1)}, bf16[256,1536]{1,0:T(8,128)(2,1)S(1)}, u32[]{:S(2)}, u32[]{:S(2)}) collective-permute-start(bf16[256,1536]{1,0:T(8,128)(2,1)S(1)} %add_convert_fusion.3), channel_id=1, source_target_pairs={{0,6},{1,7},{2,0},{3,1},{4,2},{5,3},{6,4},{7,5},{8,14},{9,15},{10,... | collective-permute-start | bytes 2359304 | tf_op jit(solution)/shard_map/ppermute | solution.py:143
  200.8 29.8 %copy-start.2 = (f32[256,1536]{1,0:T(8,128)S(1)}, f32[256,1536]{1,0:T(8,128)}, u32[]{:S(2)}) copy-start(f32[256,1536]{1,0:T(8,128)} %copy-done.1) | copy-start | bytes 4718596
Sparse Core Ops, SparseCore 0:
  8.9 79.4 all-gather.1

commit v9 on v6

--- a/solution.py
+++ b/solution.py
@@ -197,7 +197,15 @@
     )
     gate_gathered = lax.all_gather(gate_local, "exp", axis=0, tiled=True)
     gate = lax.dynamic_slice_in_dim(gate_gathered, lax.axis_index("exp") * local_experts, local_experts, 1)
-    piece = lax.all_gather(prompt_key_value, "req", axis=1, tiled=True)
+    columns = lax.axis_size("req")
+    piece = jnp.concatenate(
+        [prompt_key_value]
+        + [
+            lax.ppermute(prompt_key_value, "req", [(s, (s + d) % columns) for s in range(columns)])
+            for d in range(1, columns)
+        ],
+        1,
+    )
     gate, piece = lax.optimization_barrier((gate, piece))
     attended = attend(queries, draft_kv, piece, cache_page_store, page_table, cache_len, parents, groups)
     mixed = resid.astype(jnp.float32) + jnp.dot(attended, w_out, preferred_element_type=jnp.float32)

time: 236 us -> 235 us (level)
  between operations: 13.8 us -> 0.38 us
  starting transfers between devices: 7.21 us -> 14.4 us
  other arithmetic: 6.04 us -> 9.47 us
  waiting for transfers between devices: 121 us -> 124 us
    ppermute x0 -> x3, waiting for transfers between devices: none -> 72.1 us  [per_device(): lax.ppermute(prompt_key_value, 'req', [(s, (s + d) % columns) for s in ra...]
    all_gather x1 -> x0, waiting for transfers between devices: 65.6 us -> none  [per_device(): piece = lax.all_gather(prompt_key_value, 'req', axis=1, tiled=True)]
    ppermute x0 -> x3, starting transfers between devices: none -> 5.51 us  [per_device(): lax.ppermute(prompt_key_value, 'req', [(s, (s + d) % columns) for s in ra...]
    concatenate x0 -> x1, other arithmetic: none -> 3.62 us  [per_device(): jnp.concatenate([prompt_key_value] + [lax.ppermute(prompt_key_value, 'req...]
  transfers between devices with their start and end apart: 15 -> 17, of which waited for: 5 -> 9; matrix products, arithmetic and copies ran while one was open for 16% -> 16% of each run, Pallas kernels for 0% -> 0%
where the time goes in v9:
time: 235 us; the launch traced here: 233 us
  waiting for transfers between devices  124 us (53%)
  matrix products  37.4 us (16%)
  Pallas kernels  35.7 us (15%)
  starting transfers between devices  14.4 us (6%)
  other arithmetic  9.47 us (4%)
  blocking collectives  9.22 us (4%)
    ppermute x3, waiting for transfers between devices, per_device(): lax.ppermute(prompt_key_value, 'req', [(s, (s + d) % columns) for s in ra...  72.1 us
    ppermute x6, waiting for transfers between devices, chip_shift(): return lax.ppermute(x, 'exp', pairs)  51.9 us
    pallas_call x1, Pallas kernels, attend(): pl.pallas_call(attention_kernel, grid_spec=grid_spec, out_shape=jax.Shape...  35.7 us
    dot_general x8, matrix products, run_experts(): jnp.einsum('td,edf->etf', rows, w_in, preferred_element_type=jnp.float32)  21.7 us
    all_gather x1, blocking collectives, per_device(): gate_gathered = lax.all_gather(gate_local, 'exp', axis=0, tiled=True)  9.22 us
    dot_general x8, matrix products, run_experts(): jnp.einsum('etf,efd->etd', act, w_down, preferred_element_type=jnp.float32)  8.65 us
    ppermute x6, starting transfers between devices, chip_shift(): return lax.ppermute(x, 'exp', pairs)  7.4 us
    ppermute x3, starting transfers between devices, per_device(): lax.ppermute(prompt_key_value, 'req', [(s, (s + d) % columns) for s in ra...  5.51 us
  transfers between devices with their start and end apart: 17, of which 9 were waited for; matrix products, arithmetic and copies ran while one was open for 16% of the time, Pallas kernels for 0%

profile of v9, /device:TPU:12, one launch (start us, length us, event | category | flops | bytes accessed | tf_op | source)
XLA Modules:
  0.0 232.5 jit_solution(16435473722061317996)
XLA Ops:
  0.0 0.4 collective-permute-start.2
  0.5 2.6 %collective-permute-start.1 = (bf16[2,256,1024]{2,1,0:T(8,128)(2,1)}, bf16[2,256,1024]{2,1,0:T(8,128)(2,1)}, u32[]{:S(2)}, u32[]{:S(2)}) collective-permute-start(bf16[2,256,1024]{2,1,0:T(8,128)(2,1)} %param.18), channel_id=1, source_target_pairs={{0,16},{8,24},{16,0},{24,8},{1,17},{9,25},{17,1},{25,9},{2,18},{10... | collective-permute-start | bytes 3145736 | tf_op jit(solution)/shard_map/ppermute | solution.py:204
  3.0 2.5 %collective-permute-start = (bf16[2,256,1024]{2,1,0:T(8,128)(2,1)}, bf16[2,256,1024]{2,1,0:T(8,128)(2,1)}, u32[]{:S(2)}, u32[]{:S(2)}) collective-permute-start(bf16[2,256,1024]{2,1,0:T(8,128)(2,1)} %param.18), channel_id=1, source_target_pairs={{0,8},{8,16},{16,24},{24,0},{1,9},{9,17},{17,25},{25,1},{2,10},{10... | collective-permute-start | bytes 3145736 | tf_op jit(solution)/shard_map/ppermute | solution.py:204
  5.5 0.7 broadcast_clamp_fusion
  6.2 0.6 min.37.pages_ref
  6.8 0.7 select_reduce_fusion
  7.5 9.2 %all_gather.3 = f32[2048,16]{0,1:T(8,128)S(1)} all-gather(f32[256,16]{0,1:T(8,128)S(1)} %select_reduce_fusion), channel_id=1, replica_groups=mesh['req'=4,'exp'=8] {'exp'}, dimensions={0}, use_global_device_ids=true | all-gather | bytes 147456 | tf_op jit(solution)/shard_map/all_gather | solution.py:198
  16.8 1.1 convolution_minimum_fusion.4
  17.9 1.2 broadcast_clamp_fusion.1.groups_ref
  19.2 0.3 convolution_minimum_fusion.3
  19.4 0.3 convolution_minimum_fusion.2
  19.7 0.3 convolution_minimum_fusion.1
  19.9 0.9 fusion.1.visible_ref
  20.8 50.5 %collective-permute-done.2 = bf16[2,256,1024]{2,1,0:T(8,128)(2,1)} collective-permute-done((bf16[2,256,1024]{2,1,0:T(8,128)(2,1)}, bf16[2,256,1024]{2,1,0:T(8,128)(2,1)}, u32[]{:S(2)}, u32[]{:S(2)}) %collective-permute-start.2) | collective-permute-done | bytes 1048608 | tf_op jit(solution)/shard_map/ppermute | solution.py:204
  71.3 0.1 collective-permute-done.1
  71.4 21.6 %collective-permute-done = bf16[2,256,1024]{2,1,0:T(8,128)(2,1)} collective-permute-done((bf16[2,256,1024]{2,1,0:T(8,128)(2,1)}, bf16[2,256,1024]{2,1,0:T(8,128)(2,1)}, u32[]{:S(2)}, u32[]{:S(2)}) %collective-permute-start) | collective-permute-done | bytes 1048608 | tf_op jit(solution)/shard_map/ppermute | solution.py:204
  93.0 3.6 %pad_maximum_fusion.prompt_ref = bf16[2,1024,1024]{2,1,0:T(8,128)(2,1)} fusion(bf16[2,256,1024]{2,1,0:T(8,128)(2,1)} %collective-permute-done.2, bf16[2,256,1024]{2,1,0:T(8,128)(2,1)} %collective-permute-done.1, bf16[2,256,1024]{2,1,0:T(8,128)(2,1)} %collective-permute-done, bf16[2,256,1024]{2,1,0:T(8,128)(2,1)} %param.18), kind=kLoop, calls=%fused_computation | loop fusion | flops 16777216 | bytes 8388608 | tf_op jit(solution)/shard_map/concatenate | solution.py:201
  96.6 35.7 %shard_map.145 = bf16[256,1536]{1,0:T(8,128)(2,1)} custom-call(s32[8]{0:T(128)} %broadcast_clamp_fusion.1.groups_ref, s32[48]{0:T(128)} %min.37.pages_ref, s32[8]{0:T(128)} %lengths_ref.1, bf16[256,1536]{1,0:T(8,128)(2,1)} %queries_ref.1, bf16[256,1024]{1,0:T(8,128)(2,1)} %tree_ref.1, f32[8,32,32]{2,1,0:T(8,128)} %fusion.1.visible_ref, ...), custom_call_target="tpu_custom_call" | custom-call | tf_op jit(solution)/shard_map/pallas_call | solution.py:118
  132.3 4.3 %multiply_reduce_fusion.8 = (f32[256]{0:T(256)S(1)}, f32[256,1536]{1,0:T(8,128)S(1)}) fusion(bf16[256,1536]{1,0:T(8,128)(2,1)} %shard_map.145, bf16[1536,1536]{1,0:T(8,128)(2,1)} %param.24, bf16[256,1536]{1,0:T(8,128)(2,1)} %param.15), kind=kOutput, calls=%fused_computation.31 | convolution fusion | flops 1209532160 | bytes 7865344 | tf_op jit(solution)/shard_map/dot_general | solution.py:211
  136.6 1.1 copy-done.1
  137.7 1.1 multiply_convert_fusion
  138.8 0.0 collective-permute-start.3
  138.8 1.4 collective-permute-start.13
  140.2 1.5 collective-permute-start.9
  141.7 0.0 collective-permute-start.5
  141.8 0.0 collective-permute-done.3
  141.9 4.8 %convolution_bitcast_fusion.6 = f32[2,256,1024]{2,1,0:T(8,128)S(1)} fusion(bf16[2,1536,1024]{2,1,0:T(8,128)(2,1)} %param.28, bf16[256,1536]{1,0:T(8,128)(2,1)} %collective-permute-done.3), kind=kOutput, calls=%fused_computation.24 | convolution fusion | flops 1610612736 | bytes 9175040 | tf_op jit(solution)/shard_map/td,edf->etf/dot_general | solution.py:126
  146.7 0.0 slice-start
  146.7 1.1 multiply_reduce_fusion.6
  147.8 0.0 slice-start.1
  147.8 0.1 collective-permute-start.4
  147.9 11.4 %collective-permute-done.13 = bf16[256,1536]{1,0:T(8,128)(2,1)S(1)} collective-permute-done((bf16[256,1536]{1,0:T(8,128)(2,1)}, bf16[256,1536]{1,0:T(8,128)(2,1)S(1)}, u32[]{:S(2)}, u32[]{:S(2)}) %collective-permute-start.13) | collective-permute-done | bytes 786464 | tf_op jit(solution)/shard_map/ppermute | solution.py:146
  159.3 4.7 %convolution_bitcast_fusion.1 = f32[2,256,1024]{2,1,0:T(8,128)S(1)} fusion(bf16[2,1536,1024]{2,1,0:T(8,128)(2,1)} %param.28, bf16[256,1536]{1,0:T(8,128)(2,1)S(1)} %collective-permute-done.13), kind=kOutput, calls=%fused_computation.19 | convolution fusion | flops 1610612736 | bytes 9175040 | tf_op jit(solution)/shard_map/td,edf->etf/dot_general | solution.py:126
  164.0 1.0 multiply_reduce_fusion.1
  165.1 0.1 collective-permute-start.14
  165.1 11.8 %collective-permute-done.9 = bf16[256,1536]{1,0:T(8,128)(2,1)S(1)} collective-permute-done((bf16[256,1536]{1,0:T(8,128)(2,1)}, bf16[256,1536]{1,0:T(8,128)(2,1)S(1)}, u32[]{:S(2)}, u32[]{:S(2)}) %collective-permute-start.9) | collective-permute-done | bytes 786464 | tf_op jit(solution)/shard_map/ppermute | solution.py:146
  177.0 1.8 convolution_bitcast_fusion.3
  178.8 0.0 collective-permute-done.5
  178.8 1.8 convolution_bitcast_fusion.5
  180.6 0.6 collective-permute-start.6
  181.1 1.1 multiply_reduce_fusion.3
  182.2 1.1 multiply_reduce_fusion.5
  183.3 1.8 convolution_bitcast_fusion
  185.1 1.1 multiply_reduce_fusion
  186.2 0.1 collective-permute-start.15
  186.3 2.0 convolution_bitcast_fusion.2
  188.3 1.1 multiply_reduce_fusion.2
  189.4 0.6 collective-permute-start.11
  190.0 1.8 convolution_bitcast_fusion.4
  191.8 1.1 multiply_reduce_fusion.4
  192.9 0.1 collective-permute-start.7
  193.0 0.2 add_convert_fusion.1
  193.2 0.7 collective-permute-start.16
  193.8 0.2 add_convert_fusion.2
  194.1 1.0 collective-permute-start.12
  195.1 0.2 collective-permute-done.7
  195.2 0.2 add_convert_fusion.3
  195.4 2.8 %collective-permute-start.8 = (bf16[256,1536]{1,0:T(8,128)(2,1)S(1)}, bf16[256,1536]{1,0:T(8,128)(2,1)S(1)}, u32[]{:S(2)}, u32[]{:S(2)}) collective-permute-start(bf16[256,1536]{1,0:T(8,128)(2,1)S(1)} %add_convert_fusion.3), channel_id=1, source_target_pairs={{0,6},{1,7},{2,0},{3,1},{4,2},{5,3},{6,4},{7,5},{8,14},{9,15},{10,... | collective-permute-start | bytes 2359304 | tf_op jit(solution)/shard_map/ppermute | solution.py:146
  198.2 3.0 %convolution_bitcast_fusion.7 = f32[2,256,1024]{2,1,0:T(8,128)S(1)} fusion(bf16[2,1536,1024]{2,1,0:T(8,128)(2,1)S(1)} %bitcast.113, bf16[256,1536]{1,0:T(8,128)(2,1)} %multiply_convert_fusion), kind=kOutput, calls=%fused_computation.25 | convolution fusion | flops 1610612736 | bytes 9175040 | tf_op jit(solution)/shard_map/td,edf->etf/dot_general | solution.py:126
  201.3 1.1 multiply_reduce_fusion.7
  202.4 12.1 %collective-permute-done.16 = bf16[256,1536]{1,0:T(8,128)(2,1)S(1)} collective-permute-done((bf16[256,1536]{1,0:T(8,128)(2,1)S(1)}, bf16[256,1536]{1,0:T(8,128)(2,1)S(1)}, u32[]{:S(2)}, u32[]{:S(2)}) %collective-permute-start.16) | collective-permute-done | bytes 786464 | tf_op jit(solution)/shard_map/ppermute | solution.py:146
  214.5 16.1 %collective-permute-done.12 = bf16[256,1536]{1,0:T(8,128)(2,1)S(1)} collective-permute-done((bf16[256,1536]{1,0:T(8,128)(2,1)S(1)}, bf16[256,1536]{1,0:T(8,128)(2,1)S(1)}, u32[]{:S(2)}, u32[]{:S(2)}) %collective-permute-start.12) | collective-permute-done | bytes 786464 | tf_op jit(solution)/shard_map/ppermute | solution.py:146
  230.6 0.4 collective-permute-done.8
  231.0 1.5 add_convert_fusion
  (30 shorter events, 0.1 us)
Async XLA Ops:
  0.0 146.7 %copy-start = (bf16[2,512,1536]{2,1,0:T(8,128)(2,1)S(1)}, bf16[2,512,1536]{2,1,0:T(8,128)(2,1)}, u32[]{:S(2)}) copy-start(bf16[2,512,1536]{2,1,0:T(8,128)(2,1)} %param.29) | copy-start | bytes 9437188
  0.0 71.3 %collective-permute-start.2 = (bf16[2,256,1024]{2,1,0:T(8,128)(2,1)}, bf16[2,256,1024]{2,1,0:T(8,128)(2,1)}, u32[]{:S(2)}, u32[]{:S(2)}) collective-permute-start(bf16[2,256,1024]{2,1,0:T(8,128)(2,1)} %param.18), channel_id=1, source_target_pairs={{0,24},{8,0},{16,8},{24,16},{1,25},{9,1},{17,9},{25,17},{2,26},{10... | collective-permute-start | bytes 3145736 | tf_op jit(solution)/shard_map/ppermute | solution.py:204
  0.5 70.9 %collective-permute-start.1 = (bf16[2,256,1024]{2,1,0:T(8,128)(2,1)}, bf16[2,256,1024]{2,1,0:T(8,128)(2,1)}, u32[]{:S(2)}, u32[]{:S(2)}) collective-permute-start(bf16[2,256,1024]{2,1,0:T(8,128)(2,1)} %param.18), channel_id=1, source_target_pairs={{0,16},{8,24},{16,0},{24,8},{1,17},{9,25},{17,1},{25,9},{2,18},{10... | collective-permute-start | bytes 3145736 | tf_op jit(solution)/shard_map/ppermute | solution.py:204
  3.0 89.9 %collective-permute-start = (bf16[2,256,1024]{2,1,0:T(8,128)(2,1)}, bf16[2,256,1024]{2,1,0:T(8,128)(2,1)}, u32[]{:S(2)}, u32[]{:S(2)}) collective-permute-start(bf16[2,256,1024]{2,1,0:T(8,128)(2,1)} %param.18), channel_id=1, source_target_pairs={{0,8},{8,16},{16,24},{24,0},{1,9},{9,17},{17,25},{25,1},{2,10},{10... | collective-permute-start | bytes 3145736 | tf_op jit(solution)/shard_map/ppermute | solution.py:204
  132.3 5.4 %copy-start.3 = (f32[1536]{0:T(1024)S(1)}, f32[1536]{0:T(1024)}, u32[]{:S(2)}) copy-start(f32[1536]{0:T(1024)} %param.25) | copy-start | bytes 18436
  136.5 1.2 copy-start.1
  138.8 3.1 %collective-permute-start.3 = (bf16[256,1536]{1,0:T(8,128)(2,1)}, bf16[256,1536]{1,0:T(8,128)(2,1)}, u32[]{:S(2)}, u32[]{:S(2)}) collective-permute-start(bf16[256,1536]{1,0:T(8,128)(2,1)} %multiply_convert_fusion), channel_id=1, source_target_pairs={{0,1},{1,0},{2,3},{3,2},{4,5},{5,4},{6,7},{7,6},{8,9},{9,8},{10,11... | collective-permute-start | bytes 2359304 | tf_op jit(solution)/shard_map/ppermute | solution.py:149
  138.8 20.5 %collective-permute-start.13 = (bf16[256,1536]{1,0:T(8,128)(2,1)}, bf16[256,1536]{1,0:T(8,128)(2,1)S(1)}, u32[]{:S(2)}, u32[]{:S(2)}) collective-permute-start(bf16[256,1536]{1,0:T(8,128)(2,1)} %multiply_convert_fusion), channel_id=1, source_target_pairs={{0,6},{1,7},{2,0},{3,1},{4,2},{5,3},{6,4},{7,5},{8,14},{9,15},{10,... | collective-permute-start | bytes 2359304 | tf_op jit(solution)/shard_map/ppermute | solution.py:146
  140.2 36.7 %collective-permute-start.9 = (bf16[256,1536]{1,0:T(8,128)(2,1)}, bf16[256,1536]{1,0:T(8,128)(2,1)S(1)}, u32[]{:S(2)}, u32[]{:S(2)}) collective-permute-start(bf16[256,1536]{1,0:T(8,128)(2,1)} %multiply_convert_fusion), channel_id=1, source_target_pairs={{0,4},{1,5},{2,6},{3,7},{4,0},{5,1},{6,2},{7,3},{8,12},{9,13},{10,... | collective-permute-start | bytes 2359304 | tf_op jit(solution)/shard_map/ppermute | solution.py:146
  141.7 37.0 %collective-permute-start.5 = (bf16[256,1536]{1,0:T(8,128)(2,1)}, bf16[256,1536]{1,0:T(8,128)(2,1)S(1)}, u32[]{:S(2)}, u32[]{:S(2)}) collective-permute-start(bf16[256,1536]{1,0:T(8,128)(2,1)} %multiply_convert_fusion), channel_id=1, source_target_pairs={{0,2},{1,3},{2,4},{3,5},{4,6},{5,7},{6,0},{7,1},{8,10},{9,11},{10,... | collective-permute-start | bytes 2359304 | tf_op jit(solution)/shard_map/ppermute | solution.py:146
  146.7 30.2 %slice-start = ((s8[6291456]{0:T(1024)(128)(4,1)}), s8[4194304]{0:T(1024)(128)(4,1)S(1)}, s32[]{:S(2)}) async-start(s8[6291456]{0:T(1024)(128)(4,1)} %bitcast.112), calls=%async_computation | async-start | bytes 8388608
  147.8 29.1 %slice-start.1 = ((s8[6291456]{0:T(1024)(128)(4,1)}), s8[2097152]{0:T(1024)(128)(4,1)S(1)}, s32[]{:S(2)}) async-start(s8[6291456]{0:T(1024)(128)(4,1)} %bitcast.112), calls=%async_computation.1 | async-start | bytes 4194304
  147.8 54.5 %collective-permute-start.4 = (bf16[256,1536]{1,0:T(8,128)(2,1)S(1)}, bf16[256,1536]{1,0:T(8,128)(2,1)S(1)}, u32[]{:S(2)}, u32[]{:S(2)}) collective-permute-start(bf16[256,1536]{1,0:T(8,128)(2,1)S(1)} %multiply_reduce_fusion.6), channel_id=1, source_target_pairs={{0,1},{1,0},{2,3},{3,2},{4,5},{5,4},{6,7},{7,6},{8,9},{9,8},{10,11... | collective-permute-start | bytes 2359304 | tf_op jit(solution)/shard_map/ppermute | solution.py:149
  165.1 18.3 %collective-permute-start.14 = (bf16[256,1536]{1,0:T(8,128)(2,1)S(1)}, bf16[256,1536]{1,0:T(8,128)(2,1)S(1)}, u32[]{:S(2)}, u32[]{:S(2)}) collective-permute-start(bf16[256,1536]{1,0:T(8,128)(2,1)S(1)} %collective-permute-done.13), channel_id=1, source_target_pairs={{0,1},{1,0},{2,3},{3,2},{4,5},{5,4},{6,7},{7,6},{8,9},{9,8},{10,11... | collective-permute-start | bytes 2359304 | tf_op jit(solution)/shard_map/ppermute | solution.py:149
  176.9 9.4 %collective-permute-start.10 = (bf16[256,1536]{1,0:T(8,128)(2,1)S(1)}, bf16[256,1536]{1,0:T(8,128)(2,1)S(1)}, u32[]{:S(2)}, u32[]{:S(2)}) collective-permute-start(bf16[256,1536]{1,0:T(8,128)(2,1)S(1)} %collective-permute-done.9), channel_id=1, source_target_pairs={{0,1},{1,0},{2,3},{3,2},{4,5},{5,4},{6,7},{7,6},{8,9},{9,8},{10,11... | collective-permute-start | bytes 2359304 | tf_op jit(solution)/shard_map/ppermute | solution.py:149
  180.6 9.4 %collective-permute-start.6 = (bf16[256,1536]{1,0:T(8,128)(2,1)S(1)}, bf16[256,1536]{1,0:T(8,128)(2,1)S(1)}, u32[]{:S(2)}, u32[]{:S(2)}) collective-permute-start(bf16[256,1536]{1,0:T(8,128)(2,1)S(1)} %collective-permute-done.5), channel_id=1, source_target_pairs={{0,1},{1,0},{2,3},{3,2},{4,5},{5,4},{6,7},{7,6},{8,9},{9,8},{10,11... | collective-permute-start | bytes 2359304 | tf_op jit(solution)/shard_map/ppermute | solution.py:149
  186.2 6.8 %collective-permute-start.15 = (bf16[256,1536]{1,0:T(8,128)(2,1)S(1)}, bf16[256,1536]{1,0:T(8,128)(2,1)S(1)}, u32[]{:S(2)}, u32[]{:S(2)}) collective-permute-start(bf16[256,1536]{1,0:T(8,128)(2,1)S(1)} %multiply_reduce_fusion), channel_id=1, source_target_pairs={{0,1},{1,0},{2,3},{3,2},{4,5},{5,4},{6,7},{7,6},{8,9},{9,8},{10,11... | collective-permute-start | bytes 2359304 | tf_op jit(solution)/shard_map/ppermute | solution.py:149
  189.4 4.4 %collective-permute-start.11 = (bf16[256,1536]{1,0:T(8,128)(2,1)S(1)}, bf16[256,1536]{1,0:T(8,128)(2,1)S(1)}, u32[]{:S(2)}, u32[]{:S(2)}) collective-permute-start(bf16[256,1536]{1,0:T(8,128)(2,1)S(1)} %multiply_reduce_fusion.2), channel_id=1, source_target_pairs={{0,1},{1,0},{2,3},{3,2},{4,5},{5,4},{6,7},{7,6},{8,9},{9,8},{10,11... | collective-permute-start | bytes 2359304 | tf_op jit(solution)/shard_map/ppermute | solution.py:149
  192.9 2.4 %collective-permute-start.7 = (bf16[256,1536]{1,0:T(8,128)(2,1)S(1)}, bf16[256,1536]{1,0:T(8,128)(2,1)S(1)}, u32[]{:S(2)}, u32[]{:S(2)}) collective-permute-start(bf16[256,1536]{1,0:T(8,128)(2,1)S(1)} %multiply_reduce_fusion.4), channel_id=1, source_target_pairs={{0,1},{1,0},{2,3},{3,2},{4,5},{5,4},{6,7},{7,6},{8,9},{9,8},{10,11... | collective-permute-start | bytes 2359304 | tf_op jit(solution)/shard_map/ppermute | solution.py:149
  193.2 21.3 %collective-permute-start.16 = (bf16[256,1536]{1,0:T(8,128)(2,1)S(1)}, bf16[256,1536]{1,0:T(8,128)(2,1)S(1)}, u32[]{:S(2)}, u32[]{:S(2)}) collective-permute-start(bf16[256,1536]{1,0:T(8,128)(2,1)S(1)} %add_convert_fusion.1), channel_id=1, source_target_pairs={{0,2},{1,3},{2,4},{3,5},{4,6},{5,7},{6,0},{7,1},{8,10},{9,11},{10,... | collective-permute-start | bytes 2359304 | tf_op jit(solution)/shard_map/ppermute | solution.py:146
  194.1 36.6 %collective-permute-start.12 = (bf16[256,1536]{1,0:T(8,128)(2,1)S(1)}, bf16[256,1536]{1,0:T(8,128)(2,1)S(1)}, u32[]{:S(2)}, u32[]{:S(2)}) collective-permute-start(bf16[256,1536]{1,0:T(8,128)(2,1)S(1)} %add_convert_fusion.2), channel_id=1, source_target_pairs={{0,4},{1,5},{2,6},{3,7},{4,0},{5,1},{6,2},{7,3},{8,12},{9,13},{10,... | collective-permute-start | bytes 2359304 | tf_op jit(solution)/shard_map/ppermute | solution.py:146
  195.4 35.6 %collective-permute-start.8 = (bf16[256,1536]{1,0:T(8,128)(2,1)S(1)}, bf16[256,1536]{1,0:T(8,128)(2,1)S(1)}, u32[]{:S(2)}, u32[]{:S(2)}) collective-permute-start(bf16[256,1536]{1,0:T(8,128)(2,1)S(1)} %add_convert_fusion.3), channel_id=1, source_target_pairs={{0,6},{1,7},{2,0},{3,1},{4,2},{5,3},{6,4},{7,5},{8,14},{9,15},{10,... | collective-permute-start | bytes 2359304 | tf_op jit(solution)/shard_map/ppermute | solution.py:146
  201.3 29.8 %copy-start.2 = (f32[256,1536]{1,0:T(8,128)S(1)}, f32[256,1536]{1,0:T(8,128)}, u32[]{:S(2)}) copy-start(f32[256,1536]{1,0:T(8,128)} %copy-done.1) | copy-start | bytes 4718596

commit v10 on v6

--- a/solution.py
+++ b/solution.py
@@ -32,9 +32,10 @@
     return reach > 0.5
 
 
-def attention_kernel(groups_ref, pages_ref, lengths_ref, queries_ref, tree_ref, visible_ref, prompt_ref, *rest):
-    page_refs = rest[:MAXP]
-    out_ref = rest[MAXP]
+def attention_kernel(groups_ref, pages_ref, lengths_ref, queries_ref, tree_ref, visible_ref, *rest):
+    prompt_refs = rest[: len(rest) - MAXP - 1]
+    page_refs = rest[len(prompt_refs) : len(prompt_refs) + MAXP]
+    out_ref = rest[-1]
     request = pl.program_id(0)
     key_value_width = KEY_VALUE_HEADS * HEAD_WIDTH
     heads_repeated = QUERY_HEADS // KEY_VALUE_HEADS
@@ -55,8 +56,8 @@
             ],
             0,
         )
-        prompt_keys = prompt_ref[0, :, key_at : key_at + HEAD_WIDTH]
-        prompt_values = prompt_ref[0, :, value_at : value_at + HEAD_WIDTH]
+        prompt_keys = jnp.concatenate([p[0, :, key_at : key_at + HEAD_WIDTH] for p in prompt_refs], 0)
+        prompt_values = jnp.concatenate([p[0, :, value_at : value_at + HEAD_WIDTH] for p in prompt_refs], 0)
         cache_keys = jnp.concatenate([p[0, :, key_at : key_at + HEAD_WIDTH] for p in page_refs], 0)
         cache_values = jnp.concatenate([p[0, :, value_at : value_at + HEAD_WIDTH] for p in page_refs], 0)
         tree_keys = tree_ref[:, key_at : key_at + HEAD_WIDTH]
@@ -89,14 +90,14 @@
             out_ref[:, head * HEAD_WIDTH : (head + 1) * HEAD_WIDTH] = result[j * TREE_TOKENS : (j + 1) * TREE_TOKENS]
 
 
-def attend(queries, draft_kv, piece, cache_page_store, page_table, cache_len, parents, groups):
+def attend(queries, draft_kv, pieces, cache_page_store, page_table, cache_len, parents, groups):
     count_of_tokens, width = queries.shape
     count_of_requests = page_table.shape[0]
     row_width = draft_kv.shape[1]
     store_pages = cache_page_store.shape[0]
     visible = ancestry(parents).astype(jnp.float32)
     flat_pages = jnp.clip(page_table.reshape(-1), 0, store_pages - 1).astype(jnp.int32)
-    prompt_groups = jnp.clip(groups, 0, piece.shape[0] - 1).astype(jnp.int32)
+    prompt_groups = jnp.clip(groups, 0, pieces[0].shape[0] - 1).astype(jnp.int32)
 
     def page_spec(slot):
         return pl.BlockSpec(
@@ -110,8 +111,8 @@
             pl.BlockSpec((TREE_TOKENS, width), lambda r, g, p, c: (r, 0)),
             pl.BlockSpec((TREE_TOKENS, row_width), lambda r, g, p, c: (r, 0)),
             pl.BlockSpec((1, TREE_TOKENS, TREE_TOKENS), lambda r, g, p, c: (r, 0, 0)),
-            pl.BlockSpec((1, piece.shape[1], row_width), lambda r, g, p, c: (g[r], 0, 0)),
         ]
+        + [pl.BlockSpec((1, part.shape[1], row_width), lambda r, g, p, c: (g[r], 0, 0)) for part in pieces]
         + [page_spec(slot) for slot in range(MAXP)],
         out_specs=pl.BlockSpec((TREE_TOKENS, width), lambda r, g, p, c: (r, 0)),
     )
@@ -119,7 +120,7 @@
         attention_kernel,
         grid_spec=grid_spec,
         out_shape=jax.ShapeDtypeStruct((count_of_tokens, width), jnp.bfloat16),
-    )(prompt_groups, flat_pages, cache_len.astype(jnp.int32), queries, draft_kv, visible, piece, *([cache_page_store] * MAXP))
+    )(prompt_groups, flat_pages, cache_len.astype(jnp.int32), queries, draft_kv, visible, *pieces, *([cache_page_store] * MAXP))
 
 
 def run_experts(rows, row_gate, w_in, w_down):
@@ -197,9 +198,13 @@
     )
     gate_gathered = lax.all_gather(gate_local, "exp", axis=0, tiled=True)
     gate = lax.dynamic_slice_in_dim(gate_gathered, lax.axis_index("exp") * local_experts, local_experts, 1)
-    piece = lax.all_gather(prompt_key_value, "req", axis=1, tiled=True)
-    gate, piece = lax.optimization_barrier((gate, piece))
-    attended = attend(queries, draft_kv, piece, cache_page_store, page_table, cache_len, parents, groups)
+    columns = lax.axis_size("req")
+    pieces = [prompt_key_value] + [
+        lax.ppermute(prompt_key_value, "req", [(s, (s + d) % columns) for s in range(columns)])
+        for d in range(1, columns)
+    ]
+    gate, pieces = lax.optimization_barrier((gate, pieces))
+    attended = attend(queries, draft_kv, pieces, cache_page_store, page_table, cache_len, parents, groups)
     mixed = resid.astype(jnp.float32) + jnp.dot(attended, w_out, preferred_element_type=jnp.float32)
     spread = jnp.mean(mixed * mixed, -1, keepdims=True)
     normed = (mixed * lax.rsqrt(spread + 1e-05) * norm_gain).astype(jnp.bfloat16)

time: 236 us -> 231 us (0.979); the launches traced: 232 us -> 230 us
  between operations: 13.8 us -> 0.39 us
  starting transfers between devices: 7.21 us -> 13.4 us
  waiting for transfers between devices: 121 us -> 126 us
    ppermute x0 -> x3, waiting for transfers between devices: none -> 73.6 us  [per_device(): lax.ppermute(prompt_key_value, 'req', [(s, (s + d) % columns) for s in ra...]
    all_gather x1 -> x0, waiting for transfers between devices: 65.6 us -> none  [per_device(): piece = lax.all_gather(prompt_key_value, 'req', axis=1, tiled=True)]
    ppermute x0 -> x3, starting transfers between devices: none -> 4.61 us  [per_device(): lax.ppermute(prompt_key_value, 'req', [(s, (s + d) % columns) for s in ra...]
  transfers between devices with their start and end apart: 15 -> 17, of which waited for: 5 -> 9; matrix products, arithmetic and copies ran while one was open for 16% -> 16% of each run, Pallas kernels for 0% -> 0%
where the time goes in v10:
time: 231 us; the launch traced here: 230 us
  waiting for transfers between devices  126 us (55%)
  matrix products  37.4 us (16%)
  Pallas kernels  36.1 us (16%)
  starting transfers between devices  13.4 us (6%)
  blocking collectives  9.22 us (4%)
  other arithmetic  5.78 us (3%)
    ppermute x3, waiting for transfers between devices, per_device(): lax.ppermute(prompt_key_value, 'req', [(s, (s + d) % columns) for s in ra...  73.6 us
    ppermute x6, waiting for transfers between devices, chip_shift(): return lax.ppermute(x, 'exp', pairs)  51.9 us
    pallas_call x1, Pallas kernels, attend(): pl.pallas_call(attention_kernel, grid_spec=grid_spec, out_shape=jax.Shape...  36.1 us
    dot_general x8, matrix products, run_experts(): jnp.einsum('td,edf->etf', rows, w_in, preferred_element_type=jnp.float32)  21.7 us
    all_gather x1, blocking collectives, per_device(): gate_gathered = lax.all_gather(gate_local, 'exp', axis=0, tiled=True)  9.22 us
    dot_general x8, matrix products, run_experts(): jnp.einsum('etf,efd->etd', act, w_down, preferred_element_type=jnp.float32)  8.65 us
    ppermute x6, starting transfers between devices, chip_shift(): return lax.ppermute(x, 'exp', pairs)  7.38 us
  transfers between devices with their start and end apart: 17, of which 9 were waited for; matrix products, arithmetic and copies ran while one was open for 16% of the time, Pallas kernels for 0%

profile of v10, /device:TPU:12, one launch (start us, length us, event | category | flops | bytes accessed | tf_op | source)
XLA Modules:
  0.0 229.8 jit_solution(14415307432107655249)
XLA Ops:
  0.0 1.6 collective-permute-start
  1.6 1.2 collective-permute-start.1
  2.8 1.8 collective-permute-start.2
  4.6 0.7 broadcast_clamp_fusion
  5.3 0.6 min.37.pages_ref
  5.9 0.7 select_reduce_fusion
  6.7 9.2 %all_gather.3 = f32[2048,16]{0,1:T(8,128)S(1)} all-gather(f32[256,16]{0,1:T(8,128)S(1)} %select_reduce_fusion), channel_id=1, replica_groups=mesh['req'=4,'exp'=8] {'exp'}, dimensions={0}, use_global_device_ids=true | all-gather | bytes 147456 | tf_op jit(solution)/shard_map/all_gather | solution.py:199
  15.9 1.1 convolution_minimum_fusion.4
  17.0 1.2 broadcast_clamp_fusion.1.groups_ref
  18.2 0.3 convolution_minimum_fusion.3
  18.5 0.3 convolution_minimum_fusion.2
  18.7 0.3 convolution_minimum_fusion.1
  19.0 0.9 fusion.1.visible_ref
  19.9 50.5 %collective-permute-done.rest_1_ = bf16[2,256,1024]{2,1,0:T(8,128)(2,1)} collective-permute-done((bf16[2,256,1024]{2,1,0:T(8,128)(2,1)}, bf16[2,256,1024]{2,1,0:T(8,128)(2,1)}, u32[]{:S(2)}, u32[]{:S(2)}) %collective-permute-start) | collective-permute-done | bytes 1048608 | tf_op jit(solution)/shard_map/ppermute | solution.py:203
  70.4 21.3 %collective-permute-done.1.rest_2_ = bf16[2,256,1024]{2,1,0:T(8,128)(2,1)} collective-permute-done((bf16[2,256,1024]{2,1,0:T(8,128)(2,1)}, bf16[2,256,1024]{2,1,0:T(8,128)(2,1)}, u32[]{:S(2)}, u32[]{:S(2)}) %collective-permute-start.1) | collective-permute-done | bytes 1048608 | tf_op jit(solution)/shard_map/ppermute | solution.py:203
  91.7 1.8 collective-permute-done.2.rest_3_
  93.5 36.1 %shard_map.145 = bf16[256,1536]{1,0:T(8,128)(2,1)} custom-call(s32[8]{0:T(128)} %broadcast_clamp_fusion.1.groups_ref, s32[48]{0:T(128)} %min.37.pages_ref, s32[8]{0:T(128)} %lengths_ref.1, bf16[256,1536]{1,0:T(8,128)(2,1)} %queries_ref.1, bf16[256,1024]{1,0:T(8,128)(2,1)} %tree_ref.1, f32[8,32,32]{2,1,0:T(8,128)} %fusion.1.visible_ref, ...), custom_call_target="tpu_custom_call" | custom-call | tf_op jit(solution)/shard_map/pallas_call | solution.py:119
  129.6 4.3 %multiply_reduce_fusion.8 = (f32[256]{0:T(256)S(1)}, f32[256,1536]{1,0:T(8,128)S(1)}) fusion(bf16[256,1536]{1,0:T(8,128)(2,1)} %shard_map.145, bf16[1536,1536]{1,0:T(8,128)(2,1)} %param.24, bf16[256,1536]{1,0:T(8,128)(2,1)} %param.15), kind=kOutput, calls=%fused_computation.30 | convolution fusion | flops 1209532160 | bytes 7865344 | tf_op jit(solution)/shard_map/dot_general | solution.py:208
  133.9 1.1 copy-done.1
  135.0 1.1 multiply_convert_fusion
  136.1 0.0 collective-permute-start.3
  136.1 1.4 collective-permute-start.13
  137.5 1.5 collective-permute-start.9
  139.1 0.0 collective-permute-start.5
  139.2 0.0 collective-permute-done.3
  139.2 4.8 %convolution_bitcast_fusion.6 = f32[2,256,1024]{2,1,0:T(8,128)S(1)} fusion(bf16[2,1536,1024]{2,1,0:T(8,128)(2,1)} %param.28, bf16[256,1536]{1,0:T(8,128)(2,1)} %collective-permute-done.3), kind=kOutput, calls=%fused_computation.23 | convolution fusion | flops 1610612736 | bytes 9175040 | tf_op jit(solution)/shard_map/td,edf->etf/dot_general | solution.py:127
  144.0 0.0 slice-start
  144.1 1.1 multiply_reduce_fusion.6
  145.2 0.0 slice-start.1
  145.2 0.1 collective-permute-start.4
  145.2 11.4 %collective-permute-done.13 = bf16[256,1536]{1,0:T(8,128)(2,1)S(1)} collective-permute-done((bf16[256,1536]{1,0:T(8,128)(2,1)}, bf16[256,1536]{1,0:T(8,128)(2,1)S(1)}, u32[]{:S(2)}, u32[]{:S(2)}) %collective-permute-start.13) | collective-permute-done | bytes 786464 | tf_op jit(solution)/shard_map/ppermute | solution.py:147
  156.7 4.7 %convolution_bitcast_fusion.1 = f32[2,256,1024]{2,1,0:T(8,128)S(1)} fusion(bf16[2,1536,1024]{2,1,0:T(8,128)(2,1)} %param.28, bf16[256,1536]{1,0:T(8,128)(2,1)S(1)} %collective-permute-done.13), kind=kOutput, calls=%fused_computation.18 | convolution fusion | flops 1610612736 | bytes 9175040 | tf_op jit(solution)/shard_map/td,edf->etf/dot_general | solution.py:127
  161.4 1.0 multiply_reduce_fusion.1
  162.4 0.1 collective-permute-start.14
  162.5 11.8 %collective-permute-done.9 = bf16[256,1536]{1,0:T(8,128)(2,1)S(1)} collective-permute-done((bf16[256,1536]{1,0:T(8,128)(2,1)}, bf16[256,1536]{1,0:T(8,128)(2,1)S(1)}, u32[]{:S(2)}, u32[]{:S(2)}) %collective-permute-start.9) | collective-permute-done | bytes 786464 | tf_op jit(solution)/shard_map/ppermute | solution.py:147
  174.3 0.0 collective-permute-start.10
  174.3 1.8 convolution_bitcast_fusion.3
  176.1 1.8 convolution_bitcast_fusion.5
  177.9 0.6 collective-permute-start.6
  178.5 1.1 multiply_reduce_fusion.3
  179.6 1.1 multiply_reduce_fusion.5
  180.7 1.8 convolution_bitcast_fusion
  182.4 1.1 multiply_reduce_fusion
  183.6 0.1 collective-permute-start.15
  183.6 0.0 collective-permute-done.10
  183.6 2.0 convolution_bitcast_fusion.2
  185.7 1.1 multiply_reduce_fusion.2
  186.8 0.6 collective-permute-start.11
  187.3 1.8 convolution_bitcast_fusion.4
  189.1 1.1 multiply_reduce_fusion.4
  190.2 0.1 collective-permute-start.7
  190.3 0.2 add_convert_fusion.1
  190.5 0.6 collective-permute-start.16
  191.2 0.2 add_convert_fusion.2
  191.4 1.0 collective-permute-start.12
  192.4 0.2 collective-permute-done.7
  192.6 0.2 add_convert_fusion.3
  192.8 2.8 %collective-permute-start.8 = (bf16[256,1536]{1,0:T(8,128)(2,1)S(1)}, bf16[256,1536]{1,0:T(8,128)(2,1)S(1)}, u32[]{:S(2)}, u32[]{:S(2)}) collective-permute-start(bf16[256,1536]{1,0:T(8,128)(2,1)S(1)} %add_convert_fusion.3), channel_id=1, source_target_pairs={{0,6},{1,7},{2,0},{3,1},{4,2},{5,3},{6,4},{7,5},{8,14},{9,15},{10,... | collective-permute-start | bytes 2359304 | tf_op jit(solution)/shard_map/ppermute | solution.py:147
  195.6 3.0 %convolution_bitcast_fusion.7 = f32[2,256,1024]{2,1,0:T(8,128)S(1)} fusion(bf16[2,1536,1024]{2,1,0:T(8,128)(2,1)S(1)} %bitcast.113, bf16[256,1536]{1,0:T(8,128)(2,1)} %multiply_convert_fusion), kind=kOutput, calls=%fused_computation.24 | convolution fusion | flops 1610612736 | bytes 9175040 | tf_op jit(solution)/shard_map/td,edf->etf/dot_general | solution.py:127
  198.6 1.1 multiply_reduce_fusion.7
  199.7 12.2 %collective-permute-done.16 = bf16[256,1536]{1,0:T(8,128)(2,1)S(1)} collective-permute-done((bf16[256,1536]{1,0:T(8,128)(2,1)S(1)}, bf16[256,1536]{1,0:T(8,128)(2,1)S(1)}, u32[]{:S(2)}, u32[]{:S(2)}) %collective-permute-start.16) | collective-permute-done | bytes 786464 | tf_op jit(solution)/shard_map/ppermute | solution.py:147
  211.9 16.1 %collective-permute-done.12 = bf16[256,1536]{1,0:T(8,128)(2,1)S(1)} collective-permute-done((bf16[256,1536]{1,0:T(8,128)(2,1)S(1)}, bf16[256,1536]{1,0:T(8,128)(2,1)S(1)}, u32[]{:S(2)}, u32[]{:S(2)}) %collective-permute-start.12) | collective-permute-done | bytes 786464 | tf_op jit(solution)/shard_map/ppermute | solution.py:147
  228.0 0.4 collective-permute-done.8
  228.4 1.5 add_convert_fusion
  (29 shorter events, 0.1 us)
Async XLA Ops:
  0.0 144.0 %copy-start = (bf16[2,512,1536]{2,1,0:T(8,128)(2,1)S(1)}, bf16[2,512,1536]{2,1,0:T(8,128)(2,1)}, u32[]{:S(2)}) copy-start(bf16[2,512,1536]{2,1,0:T(8,128)(2,1)} %param.29) | copy-start | bytes 9437188
  0.0 70.4 %collective-permute-start = (bf16[2,256,1024]{2,1,0:T(8,128)(2,1)}, bf16[2,256,1024]{2,1,0:T(8,128)(2,1)}, u32[]{:S(2)}, u32[]{:S(2)}) collective-permute-start(bf16[2,256,1024]{2,1,0:T(8,128)(2,1)} %rest_0_), channel_id=1, source_target_pairs={{0,8},{8,16},{16,24},{24,0},{1,9},{9,17},{17,25},{25,1},{2,10},{10... | collective-permute-start | bytes 3145736 | tf_op jit(solution)/shard_map/ppermute | solution.py:203
  1.6 90.1 %collective-permute-start.1 = (bf16[2,256,1024]{2,1,0:T(8,128)(2,1)}, bf16[2,256,1024]{2,1,0:T(8,128)(2,1)}, u32[]{:S(2)}, u32[]{:S(2)}) collective-permute-start(bf16[2,256,1024]{2,1,0:T(8,128)(2,1)} %rest_0_), channel_id=1, source_target_pairs={{0,16},{8,24},{16,0},{24,8},{1,17},{9,25},{17,1},{25,9},{2,18},{10... | collective-permute-start | bytes 3145736 | tf_op jit(solution)/shard_map/ppermute | solution.py:203
  2.8 90.7 %collective-permute-start.2 = (bf16[2,256,1024]{2,1,0:T(8,128)(2,1)}, bf16[2,256,1024]{2,1,0:T(8,128)(2,1)}, u32[]{:S(2)}, u32[]{:S(2)}) collective-permute-start(bf16[2,256,1024]{2,1,0:T(8,128)(2,1)} %rest_0_), channel_id=1, source_target_pairs={{0,24},{8,0},{16,8},{24,16},{1,25},{9,1},{17,9},{25,17},{2,26},{10... | collective-permute-start | bytes 3145736 | tf_op jit(solution)/shard_map/ppermute | solution.py:203
  129.6 5.4 %copy-start.3 = (f32[1536]{0:T(1024)S(1)}, f32[1536]{0:T(1024)}, u32[]{:S(2)}) copy-start(f32[1536]{0:T(1024)} %param.25) | copy-start | bytes 18436
  133.9 1.2 copy-start.1
  136.1 3.1 %collective-permute-start.3 = (bf16[256,1536]{1,0:T(8,128)(2,1)}, bf16[256,1536]{1,0:T(8,128)(2,1)}, u32[]{:S(2)}, u32[]{:S(2)}) collective-permute-start(bf16[256,1536]{1,0:T(8,128)(2,1)} %multiply_convert_fusion), channel_id=1, source_target_pairs={{0,1},{1,0},{2,3},{3,2},{4,5},{5,4},{6,7},{7,6},{8,9},{9,8},{10,11... | collective-permute-start | bytes 2359304 | tf_op jit(solution)/shard_map/ppermute | solution.py:150
  136.1 20.5 %collective-permute-start.13 = (bf16[256,1536]{1,0:T(8,128)(2,1)}, bf16[256,1536]{1,0:T(8,128)(2,1)S(1)}, u32[]{:S(2)}, u32[]{:S(2)}) collective-permute-start(bf16[256,1536]{1,0:T(8,128)(2,1)} %multiply_convert_fusion), channel_id=1, source_target_pairs={{0,6},{1,7},{2,0},{3,1},{4,2},{5,3},{6,4},{7,5},{8,14},{9,15},{10,... | collective-permute-start | bytes 2359304 | tf_op jit(solution)/shard_map/ppermute | solution.py:147
  137.5 36.7 %collective-permute-start.9 = (bf16[256,1536]{1,0:T(8,128)(2,1)}, bf16[256,1536]{1,0:T(8,128)(2,1)S(1)}, u32[]{:S(2)}, u32[]{:S(2)}) collective-permute-start(bf16[256,1536]{1,0:T(8,128)(2,1)} %multiply_convert_fusion), channel_id=1, source_target_pairs={{0,4},{1,5},{2,6},{3,7},{4,0},{5,1},{6,2},{7,3},{8,12},{9,13},{10,... | collective-permute-start | bytes 2359304 | tf_op jit(solution)/shard_map/ppermute | solution.py:147
  139.1 37.0 %collective-permute-start.5 = (bf16[256,1536]{1,0:T(8,128)(2,1)}, bf16[256,1536]{1,0:T(8,128)(2,1)S(1)}, u32[]{:S(2)}, u32[]{:S(2)}) collective-permute-start(bf16[256,1536]{1,0:T(8,128)(2,1)} %multiply_convert_fusion), channel_id=1, source_target_pairs={{0,2},{1,3},{2,4},{3,5},{4,6},{5,7},{6,0},{7,1},{8,10},{9,11},{10,... | collective-permute-start | bytes 2359304 | tf_op jit(solution)/shard_map/ppermute | solution.py:147
  144.0 30.2 %slice-start = ((s8[6291456]{0:T(1024)(128)(4,1)}), s8[4194304]{0:T(1024)(128)(4,1)S(1)}, s32[]{:S(2)}) async-start(s8[6291456]{0:T(1024)(128)(4,1)} %bitcast.112), calls=%async_computation | async-start | bytes 8388608
  145.2 29.1 %slice-start.1 = ((s8[6291456]{0:T(1024)(128)(4,1)}), s8[2097152]{0:T(1024)(128)(4,1)S(1)}, s32[]{:S(2)}) async-start(s8[6291456]{0:T(1024)(128)(4,1)} %bitcast.112), calls=%async_computation.1 | async-start | bytes 4194304
  145.2 54.5 %collective-permute-start.4 = (bf16[256,1536]{1,0:T(8,128)(2,1)S(1)}, bf16[256,1536]{1,0:T(8,128)(2,1)S(1)}, u32[]{:S(2)}, u32[]{:S(2)}) collective-permute-start(bf16[256,1536]{1,0:T(8,128)(2,1)S(1)} %multiply_reduce_fusion.6), channel_id=1, source_target_pairs={{0,1},{1,0},{2,3},{3,2},{4,5},{5,4},{6,7},{7,6},{8,9},{9,8},{10,11... | collective-permute-start | bytes 2359304 | tf_op jit(solution)/shard_map/ppermute | solution.py:150
  162.4 18.3 %collective-permute-start.14 = (bf16[256,1536]{1,0:T(8,128)(2,1)S(1)}, bf16[256,1536]{1,0:T(8,128)(2,1)S(1)}, u32[]{:S(2)}, u32[]{:S(2)}) collective-permute-start(bf16[256,1536]{1,0:T(8,128)(2,1)S(1)} %collective-permute-done.13), channel_id=1, source_target_pairs={{0,1},{1,0},{2,3},{3,2},{4,5},{5,4},{6,7},{7,6},{8,9},{9,8},{10,11... | collective-permute-start | bytes 2359304 | tf_op jit(solution)/shard_map/ppermute | solution.py:150
  174.3 9.4 %collective-permute-start.10 = (bf16[256,1536]{1,0:T(8,128)(2,1)S(1)}, bf16[256,1536]{1,0:T(8,128)(2,1)S(1)}, u32[]{:S(2)}, u32[]{:S(2)}) collective-permute-start(bf16[256,1536]{1,0:T(8,128)(2,1)S(1)} %collective-permute-done.9), channel_id=1, source_target_pairs={{0,1},{1,0},{2,3},{3,2},{4,5},{5,4},{6,7},{7,6},{8,9},{9,8},{10,11... | collective-permute-start | bytes 2359304 | tf_op jit(solution)/shard_map/ppermute | solution.py:150
  177.9 9.4 %collective-permute-start.6 = (bf16[256,1536]{1,0:T(8,128)(2,1)S(1)}, bf16[256,1536]{1,0:T(8,128)(2,1)S(1)}, u32[]{:S(2)}, u32[]{:S(2)}) collective-permute-start(bf16[256,1536]{1,0:T(8,128)(2,1)S(1)} %collective-permute-done.5), channel_id=1, source_target_pairs={{0,1},{1,0},{2,3},{3,2},{4,5},{5,4},{6,7},{7,6},{8,9},{9,8},{10,11... | collective-permute-start | bytes 2359304 | tf_op jit(solution)/shard_map/ppermute | solution.py:150
  183.6 6.8 %collective-permute-start.15 = (bf16[256,1536]{1,0:T(8,128)(2,1)S(1)}, bf16[256,1536]{1,0:T(8,128)(2,1)S(1)}, u32[]{:S(2)}, u32[]{:S(2)}) collective-permute-start(bf16[256,1536]{1,0:T(8,128)(2,1)S(1)} %multiply_reduce_fusion), channel_id=1, source_target_pairs={{0,1},{1,0},{2,3},{3,2},{4,5},{5,4},{6,7},{7,6},{8,9},{9,8},{10,11... | collective-permute-start | bytes 2359304 | tf_op jit(solution)/shard_map/ppermute | solution.py:150
  186.8 4.4 %collective-permute-start.11 = (bf16[256,1536]{1,0:T(8,128)(2,1)S(1)}, bf16[256,1536]{1,0:T(8,128)(2,1)S(1)}, u32[]{:S(2)}, u32[]{:S(2)}) collective-permute-start(bf16[256,1536]{1,0:T(8,128)(2,1)S(1)} %multiply_reduce_fusion.2), channel_id=1, source_target_pairs={{0,1},{1,0},{2,3},{3,2},{4,5},{5,4},{6,7},{7,6},{8,9},{9,8},{10,11... | collective-permute-start | bytes 2359304 | tf_op jit(solution)/shard_map/ppermute | solution.py:150
  190.2 2.4 %collective-permute-start.7 = (bf16[256,1536]{1,0:T(8,128)(2,1)S(1)}, bf16[256,1536]{1,0:T(8,128)(2,1)S(1)}, u32[]{:S(2)}, u32[]{:S(2)}) collective-permute-start(bf16[256,1536]{1,0:T(8,128)(2,1)S(1)} %multiply_reduce_fusion.4), channel_id=1, source_target_pairs={{0,1},{1,0},{2,3},{3,2},{4,5},{5,4},{6,7},{7,6},{8,9},{9,8},{10,11... | collective-permute-start | bytes 2359304 | tf_op jit(solution)/shard_map/ppermute | solution.py:150
  190.5 21.3 %collective-permute-start.16 = (bf16[256,1536]{1,0:T(8,128)(2,1)S(1)}, bf16[256,1536]{1,0:T(8,128)(2,1)S(1)}, u32[]{:S(2)}, u32[]{:S(2)}) collective-permute-start(bf16[256,1536]{1,0:T(8,128)(2,1)S(1)} %add_convert_fusion.1), channel_id=1, source_target_pairs={{0,2},{1,3},{2,4},{3,5},{4,6},{5,7},{6,0},{7,1},{8,10},{9,11},{10,... | collective-permute-start | bytes 2359304 | tf_op jit(solution)/shard_map/ppermute | solution.py:147
  191.4 36.6 %collective-permute-start.12 = (bf16[256,1536]{1,0:T(8,128)(2,1)S(1)}, bf16[256,1536]{1,0:T(8,128)(2,1)S(1)}, u32[]{:S(2)}, u32[]{:S(2)}) collective-permute-start(bf16[256,1536]{1,0:T(8,128)(2,1)S(1)} %add_convert_fusion.2), channel_id=1, source_target_pairs={{0,4},{1,5},{2,6},{3,7},{4,0},{5,1},{6,2},{7,3},{8,12},{9,13},{10,... | collective-permute-start | bytes 2359304 | tf_op jit(solution)/shard_map/ppermute | solution.py:147
  192.8 35.6 %collective-permute-start.8 = (bf16[256,1536]{1,0:T(8,128)(2,1)S(1)}, bf16[256,1536]{1,0:T(8,128)(2,1)S(1)}, u32[]{:S(2)}, u32[]{:S(2)}) collective-permute-start(bf16[256,1536]{1,0:T(8,128)(2,1)S(1)} %add_convert_fusion.3), channel_id=1, source_target_pairs={{0,6},{1,7},{2,0},{3,1},{4,2},{5,3},{6,4},{7,5},{8,14},{9,15},{10,... | collective-permute-start | bytes 2359304 | tf_op jit(solution)/shard_map/ppermute | solution.py:147
  198.6 29.8 %copy-start.2 = (f32[256,1536]{1,0:T(8,128)S(1)}, f32[256,1536]{1,0:T(8,128)}, u32[]{:S(2)}) copy-start(f32[256,1536]{1,0:T(8,128)} %copy-done.1) | copy-start | bytes 4718596

commit v11 on v10

--- a/solution.py
+++ b/solution.py
@@ -159,8 +159,14 @@
     total = None
     for d in range(half):
         source_chip = (chip - d) % half
-        other_partial = run_experts(other_core[d], block_gate(2 * source_chip + 1 - core), w_in, w_down)
-        same_partial = run_experts(same_core[d], block_gate(2 * source_chip + core), w_in, w_down)
+        paired = run_experts(
+            jnp.concatenate([same_core[d], other_core[d]], 0),
+            jnp.concatenate([block_gate(2 * source_chip + core), block_gate(2 * source_chip + 1 - core)], 0),
+            w_in,
+            w_down,
+        )
+        same_partial = paired[:count_of_tokens]
+        other_partial = paired[count_of_tokens:]
         merged = same_partial + sibling(other_partial.astype(jnp.bfloat16)).astype(jnp.float32)
         if d == 0:
             total = merged if total is None else total + merged

time: 231 us -> 242 us (1.048)
  waiting for transfers between devices: 126 us -> 135 us
  matrix products: 37.4 us -> 42.7 us
    ppermute x6, waiting for transfers between devices: 51.9 us -> 61 us  [chip_shift(): return lax.ppermute(x, 'exp', pairs)]
    dot_general x8 -> x4, matrix products: 8.65 us -> 14.9 us  [run_experts(): jnp.einsum('etf,efd->etd', act, w_down, preferred_element_type=jnp.float32)]
    dot_general x8 -> x4, matrix products: 21.7 us -> 20.8 us  [run_experts(): jnp.einsum('td,edf->etf', rows, w_in, preferred_element_type=jnp.float32)]
  transfers between devices with their start and end apart: 17 -> 17, of which waited for: 9 -> 7; matrix products, arithmetic and copies ran while one was open for 16% -> 18% of each run, Pallas kernels for 0% -> 0%
where the time goes in v11:
time: 242 us
  waiting for transfers between devices  135 us (56%)
  matrix products  42.7 us (18%)
  Pallas kernels  36.1 us (15%)
  starting transfers between devices  12.7 us (5%)
  blocking collectives  9.22 us (4%)
  other arithmetic  4.92 us (2%)
    ppermute x3, waiting for transfers between devices, per_device(): lax.ppermute(prompt_key_value, 'req', [(s, (s + d) % columns) for s in ra...  73.6 us
    ppermute x6, waiting for transfers between devices, chip_shift(): return lax.ppermute(x, 'exp', pairs)  61 us
    pallas_call x1, Pallas kernels, attend(): pl.pallas_call(attention_kernel, grid_spec=grid_spec, out_shape=jax.Shape...  36.1 us
    dot_general x4, matrix products, run_experts(): jnp.einsum('td,edf->etf', rows, w_in, preferred_element_type=jnp.float32)  20.8 us
    dot_general x4, matrix products, run_experts(): jnp.einsum('etf,efd->etd', act, w_down, preferred_element_type=jnp.float32)  14.9 us
    all_gather x1, blocking collectives, per_device(): gate_gathered = lax.all_gather(gate_local, 'exp', axis=0, tiled=True)  9.22 us
    ppermute x6, starting transfers between devices, chip_shift(): return lax.ppermute(x, 'exp', pairs)  6.25 us
  transfers between devices with their start and end apart: 17, of which 7 were waited for; matrix products, arithmetic and copies ran while one was open for 18% of the time, Pallas kernels for 0%

profile of v11, /device:TPU:12, one launch (start us, length us, event | category | flops | bytes accessed | tf_op | source)
XLA Modules:
  0.0 241.5 jit_solution(17038073703924385983)
XLA Ops:
  0.0 1.6 collective-permute-start
  1.6 1.2 collective-permute-start.1
  2.8 1.8 collective-permute-start.2
  4.6 0.7 select_reduce_fusion
  5.4 9.2 %all_gather.3 = f32[2048,16]{0,1:T(8,128)S(1)} all-gather(f32[256,16]{0,1:T(8,128)S(1)} %select_reduce_fusion), channel_id=1, replica_groups=mesh['req'=4,'exp'=8] {'exp'}, dimensions={0}, use_global_device_ids=true | all-gather | bytes 147456 | tf_op jit(solution)/shard_map/all_gather | solution.py:205
  14.6 0.7 broadcast_clamp_fusion
  15.3 0.7 min.37.pages_ref
  16.0 1.1 convolution_minimum_fusion.4
  17.1 1.2 broadcast_clamp_fusion.1.groups_ref
  18.3 0.3 convolution_minimum_fusion.3
  18.5 0.3 convolution_minimum_fusion.2
  18.8 0.3 convolution_minimum_fusion.1
  19.0 0.9 fusion.21.visible_ref
  19.9 50.5 %collective-permute-done.rest_1_ = bf16[2,256,1024]{2,1,0:T(8,128)(2,1)} collective-permute-done((bf16[2,256,1024]{2,1,0:T(8,128)(2,1)}, bf16[2,256,1024]{2,1,0:T(8,128)(2,1)}, u32[]{:S(2)}, u32[]{:S(2)}) %collective-permute-start) | collective-permute-done | bytes 1048608 | tf_op jit(solution)/shard_map/ppermute | solution.py:209
  70.4 21.3 %collective-permute-done.1.rest_2_ = bf16[2,256,1024]{2,1,0:T(8,128)(2,1)} collective-permute-done((bf16[2,256,1024]{2,1,0:T(8,128)(2,1)}, bf16[2,256,1024]{2,1,0:T(8,128)(2,1)}, u32[]{:S(2)}, u32[]{:S(2)}) %collective-permute-start.1) | collective-permute-done | bytes 1048608 | tf_op jit(solution)/shard_map/ppermute | solution.py:209
  91.7 1.8 collective-permute-done.2.rest_3_
  93.5 36.1 %shard_map.145 = bf16[256,1536]{1,0:T(8,128)(2,1)} custom-call(s32[8]{0:T(128)} %broadcast_clamp_fusion.1.groups_ref, s32[48]{0:T(128)} %min.37.pages_ref, s32[8]{0:T(128)} %lengths_ref.1, bf16[256,1536]{1,0:T(8,128)(2,1)} %queries_ref.1, bf16[256,1024]{1,0:T(8,128)(2,1)} %tree_ref.1, f32[8,32,32]{2,1,0:T(8,128)} %fusion.21.visible_ref, ...), custom_call_target="tpu_custom_call" | custom-call | tf_op jit(solution)/shard_map/pallas_call | solution.py:119
  129.6 4.3 %multiply_reduce_fusion.4 = (f32[256]{0:T(256)S(1)}, f32[256,1536]{1,0:T(8,128)S(1)}) fusion(bf16[256,1536]{1,0:T(8,128)(2,1)} %shard_map.145, bf16[1536,1536]{1,0:T(8,128)(2,1)} %param.24, bf16[256,1536]{1,0:T(8,128)(2,1)} %param.15), kind=kOutput, calls=%fused_computation.50 | convolution fusion | flops 1209532160 | bytes 7865344 | tf_op jit(solution)/shard_map/dot_general | solution.py:214
  133.9 0.0 slice-start
  133.9 0.2 multiply_convert_fusion
  134.1 1.5 collective-permute-start.5
  135.6 0.5 collective-permute-start.9
  136.1 1.4 collective-permute-start.13
  137.6 0.0 collective-permute-start.3
  137.7 0.0 slice-start.1
  137.7 17.8 %collective-permute-done.5 = bf16[256,1536]{1,0:T(8,128)(2,1)S(1)} collective-permute-done((bf16[256,1536]{1,0:T(8,128)(2,1)S(1)}, bf16[256,1536]{1,0:T(8,128)(2,1)S(1)}, u32[]{:S(2)}, u32[]{:S(2)}) %collective-permute-start.5) | collective-permute-done | bytes 786464 | tf_op jit(solution)/shard_map/ppermute | solution.py:147
  155.5 0.0 collective-permute-start.6
  155.5 0.0 collective-permute-done.3
  155.5 5.5 %convolution_bitcast_fusion.3 = f32[2,512,1024]{2,1,0:T(8,128)S(1)} fusion(bf16[2,1536,1024]{2,1,0:T(8,128)(2,1)} %param.28, bf16[256,1536]{1,0:T(8,128)(2,1)S(1)} %collective-permute-done.3, bf16[256,1536]{1,0:T(8,128)(2,1)S(1)} %multiply_convert_fusion), kind=kOutput, calls=%fused_computation.12 | convolution fusion | flops 3224371200 | bytes 12058624 | tf_op jit(solution)/shard_map/td,edf->etf/dot_general | solution.py:127
  161.0 1.8 multiply_reduce_fusion.3
  162.9 0.1 slice.135
  163.0 0.6 collective-permute-start.4
  163.5 7.8 %collective-permute-done.9 = bf16[256,1536]{1,0:T(8,128)(2,1)S(1)} collective-permute-done((bf16[256,1536]{1,0:T(8,128)(2,1)S(1)}, bf16[256,1536]{1,0:T(8,128)(2,1)S(1)}, u32[]{:S(2)}, u32[]{:S(2)}) %collective-permute-start.9) | collective-permute-done | bytes 786464 | tf_op jit(solution)/shard_map/ppermute | solution.py:147
  171.4 0.0 collective-permute-start.10
  171.4 0.0 collective-permute-done.13
  171.4 0.5 collective-permute-start.14
  171.9 0.0 collective-permute-done.6
  171.9 5.1 %convolution_bitcast_fusion.2 = f32[2,512,1024]{2,1,0:T(8,128)} fusion(bf16[2,1536,1024]{2,1,0:T(8,128)(2,1)S(1)} %bitcast.71, bf16[256,1536]{1,0:T(8,128)(2,1)S(1)} %collective-permute-done.6, bf16[256,1536]{1,0:T(8,128)(2,1)S(1)} %collective-permute-done.5), kind=kOutput, calls=%fused_computation.11 | convolution fusion | flops 3224371200 | bytes 12058624 | tf_op jit(solution)/shard_map/td,edf->etf/dot_general | solution.py:127
  177.0 4.3 %multiply_reduce_fusion.2 = f32[512,1536]{1,0:T(8,128)S(1)} fusion(f32[2,512]{1,0:T(2,128)S(1)} %maximum_bitcast_fusion.9, bf16[2,512,1536]{2,1,0:T(8,128)(2,1)S(1)} %copy-done, f32[2,512,1024]{2,1,0:T(8,128)} %convolution_bitcast_fusion.2), kind=kOutput, calls=%fused_computation.2 | convolution fusion | flops 1619263488 | bytes 10489856 | tf_op jit(solution)/shard_map/etf,efd->etd/dot_general | solution.py:129
  181.3 0.1 slice.134
  181.4 0.1 collective-permute-start.7
  181.5 0.0 collective-permute-done.10
  181.5 5.1 %convolution_bitcast_fusion.1 = f32[2,512,1024]{2,1,0:T(8,128)} fusion(bf16[2,1536,1024]{2,1,0:T(8,128)(2,1)S(1)} %bitcast.71, bf16[256,1536]{1,0:T(8,128)(2,1)S(1)} %collective-permute-done.10, bf16[256,1536]{1,0:T(8,128)(2,1)S(1)} %collective-permute-done.9), kind=kOutput, calls=%fused_computation.10 | convolution fusion | flops 3224371200 | bytes 12058624 | tf_op jit(solution)/shard_map/td,edf->etf/dot_general | solution.py:127
  186.6 4.3 %multiply_reduce_fusion.1 = f32[512,1536]{1,0:T(8,128)S(1)} fusion(f32[2,512]{1,0:T(2,128)S(1)} %maximum_bitcast_fusion.10, bf16[2,512,1536]{2,1,0:T(8,128)(2,1)S(1)} %copy-done, f32[2,512,1024]{2,1,0:T(8,128)} %convolution_bitcast_fusion.1), kind=kOutput, calls=%fused_computation.1 | convolution fusion | flops 1619263488 | bytes 10489856 | tf_op jit(solution)/shard_map/etf,efd->etd/dot_general | solution.py:129
  190.9 0.1 slice.133
  191.0 0.5 collective-permute-start.11
  191.6 0.0 collective-permute-done.14
  191.6 5.1 %convolution_bitcast_fusion = f32[2,512,1024]{2,1,0:T(8,128)} fusion(bf16[2,1536,1024]{2,1,0:T(8,128)(2,1)S(1)} %bitcast.71, bf16[256,1536]{1,0:T(8,128)(2,1)S(1)} %collective-permute-done.14, bf16[256,1536]{1,0:T(8,128)(2,1)S(1)} %collective-permute-done.13), kind=kOutput, calls=%fused_computation.9 | convolution fusion | flops 3224371200 | bytes 12058624 | tf_op jit(solution)/shard_map/td,edf->etf/dot_general | solution.py:127
  196.6 4.4 %multiply_reduce_fusion = f32[512,1536]{1,0:T(8,128)S(1)} fusion(f32[2,512]{1,0:T(2,128)S(1)} %maximum_bitcast_fusion.11, bf16[2,512,1536]{2,1,0:T(8,128)(2,1)S(1)} %copy-done, f32[2,512,1024]{2,1,0:T(8,128)} %convolution_bitcast_fusion), kind=kOutput, calls=%fused_computation | convolution fusion | flops 1619263488 | bytes 10489856 | tf_op jit(solution)/shard_map/etf,efd->etd/dot_general | solution.py:129
  201.1 0.1 slice.132
  201.1 0.1 collective-permute-start.15
  201.3 0.2 fusion.6
  201.4 1.8 collective-permute-start.8
  203.2 0.0 collective-permute-done.11
  203.2 0.2 fusion.5
  203.4 0.6 collective-permute-start.12
  204.0 0.0 collective-permute-done.15
  204.0 0.2 fusion.4
  204.2 0.4 collective-permute-start.16
  204.6 0.0 collective-permute-done.4
  204.6 17.3 %collective-permute-done.8 = bf16[256,1536]{1,0:T(8,128)(2,1)S(1)} collective-permute-done((bf16[256,1536]{1,0:T(8,128)(2,1)S(1)}, bf16[256,1536]{1,0:T(8,128)(2,1)S(1)}, u32[]{:S(2)}, u32[]{:S(2)}) %collective-permute-start.8) | collective-permute-done | bytes 786464 | tf_op jit(solution)/shard_map/ppermute | solution.py:147
  221.8 18.1 %collective-permute-done.12 = bf16[256,1536]{1,0:T(8,128)(2,1)S(1)} collective-permute-done((bf16[256,1536]{1,0:T(8,128)(2,1)S(1)}, bf16[256,1536]{1,0:T(8,128)(2,1)S(1)}, u32[]{:S(2)}, u32[]{:S(2)}) %collective-permute-start.12) | collective-permute-done | bytes 786464 | tf_op jit(solution)/shard_map/ppermute | solution.py:147
  240.0 0.0 collective-permute-done.16
  240.0 1.5 fusion.11
  (21 shorter events, 0.1 us)
Async XLA Ops:
  0.0 161.0 %copy-start = (bf16[2,512,1536]{2,1,0:T(8,128)(2,1)S(1)}, bf16[2,512,1536]{2,1,0:T(8,128)(2,1)}, u32[]{:S(2)}) copy-start(bf16[2,512,1536]{2,1,0:T(8,128)(2,1)} %param.29) | copy-start | bytes 9437188
  0.0 70.4 %collective-permute-start = (bf16[2,256,1024]{2,1,0:T(8,128)(2,1)}, bf16[2,256,1024]{2,1,0:T(8,128)(2,1)}, u32[]{:S(2)}, u32[]{:S(2)}) collective-permute-start(bf16[2,256,1024]{2,1,0:T(8,128)(2,1)} %rest_0_), channel_id=1, source_target_pairs={{0,8},{8,16},{16,24},{24,0},{1,9},{9,17},{17,25},{25,1},{2,10},{10... | collective-permute-start | bytes 3145736 | tf_op jit(solution)/shard_map/ppermute | solution.py:209
  1.6 90.1 %collective-permute-start.1 = (bf16[2,256,1024]{2,1,0:T(8,128)(2,1)}, bf16[2,256,1024]{2,1,0:T(8,128)(2,1)}, u32[]{:S(2)}, u32[]{:S(2)}) collective-permute-start(bf16[2,256,1024]{2,1,0:T(8,128)(2,1)} %rest_0_), channel_id=1, source_target_pairs={{0,16},{8,24},{16,0},{24,8},{1,17},{9,25},{17,1},{25,9},{2,18},{10... | collective-permute-start | bytes 3145736 | tf_op jit(solution)/shard_map/ppermute | solution.py:209
  2.8 90.7 %collective-permute-start.2 = (bf16[2,256,1024]{2,1,0:T(8,128)(2,1)}, bf16[2,256,1024]{2,1,0:T(8,128)(2,1)}, u32[]{:S(2)}, u32[]{:S(2)}) collective-permute-start(bf16[2,256,1024]{2,1,0:T(8,128)(2,1)} %rest_0_), channel_id=1, source_target_pairs={{0,24},{8,0},{16,8},{24,16},{1,25},{9,1},{17,9},{25,17},{2,26},{10... | collective-permute-start | bytes 3145736 | tf_op jit(solution)/shard_map/ppermute | solution.py:209
  129.6 4.3 %copy-start.1 = (f32[1536]{0:T(1024)S(1)}, f32[1536]{0:T(1024)}, u32[]{:S(2)}) copy-start(f32[1536]{0:T(1024)} %param.25) | copy-start | bytes 18436
  133.9 38.0 %slice-start = ((s8[6291456]{0:T(1024)(128)(4,1)}), s8[4194304]{0:T(1024)(128)(4,1)S(1)}, s32[]{:S(2)}) async-start(s8[6291456]{0:T(1024)(128)(4,1)} %bitcast.70), calls=%async_computation | async-start | bytes 8388608
  134.1 21.4 %collective-permute-start.5 = (bf16[256,1536]{1,0:T(8,128)(2,1)S(1)}, bf16[256,1536]{1,0:T(8,128)(2,1)S(1)}, u32[]{:S(2)}, u32[]{:S(2)}) collective-permute-start(bf16[256,1536]{1,0:T(8,128)(2,1)S(1)} %multiply_convert_fusion), channel_id=1, source_target_pairs={{0,2},{1,3},{2,4},{3,5},{4,6},{5,7},{6,0},{7,1},{8,10},{9,11},{10,... | collective-permute-start | bytes 2359304 | tf_op jit(solution)/shard_map/ppermute | solution.py:147
  135.6 35.7 %collective-permute-start.9 = (bf16[256,1536]{1,0:T(8,128)(2,1)S(1)}, bf16[256,1536]{1,0:T(8,128)(2,1)S(1)}, u32[]{:S(2)}, u32[]{:S(2)}) collective-permute-start(bf16[256,1536]{1,0:T(8,128)(2,1)S(1)} %multiply_convert_fusion), channel_id=1, source_target_pairs={{0,4},{1,5},{2,6},{3,7},{4,0},{5,1},{6,2},{7,3},{8,12},{9,13},{10,... | collective-permute-start | bytes 2359304 | tf_op jit(solution)/shard_map/ppermute | solution.py:147
  136.1 35.2 %collective-permute-start.13 = (bf16[256,1536]{1,0:T(8,128)(2,1)S(1)}, bf16[256,1536]{1,0:T(8,128)(2,1)S(1)}, u32[]{:S(2)}, u32[]{:S(2)}) collective-permute-start(bf16[256,1536]{1,0:T(8,128)(2,1)S(1)} %multiply_convert_fusion), channel_id=1, source_target_pairs={{0,6},{1,7},{2,0},{3,1},{4,2},{5,3},{6,4},{7,5},{8,14},{9,15},{10,... | collective-permute-start | bytes 2359304 | tf_op jit(solution)/shard_map/ppermute | solution.py:147
  137.6 17.9 %collective-permute-start.3 = (bf16[256,1536]{1,0:T(8,128)(2,1)S(1)}, bf16[256,1536]{1,0:T(8,128)(2,1)S(1)}, u32[]{:S(2)}, u32[]{:S(2)}) collective-permute-start(bf16[256,1536]{1,0:T(8,128)(2,1)S(1)} %multiply_convert_fusion), channel_id=1, source_target_pairs={{0,1},{1,0},{2,3},{3,2},{4,5},{5,4},{6,7},{7,6},{8,9},{9,8},{10,11... | collective-permute-start | bytes 2359304 | tf_op jit(solution)/shard_map/ppermute | solution.py:150
  137.7 34.2 %slice-start.1 = ((s8[6291456]{0:T(1024)(128)(4,1)}), s8[2097152]{0:T(1024)(128)(4,1)S(1)}, s32[]{:S(2)}) async-start(s8[6291456]{0:T(1024)(128)(4,1)} %bitcast.70), calls=%async_computation.1 | async-start | bytes 4194304
  155.5 16.4 %collective-permute-start.6 = (bf16[256,1536]{1,0:T(8,128)(2,1)S(1)}, bf16[256,1536]{1,0:T(8,128)(2,1)S(1)}, u32[]{:S(2)}, u32[]{:S(2)}) collective-permute-start(bf16[256,1536]{1,0:T(8,128)(2,1)S(1)} %collective-permute-done.5), channel_id=1, source_target_pairs={{0,1},{1,0},{2,3},{3,2},{4,5},{5,4},{6,7},{7,6},{8,9},{9,8},{10,11... | collective-permute-start | bytes 2359304 | tf_op jit(solution)/shard_map/ppermute | solution.py:150
  163.0 41.6 %collective-permute-start.4 = (bf16[256,1536]{1,0:T(8,128)(2,1)S(1)}, bf16[256,1536]{1,0:T(8,128)(2,1)S(1)}, u32[]{:S(2)}, u32[]{:S(2)}) collective-permute-start(bf16[256,1536]{1,0:T(8,128)(2,1)S(1)} %slice.135), channel_id=1, source_target_pairs={{0,1},{1,0},{2,3},{3,2},{4,5},{5,4},{6,7},{7,6},{8,9},{9,8},{10,11... | collective-permute-start | bytes 2359304 | tf_op jit(solution)/shard_map/ppermute | solution.py:150
  171.4 10.1 %collective-permute-start.10 = (bf16[256,1536]{1,0:T(8,128)(2,1)S(1)}, bf16[256,1536]{1,0:T(8,128)(2,1)S(1)}, u32[]{:S(2)}, u32[]{:S(2)}) collective-permute-start(bf16[256,1536]{1,0:T(8,128)(2,1)S(1)} %collective-permute-done.9), channel_id=1, source_target_pairs={{0,1},{1,0},{2,3},{3,2},{4,5},{5,4},{6,7},{7,6},{8,9},{9,8},{10,11... | collective-permute-start | bytes 2359304 | tf_op jit(solution)/shard_map/ppermute | solution.py:150
  171.4 20.2 %collective-permute-start.14 = (bf16[256,1536]{1,0:T(8,128)(2,1)S(1)}, bf16[256,1536]{1,0:T(8,128)(2,1)S(1)}, u32[]{:S(2)}, u32[]{:S(2)}) collective-permute-start(bf16[256,1536]{1,0:T(8,128)(2,1)S(1)} %collective-permute-done.13), channel_id=1, source_target_pairs={{0,1},{1,0},{2,3},{3,2},{4,5},{5,4},{6,7},{7,6},{8,9},{9,8},{10,11... | collective-permute-start | bytes 2359304 | tf_op jit(solution)/shard_map/ppermute | solution.py:150
  181.4 19.8 %collective-permute-start.7 = (bf16[256,1536]{1,0:T(8,128)(2,1)S(1)}, bf16[256,1536]{1,0:T(8,128)(2,1)S(1)}, u32[]{:S(2)}, u32[]{:S(2)}) collective-permute-start(bf16[256,1536]{1,0:T(8,128)(2,1)S(1)} %slice.134), channel_id=1, source_target_pairs={{0,1},{1,0},{2,3},{3,2},{4,5},{5,4},{6,7},{7,6},{8,9},{9,8},{10,11... | collective-permute-start | bytes 2359304 | tf_op jit(solution)/shard_map/ppermute | solution.py:150
  191.0 12.2 %collective-permute-start.11 = (bf16[256,1536]{1,0:T(8,128)(2,1)S(1)}, bf16[256,1536]{1,0:T(8,128)(2,1)S(1)}, u32[]{:S(2)}, u32[]{:S(2)}) collective-permute-start(bf16[256,1536]{1,0:T(8,128)(2,1)S(1)} %slice.133), channel_id=1, source_target_pairs={{0,1},{1,0},{2,3},{3,2},{4,5},{5,4},{6,7},{7,6},{8,9},{9,8},{10,11... | collective-permute-start | bytes 2359304 | tf_op jit(solution)/shard_map/ppermute | solution.py:150
  201.1 2.8 %collective-permute-start.15 = (bf16[256,1536]{1,0:T(8,128)(2,1)S(1)}, bf16[256,1536]{1,0:T(8,128)(2,1)S(1)}, u32[]{:S(2)}, u32[]{:S(2)}) collective-permute-start(bf16[256,1536]{1,0:T(8,128)(2,1)S(1)} %slice.132), channel_id=1, source_target_pairs={{0,1},{1,0},{2,3},{3,2},{4,5},{5,4},{6,7},{7,6},{8,9},{9,8},{10,11... | collective-permute-start | bytes 2359304 | tf_op jit(solution)/shard_map/ppermute | solution.py:150
  201.4 20.4 %collective-permute-start.8 = (bf16[256,1536]{1,0:T(8,128)(2,1)S(1)}, bf16[256,1536]{1,0:T(8,128)(2,1)S(1)}, u32[]{:S(2)}, u32[]{:S(2)}) collective-permute-start(bf16[256,1536]{1,0:T(8,128)(2,1)S(1)} %fusion.6), channel_id=1, source_target_pairs={{0,6},{1,7},{2,0},{3,1},{4,2},{5,3},{6,4},{7,5},{8,14},{9,15},{10,... | collective-permute-start | bytes 2359304 | tf_op jit(solution)/shard_map/ppermute | solution.py:147
  203.4 36.6 %collective-permute-start.12 = (bf16[256,1536]{1,0:T(8,128)(2,1)S(1)}, bf16[256,1536]{1,0:T(8,128)(2,1)S(1)}, u32[]{:S(2)}, u32[]{:S(2)}) collective-permute-start(bf16[256,1536]{1,0:T(8,128)(2,1)S(1)} %fusion.5), channel_id=1, source_target_pairs={{0,4},{1,5},{2,6},{3,7},{4,0},{5,1},{6,2},{7,3},{8,12},{9,13},{10,... | collective-permute-start | bytes 2359304 | tf_op jit(solution)/shard_map/ppermute | solution.py:147
  204.2 35.8 %collective-permute-start.16 = (bf16[256,1536]{1,0:T(8,128)(2,1)S(1)}, bf16[256,1536]{1,0:T(8,128)(2,1)S(1)}, u32[]{:S(2)}, u32[]{:S(2)}) collective-permute-start(bf16[256,1536]{1,0:T(8,128)(2,1)S(1)} %fusion.4), channel_id=1, source_target_pairs={{0,2},{1,3},{2,4},{3,5},{4,6},{5,7},{6,0},{7,1},{8,10},{9,11},{10,... | collective-permute-start | bytes 2359304 | tf_op jit(solution)/shard_map/ppermute | solution.py:147

commit v12 on v10

--- a/solution.py
+++ b/solution.py
@@ -154,10 +154,11 @@
     def block_gate(device):
         return lax.dynamic_index_in_dim(gate_blocks, device, 0, keepdims=False)
 
-    same_core = [normed] + [chip_shift(normed, d) for d in range(1, half)]
-    other_core = [sibling(rows) for rows in same_core]
+    order = [0] + sorted(range(1, half), key=lambda d: -min(d, half - d))
+    same_core = {d: normed if d == 0 else chip_shift(normed, d) for d in order}
+    other_core = {d: sibling(same_core[d]) for d in order}
     total = None
-    for d in range(half):
+    for d in order:
         source_chip = (chip - d) % half
         other_partial = run_experts(other_core[d], block_gate(2 * source_chip + 1 - core), w_in, w_down)
         same_partial = run_experts(same_core[d], block_gate(2 * source_chip + core), w_in, w_down)

time: 231 us -> 231 us (level)
  transfers between devices with their start and end apart: 17 -> 17, of which waited for: 9 -> 7; matrix products, arithmetic and copies ran while one was open for 16% -> 16% of each run, Pallas kernels for 0% -> 0%
where the time goes in v12:
time: 231 us; the launch traced here: 229 us
  waiting for transfers between devices  124 us (54%)
  matrix products  37.4 us (16%)
  Pallas kernels  36.1 us (16%)
  starting transfers between devices  13.6 us (6%)
  blocking collectives  9.22 us (4%)
  other arithmetic  5.78 us (3%)
    ppermute x3, waiting for transfers between devices, per_device(): lax.ppermute(prompt_key_value, 'req', [(s, (s + d) % columns) for s in ra...  73.6 us
    ppermute x6, waiting for transfers between devices, chip_shift(): return lax.ppermute(x, 'exp', pairs)  50.8 us
    pallas_call x1, Pallas kernels, attend(): pl.pallas_call(attention_kernel, grid_spec=grid_spec, out_shape=jax.Shape...  36.1 us
    dot_general x8, matrix products, run_experts(): jnp.einsum('td,edf->etf', rows, w_in, preferred_element_type=jnp.float32)  21.7 us
    all_gather x1, blocking collectives, per_device(): gate_gathered = lax.all_gather(gate_local, 'exp', axis=0, tiled=True)  9.22 us
    dot_general x8, matrix products, run_experts(): jnp.einsum('etf,efd->etd', act, w_down, preferred_element_type=jnp.float32)  8.66 us
    ppermute x6, starting transfers between devices, chip_shift(): return lax.ppermute(x, 'exp', pairs)  7.55 us
  transfers between devices with their start and end apart: 17, of which 7 were waited for; matrix products, arithmetic and copies ran while one was open for 16% of the time, Pallas kernels for 0%

profile of v12, /device:TPU:12, one launch (start us, length us, event | category | flops | bytes accessed | tf_op | source)
XLA Modules:
  0.0 228.7 jit_solution(6195720886884616489)
XLA Ops:
  0.0 1.6 collective-permute-start
  1.6 1.2 collective-permute-start.1
  2.8 1.8 collective-permute-start.2
  4.6 0.7 broadcast_clamp_fusion
  5.3 0.6 min.37.pages_ref
  5.9 0.7 select_reduce_fusion
  6.7 9.2 %all_gather.3 = f32[2048,16]{0,1:T(8,128)S(1)} all-gather(f32[256,16]{0,1:T(8,128)S(1)} %select_reduce_fusion), channel_id=1, replica_groups=mesh['req'=4,'exp'=8] {'exp'}, dimensions={0}, use_global_device_ids=true | all-gather | bytes 147456 | tf_op jit(solution)/shard_map/all_gather | solution.py:200
  15.9 1.1 convolution_minimum_fusion.4
  17.0 1.2 broadcast_clamp_fusion.1.groups_ref
  18.2 0.3 convolution_minimum_fusion.3
  18.5 0.3 convolution_minimum_fusion.2
  18.7 0.3 convolution_minimum_fusion.1
  19.0 0.9 fusion.1.visible_ref
  19.9 50.5 %collective-permute-done.rest_1_ = bf16[2,256,1024]{2,1,0:T(8,128)(2,1)} collective-permute-done((bf16[2,256,1024]{2,1,0:T(8,128)(2,1)}, bf16[2,256,1024]{2,1,0:T(8,128)(2,1)}, u32[]{:S(2)}, u32[]{:S(2)}) %collective-permute-start) | collective-permute-done | bytes 1048608 | tf_op jit(solution)/shard_map/ppermute | solution.py:204
  70.4 21.3 %collective-permute-done.1.rest_2_ = bf16[2,256,1024]{2,1,0:T(8,128)(2,1)} collective-permute-done((bf16[2,256,1024]{2,1,0:T(8,128)(2,1)}, bf16[2,256,1024]{2,1,0:T(8,128)(2,1)}, u32[]{:S(2)}, u32[]{:S(2)}) %collective-permute-start.1) | collective-permute-done | bytes 1048608 | tf_op jit(solution)/shard_map/ppermute | solution.py:204
  91.7 1.8 collective-permute-done.2.rest_3_
  93.5 36.1 %shard_map.145 = bf16[256,1536]{1,0:T(8,128)(2,1)} custom-call(s32[8]{0:T(128)} %broadcast_clamp_fusion.1.groups_ref, s32[48]{0:T(128)} %min.37.pages_ref, s32[8]{0:T(128)} %lengths_ref.1, bf16[256,1536]{1,0:T(8,128)(2,1)} %queries_ref.1, bf16[256,1024]{1,0:T(8,128)(2,1)} %tree_ref.1, f32[8,32,32]{2,1,0:T(8,128)} %fusion.1.visible_ref, ...), custom_call_target="tpu_custom_call" | custom-call | tf_op jit(solution)/shard_map/pallas_call | solution.py:119
  129.6 4.3 %multiply_reduce_fusion.8 = (f32[256]{0:T(256)S(1)}, f32[256,1536]{1,0:T(8,128)S(1)}) fusion(bf16[256,1536]{1,0:T(8,128)(2,1)} %shard_map.145, bf16[1536,1536]{1,0:T(8,128)(2,1)} %param.24, bf16[256,1536]{1,0:T(8,128)(2,1)} %param.15), kind=kOutput, calls=%fused_computation.30 | convolution fusion | flops 1209532160 | bytes 7865344 | tf_op jit(solution)/shard_map/dot_general | solution.py:209
  133.9 1.1 copy-done.1
  135.0 1.1 multiply_convert_fusion
  136.1 0.0 collective-permute-start.3
  136.1 1.4 collective-permute-start.13
  137.5 0.6 collective-permute-start.9
  138.2 0.9 collective-permute-start.5
  139.2 0.0 collective-permute-done.3
  139.2 4.8 %convolution_bitcast_fusion.6 = f32[2,256,1024]{2,1,0:T(8,128)S(1)} fusion(bf16[2,1536,1024]{2,1,0:T(8,128)(2,1)} %param.28, bf16[256,1536]{1,0:T(8,128)(2,1)} %collective-permute-done.3), kind=kOutput, calls=%fused_computation.23 | convolution fusion | flops 1610612736 | bytes 9175040 | tf_op jit(solution)/shard_map/td,edf->etf/dot_general | solution.py:127
  144.0 0.0 slice-start
  144.1 1.1 multiply_reduce_fusion.6
  145.2 0.0 slice-start.1
  145.2 0.1 collective-permute-start.4
  145.3 11.4 %collective-permute-done.13 = bf16[256,1536]{1,0:T(8,128)(2,1)S(1)} collective-permute-done((bf16[256,1536]{1,0:T(8,128)(2,1)}, bf16[256,1536]{1,0:T(8,128)(2,1)S(1)}, u32[]{:S(2)}, u32[]{:S(2)}) %collective-permute-start.13) | collective-permute-done | bytes 786464 | tf_op jit(solution)/shard_map/ppermute | solution.py:147
  156.7 4.7 %convolution_bitcast_fusion.1 = f32[2,256,1024]{2,1,0:T(8,128)S(1)} fusion(bf16[2,1536,1024]{2,1,0:T(8,128)(2,1)} %param.28, bf16[256,1536]{1,0:T(8,128)(2,1)S(1)} %collective-permute-done.13), kind=kOutput, calls=%fused_computation.18 | convolution fusion | flops 1610612736 | bytes 9175040 | tf_op jit(solution)/shard_map/td,edf->etf/dot_general | solution.py:127
  161.4 1.0 multiply_reduce_fusion.1
  162.4 0.1 collective-permute-start.14
  162.5 10.7 %collective-permute-done.9 = bf16[256,1536]{1,0:T(8,128)(2,1)S(1)} collective-permute-done((bf16[256,1536]{1,0:T(8,128)(2,1)}, bf16[256,1536]{1,0:T(8,128)(2,1)S(1)}, u32[]{:S(2)}, u32[]{:S(2)}) %collective-permute-start.9) | collective-permute-done | bytes 786464 | tf_op jit(solution)/shard_map/ppermute | solution.py:147
  173.2 0.0 collective-permute-start.10
  173.2 1.8 convolution_bitcast_fusion.3
  175.0 1.8 convolution_bitcast_fusion.5
  176.8 0.6 collective-permute-start.6
  177.4 1.1 multiply_reduce_fusion.3
  178.4 1.1 multiply_reduce_fusion.5
  179.5 0.0 collective-permute-done.14
  179.6 1.8 convolution_bitcast_fusion
  181.3 1.1 multiply_reduce_fusion
  182.5 0.1 collective-permute-start.15
  182.5 0.0 collective-permute-done.10
  182.5 2.0 convolution_bitcast_fusion.2
  184.6 1.1 multiply_reduce_fusion.2
  185.7 0.6 collective-permute-start.11
  186.2 0.0 collective-permute-done.6
  186.2 1.8 convolution_bitcast_fusion.4
  188.0 1.1 multiply_reduce_fusion.4
  189.1 0.1 collective-permute-start.7
  189.2 0.2 add_convert_fusion.1
  189.4 1.5 collective-permute-start.16
  190.9 0.2 add_convert_fusion.2
  191.1 1.6 collective-permute-start.12
  192.7 0.2 add_convert_fusion.3
  192.9 1.6 collective-permute-start.8
  194.5 3.0 %convolution_bitcast_fusion.7 = f32[2,256,1024]{2,1,0:T(8,128)S(1)} fusion(bf16[2,1536,1024]{2,1,0:T(8,128)(2,1)S(1)} %bitcast.113, bf16[256,1536]{1,0:T(8,128)(2,1)} %multiply_convert_fusion), kind=kOutput, calls=%fused_computation.24 | convolution fusion | flops 1610612736 | bytes 9175040 | tf_op jit(solution)/shard_map/td,edf->etf/dot_general | solution.py:127
  197.5 1.1 multiply_reduce_fusion.7
  198.6 12.1 %collective-permute-done.16 = bf16[256,1536]{1,0:T(8,128)(2,1)S(1)} collective-permute-done((bf16[256,1536]{1,0:T(8,128)(2,1)S(1)}, bf16[256,1536]{1,0:T(8,128)(2,1)S(1)}, u32[]{:S(2)}, u32[]{:S(2)}) %collective-permute-start.16) | collective-permute-done | bytes 786464 | tf_op jit(solution)/shard_map/ppermute | solution.py:147
  210.7 16.5 %collective-permute-done.12 = bf16[256,1536]{1,0:T(8,128)(2,1)S(1)} collective-permute-done((bf16[256,1536]{1,0:T(8,128)(2,1)S(1)}, bf16[256,1536]{1,0:T(8,128)(2,1)S(1)}, u32[]{:S(2)}, u32[]{:S(2)}) %collective-permute-start.12) | collective-permute-done | bytes 786464 | tf_op jit(solution)/shard_map/ppermute | solution.py:147
  227.3 1.5 add_convert_fusion
  (29 shorter events, 0.1 us)
Async XLA Ops:
  0.0 144.0 %copy-start = (bf16[2,512,1536]{2,1,0:T(8,128)(2,1)S(1)}, bf16[2,512,1536]{2,1,0:T(8,128)(2,1)}, u32[]{:S(2)}) copy-start(bf16[2,512,1536]{2,1,0:T(8,128)(2,1)} %param.29) | copy-start | bytes 9437188
  0.0 70.4 %collective-permute-start = (bf16[2,256,1024]{2,1,0:T(8,128)(2,1)}, bf16[2,256,1024]{2,1,0:T(8,128)(2,1)}, u32[]{:S(2)}, u32[]{:S(2)}) collective-permute-start(bf16[2,256,1024]{2,1,0:T(8,128)(2,1)} %rest_0_), channel_id=1, source_target_pairs={{0,8},{8,16},{16,24},{24,0},{1,9},{9,17},{17,25},{25,1},{2,10},{10... | collective-permute-start | bytes 3145736 | tf_op jit(solution)/shard_map/ppermute | solution.py:204
  1.6 90.1 %collective-permute-start.1 = (bf16[2,256,1024]{2,1,0:T(8,128)(2,1)}, bf16[2,256,1024]{2,1,0:T(8,128)(2,1)}, u32[]{:S(2)}, u32[]{:S(2)}) collective-permute-start(bf16[2,256,1024]{2,1,0:T(8,128)(2,1)} %rest_0_), channel_id=1, source_target_pairs={{0,16},{8,24},{16,0},{24,8},{1,17},{9,25},{17,1},{25,9},{2,18},{10... | collective-permute-start | bytes 3145736 | tf_op jit(solution)/shard_map/ppermute | solution.py:204
  2.8 90.7 %collective-permute-start.2 = (bf16[2,256,1024]{2,1,0:T(8,128)(2,1)}, bf16[2,256,1024]{2,1,0:T(8,128)(2,1)}, u32[]{:S(2)}, u32[]{:S(2)}) collective-permute-start(bf16[2,256,1024]{2,1,0:T(8,128)(2,1)} %rest_0_), channel_id=1, source_target_pairs={{0,24},{8,0},{16,8},{24,16},{1,25},{9,1},{17,9},{25,17},{2,26},{10... | collective-permute-start | bytes 3145736 | tf_op jit(solution)/shard_map/ppermute | solution.py:204
  129.6 5.4 %copy-start.3 = (f32[1536]{0:T(1024)S(1)}, f32[1536]{0:T(1024)}, u32[]{:S(2)}) copy-start(f32[1536]{0:T(1024)} %param.25) | copy-start | bytes 18436
  133.9 1.2 copy-start.1
  136.1 3.1 %collective-permute-start.3 = (bf16[256,1536]{1,0:T(8,128)(2,1)}, bf16[256,1536]{1,0:T(8,128)(2,1)}, u32[]{:S(2)}, u32[]{:S(2)}) collective-permute-start(bf16[256,1536]{1,0:T(8,128)(2,1)} %multiply_convert_fusion), channel_id=1, source_target_pairs={{0,1},{1,0},{2,3},{3,2},{4,5},{5,4},{6,7},{7,6},{8,9},{9,8},{10,11... | collective-permute-start | bytes 2359304 | tf_op jit(solution)/shard_map/ppermute | solution.py:150
  136.1 20.6 %collective-permute-start.13 = (bf16[256,1536]{1,0:T(8,128)(2,1)}, bf16[256,1536]{1,0:T(8,128)(2,1)S(1)}, u32[]{:S(2)}, u32[]{:S(2)}) collective-permute-start(bf16[256,1536]{1,0:T(8,128)(2,1)} %multiply_convert_fusion), channel_id=1, source_target_pairs={{0,6},{1,7},{2,0},{3,1},{4,2},{5,3},{6,4},{7,5},{8,14},{9,15},{10,... | collective-permute-start | bytes 2359304 | tf_op jit(solution)/shard_map/ppermute | solution.py:147
  137.5 35.6 %collective-permute-start.9 = (bf16[256,1536]{1,0:T(8,128)(2,1)}, bf16[256,1536]{1,0:T(8,128)(2,1)S(1)}, u32[]{:S(2)}, u32[]{:S(2)}) collective-permute-start(bf16[256,1536]{1,0:T(8,128)(2,1)} %multiply_convert_fusion), channel_id=1, source_target_pairs={{0,2},{1,3},{2,4},{3,5},{4,6},{5,7},{6,0},{7,1},{8,10},{9,11},{10,... | collective-permute-start | bytes 2359304 | tf_op jit(solution)/shard_map/ppermute | solution.py:147
  138.2 36.8 %collective-permute-start.5 = (bf16[256,1536]{1,0:T(8,128)(2,1)}, bf16[256,1536]{1,0:T(8,128)(2,1)S(1)}, u32[]{:S(2)}, u32[]{:S(2)}) collective-permute-start(bf16[256,1536]{1,0:T(8,128)(2,1)} %multiply_convert_fusion), channel_id=1, source_target_pairs={{0,4},{1,5},{2,6},{3,7},{4,0},{5,1},{6,2},{7,3},{8,12},{9,13},{10,... | collective-permute-start | bytes 2359304 | tf_op jit(solution)/shard_map/ppermute | solution.py:147
  144.0 29.1 %slice-start = ((s8[6291456]{0:T(1024)(128)(4,1)}), s8[4194304]{0:T(1024)(128)(4,1)S(1)}, s32[]{:S(2)}) async-start(s8[6291456]{0:T(1024)(128)(4,1)} %bitcast.112), calls=%async_computation | async-start | bytes 8388608
  145.2 28.0 %slice-start.1 = ((s8[6291456]{0:T(1024)(128)(4,1)}), s8[2097152]{0:T(1024)(128)(4,1)S(1)}, s32[]{:S(2)}) async-start(s8[6291456]{0:T(1024)(128)(4,1)} %bitcast.112), calls=%async_computation.1 | async-start | bytes 4194304
  145.2 53.4 %collective-permute-start.4 = (bf16[256,1536]{1,0:T(8,128)(2,1)S(1)}, bf16[256,1536]{1,0:T(8,128)(2,1)S(1)}, u32[]{:S(2)}, u32[]{:S(2)}) collective-permute-start(bf16[256,1536]{1,0:T(8,128)(2,1)S(1)} %multiply_reduce_fusion.6), channel_id=1, source_target_pairs={{0,1},{1,0},{2,3},{3,2},{4,5},{5,4},{6,7},{7,6},{8,9},{9,8},{10,11... | collective-permute-start | bytes 2359304 | tf_op jit(solution)/shard_map/ppermute | solution.py:150
  162.4 17.1 %collective-permute-start.14 = (bf16[256,1536]{1,0:T(8,128)(2,1)S(1)}, bf16[256,1536]{1,0:T(8,128)(2,1)S(1)}, u32[]{:S(2)}, u32[]{:S(2)}) collective-permute-start(bf16[256,1536]{1,0:T(8,128)(2,1)S(1)} %collective-permute-done.13), channel_id=1, source_target_pairs={{0,1},{1,0},{2,3},{3,2},{4,5},{5,4},{6,7},{7,6},{8,9},{9,8},{10,11... | collective-permute-start | bytes 2359304 | tf_op jit(solution)/shard_map/ppermute | solution.py:150
  173.2 9.4 %collective-permute-start.10 = (bf16[256,1536]{1,0:T(8,128)(2,1)S(1)}, bf16[256,1536]{1,0:T(8,128)(2,1)S(1)}, u32[]{:S(2)}, u32[]{:S(2)}) collective-permute-start(bf16[256,1536]{1,0:T(8,128)(2,1)S(1)} %collective-permute-done.9), channel_id=1, source_target_pairs={{0,1},{1,0},{2,3},{3,2},{4,5},{5,4},{6,7},{7,6},{8,9},{9,8},{10,11... | collective-permute-start | bytes 2359304 | tf_op jit(solution)/shard_map/ppermute | solution.py:150
  176.8 9.4 %collective-permute-start.6 = (bf16[256,1536]{1,0:T(8,128)(2,1)S(1)}, bf16[256,1536]{1,0:T(8,128)(2,1)S(1)}, u32[]{:S(2)}, u32[]{:S(2)}) collective-permute-start(bf16[256,1536]{1,0:T(8,128)(2,1)S(1)} %collective-permute-done.5), channel_id=1, source_target_pairs={{0,1},{1,0},{2,3},{3,2},{4,5},{5,4},{6,7},{7,6},{8,9},{9,8},{10,11... | collective-permute-start | bytes 2359304 | tf_op jit(solution)/shard_map/ppermute | solution.py:150
  182.5 6.8 %collective-permute-start.15 = (bf16[256,1536]{1,0:T(8,128)(2,1)S(1)}, bf16[256,1536]{1,0:T(8,128)(2,1)S(1)}, u32[]{:S(2)}, u32[]{:S(2)}) collective-permute-start(bf16[256,1536]{1,0:T(8,128)(2,1)S(1)} %multiply_reduce_fusion), channel_id=1, source_target_pairs={{0,1},{1,0},{2,3},{3,2},{4,5},{5,4},{6,7},{7,6},{8,9},{9,8},{10,11... | collective-permute-start | bytes 2359304 | tf_op jit(solution)/shard_map/ppermute | solution.py:150
  185.7 5.2 %collective-permute-start.11 = (bf16[256,1536]{1,0:T(8,128)(2,1)S(1)}, bf16[256,1536]{1,0:T(8,128)(2,1)S(1)}, u32[]{:S(2)}, u32[]{:S(2)}) collective-permute-start(bf16[256,1536]{1,0:T(8,128)(2,1)S(1)} %multiply_reduce_fusion.2), channel_id=1, source_target_pairs={{0,1},{1,0},{2,3},{3,2},{4,5},{5,4},{6,7},{7,6},{8,9},{9,8},{10,11... | collective-permute-start | bytes 2359304 | tf_op jit(solution)/shard_map/ppermute | solution.py:150
  189.1 3.5 %collective-permute-start.7 = (bf16[256,1536]{1,0:T(8,128)(2,1)S(1)}, bf16[256,1536]{1,0:T(8,128)(2,1)S(1)}, u32[]{:S(2)}, u32[]{:S(2)}) collective-permute-start(bf16[256,1536]{1,0:T(8,128)(2,1)S(1)} %multiply_reduce_fusion.4), channel_id=1, source_target_pairs={{0,1},{1,0},{2,3},{3,2},{4,5},{5,4},{6,7},{7,6},{8,9},{9,8},{10,11... | collective-permute-start | bytes 2359304 | tf_op jit(solution)/shard_map/ppermute | solution.py:150
  189.4 21.3 %collective-permute-start.16 = (bf16[256,1536]{1,0:T(8,128)(2,1)S(1)}, bf16[256,1536]{1,0:T(8,128)(2,1)S(1)}, u32[]{:S(2)}, u32[]{:S(2)}) collective-permute-start(bf16[256,1536]{1,0:T(8,128)(2,1)S(1)} %add_convert_fusion.1), channel_id=1, source_target_pairs={{0,2},{1,3},{2,4},{3,5},{4,6},{5,7},{6,0},{7,1},{8,10},{9,11},{10,... | collective-permute-start | bytes 2359304 | tf_op jit(solution)/shard_map/ppermute | solution.py:147
  191.1 36.1 %collective-permute-start.12 = (bf16[256,1536]{1,0:T(8,128)(2,1)S(1)}, bf16[256,1536]{1,0:T(8,128)(2,1)S(1)}, u32[]{:S(2)}, u32[]{:S(2)}) collective-permute-start(bf16[256,1536]{1,0:T(8,128)(2,1)S(1)} %add_convert_fusion.2), channel_id=1, source_target_pairs={{0,6},{1,7},{2,0},{3,1},{4,2},{5,3},{6,4},{7,5},{8,14},{9,15},{10,... | collective-permute-start | bytes 2359304 | tf_op jit(solution)/shard_map/ppermute | solution.py:147
  192.9 34.4 %collective-permute-start.8 = (bf16[256,1536]{1,0:T(8,128)(2,1)S(1)}, bf16[256,1536]{1,0:T(8,128)(2,1)S(1)}, u32[]{:S(2)}, u32[]{:S(2)}) collective-permute-start(bf16[256,1536]{1,0:T(8,128)(2,1)S(1)} %add_convert_fusion.3), channel_id=1, source_target_pairs={{0,4},{1,5},{2,6},{3,7},{4,0},{5,1},{6,2},{7,3},{8,12},{9,13},{10,... | collective-permute-start | bytes 2359304 | tf_op jit(solution)/shard_map/ppermute | solution.py:147
  197.5 29.8 %copy-start.2 = (f32[256,1536]{1,0:T(8,128)S(1)}, f32[256,1536]{1,0:T(8,128)}, u32[]{:S(2)}) copy-start(f32[256,1536]{1,0:T(8,128)} %copy-done.1) | copy-start | bytes 4718596

commit v13 on v10

--- a/solution.py
+++ b/solution.py
@@ -199,10 +199,16 @@
     gate_gathered = lax.all_gather(gate_local, "exp", axis=0, tiled=True)
     gate = lax.dynamic_slice_in_dim(gate_gathered, lax.axis_index("exp") * local_experts, local_experts, 1)
     columns = lax.axis_size("req")
-    pieces = [prompt_key_value] + [
-        lax.ppermute(prompt_key_value, "req", [(s, (s + d) % columns) for s in range(columns)])
-        for d in range(1, columns)
-    ]
+    def shifted(x, d):
+        return lax.ppermute(x, "req", [(s, (s + d) % columns) for s in range(columns)])
+
+    if columns == 4 and prompt_key_value.shape[0] == 2:
+        forward = shifted(prompt_key_value, 1)
+        backward = shifted(prompt_key_value, columns - 1)
+        across = jnp.concatenate([shifted(forward[0:1], 1), shifted(backward[1:2], columns - 1)], 0)
+        pieces = [prompt_key_value, forward, across, backward]
+    else:
+        pieces = [prompt_key_value] + [shifted(prompt_key_value, d) for d in range(1, columns)]
     gate, pieces = lax.optimization_barrier((gate, pieces))
     attended = attend(queries, draft_kv, pieces, cache_page_store, page_table, cache_len, parents, groups)
     mixed = resid.astype(jnp.float32) + jnp.dot(attended, w_out, preferred_element_type=jnp.float32)

time: 231 us -> 217 us (0.939)
  waiting for transfers between devices: 126 us -> 105 us
  local copies, waits for them, and re-layouts: 1.85 us -> 5.57 us
    ppermute x3 -> x4, waiting for transfers between devices: 73.6 us -> 53.4 us  [shifted(): lax.ppermute(x, 'req', [(s, (s + d) % columns) for s in range(columns)])]
    slice x0 -> x2, local copies, waits for them, and re-layouts: none -> 3.74 us  [the longest x1 1.87 us: per_device(): forward[0:1]]
  transfers between devices with their start and end apart: 17 -> 18, of which waited for: 9 -> 8; matrix products, arithmetic and copies ran while one was open for 16% -> 19% of each run, Pallas kernels for 0% -> 0%
where the time goes in v13:
time: 217 us; the launch traced here: 214 us
  waiting for transfers between devices  105 us (48%)
  matrix products  37.4 us (17%)
  Pallas kernels  36.1 us (17%)
  starting transfers between devices  12.9 us (6%)
  blocking collectives  9.22 us (4%)
  other arithmetic  7.44 us (3%)
  local copies, waits for them, and re-layouts  5.57 us (3%)
    ppermute x4, waiting for transfers between devices, shifted(): lax.ppermute(x, 'req', [(s, (s + d) % columns) for s in range(columns)])  53.4 us
    ppermute x6, waiting for transfers between devices, chip_shift(): return lax.ppermute(x, 'exp', pairs)  51.9 us
    pallas_call x1, Pallas kernels, attend(): pl.pallas_call(attention_kernel, grid_spec=grid_spec, out_shape=jax.Shape...  36.1 us
    dot_general x8, matrix products, run_experts(): jnp.einsum('td,edf->etf', rows, w_in, preferred_element_type=jnp.float32)  21.7 us
    all_gather x1, blocking collectives, per_device(): gate_gathered = lax.all_gather(gate_local, 'exp', axis=0, tiled=True)  9.22 us
    dot_general x8, matrix products, run_experts(): jnp.einsum('etf,efd->etd', act, w_down, preferred_element_type=jnp.float32)  8.65 us
    ppermute x6, starting transfers between devices, chip_shift(): return lax.ppermute(x, 'exp', pairs)  7.4 us
  transfers between devices with their start and end apart: 18, of which 8 were waited for; matrix products, arithmetic and copies ran while one was open for 19% of the time, Pallas kernels for 0%

profile of v13, /device:TPU:12, one launch (start us, length us, event | category | flops | bytes accessed | tf_op | source)
XLA Modules:
  0.0 214.4 jit_solution(309756606706180074)
XLA Ops:
  0.0 1.6 collective-permute-start
  1.6 0.4 collective-permute-start.2
  2.0 0.7 broadcast_clamp_fusion
  2.7 0.7 select_reduce_fusion
  3.5 9.2 %all_gather.3 = f32[2048,16]{0,1:T(8,128)S(1)} all-gather(f32[256,16]{0,1:T(8,128)S(1)} %select_reduce_fusion), channel_id=1, replica_groups=mesh['req'=4,'exp'=8] {'exp'}, dimensions={0}, use_global_device_ids=true | all-gather | bytes 147456 | tf_op jit(solution)/shard_map/all_gather | solution.py:199
  12.7 1.1 convolution_minimum_fusion.4
  13.8 0.3 convolution_minimum_fusion.3
  14.1 0.3 convolution_minimum_fusion.2
  14.4 34.2 %collective-permute-done.2.rest_3_ = bf16[2,256,1024]{2,1,0:T(8,128)(2,1)} collective-permute-done((bf16[2,256,1024]{2,1,0:T(8,128)(2,1)}, bf16[2,256,1024]{2,1,0:T(8,128)(2,1)}, u32[]{:S(2)}, u32[]{:S(2)}) %collective-permute-start.2) | collective-permute-done | bytes 1048608 | tf_op jit(solution)/shard_map/ppermute | solution.py:203
  48.5 1.9 slice.73
  50.4 0.9 collective-permute-start.3
  51.3 0.0 collective-permute-done.rest_1_
  51.3 1.9 slice.72
  53.2 1.1 collective-permute-start.1
  54.3 0.5 broadcast_clamp_fusion.1.groups_ref
  54.9 0.6 min.37.pages_ref
  55.5 0.3 convolution_minimum_fusion.1
  55.7 0.9 fusion.1.visible_ref
  56.6 19.2 %collective-permute-done.3 = bf16[1,256,1024]{2,1,0:T(8,128)(2,1)} collective-permute-done((bf16[1,256,1024]{2,1,0:T(8,128)(2,1)}, bf16[1,256,1024]{2,1,0:T(8,128)(2,1)}, u32[]{:S(2)}, u32[]{:S(2)}) %collective-permute-start.3) | collective-permute-done | bytes 524320 | tf_op jit(solution)/shard_map/ppermute | solution.py:203
  75.8 2.3 %pad_maximum_fusion.rest_2_ = bf16[2,256,1024]{2,1,0:T(8,128)(2,1)} fusion(bf16[1,256,1024]{2,1,0:T(8,128)(2,1)} %collective-permute-done.3, bf16[1,256,1024]{2,1,0:T(8,128)(2,1)} %collective-permute-done.1), kind=kLoop, calls=%fused_computation.54 | loop fusion | flops 524288 | bytes 2097152 | tf_op jit(solution)/shard_map/concatenate | solution.py:208
  78.1 36.1 %shard_map.145 = bf16[256,1536]{1,0:T(8,128)(2,1)} custom-call(s32[8]{0:T(128)} %broadcast_clamp_fusion.1.groups_ref, s32[48]{0:T(128)} %min.37.pages_ref, s32[8]{0:T(128)} %lengths_ref.1, bf16[256,1536]{1,0:T(8,128)(2,1)} %queries_ref.1, bf16[256,1024]{1,0:T(8,128)(2,1)} %tree_ref.1, f32[8,32,32]{2,1,0:T(8,128)} %fusion.1.visible_ref, ...), custom_call_target="tpu_custom_call" | custom-call | tf_op jit(solution)/shard_map/pallas_call | solution.py:119
  114.2 4.3 %multiply_reduce_fusion.8 = (f32[256]{0:T(256)S(1)}, f32[256,1536]{1,0:T(8,128)S(1)}) fusion(bf16[256,1536]{1,0:T(8,128)(2,1)} %shard_map.145, bf16[1536,1536]{1,0:T(8,128)(2,1)} %param.24, bf16[256,1536]{1,0:T(8,128)(2,1)} %param.15), kind=kOutput, calls=%fused_computation.30 | convolution fusion | flops 1209532160 | bytes 7865344 | tf_op jit(solution)/shard_map/dot_general | solution.py:214
  118.4 1.1 copy-done.1
  119.6 1.1 multiply_convert_fusion
  120.7 1.4 collective-permute-start.14
  122.1 1.5 collective-permute-start.10
  123.6 0.0 collective-permute-start.6
  123.7 4.8 %convolution_bitcast_fusion.6 = f32[2,256,1024]{2,1,0:T(8,128)S(1)} fusion(bf16[2,1536,1024]{2,1,0:T(8,128)(2,1)} %param.28, bf16[256,1536]{1,0:T(8,128)(2,1)} %collective-permute-done.4), kind=kOutput, calls=%fused_computation.23 | convolution fusion | flops 1610612736 | bytes 9175040 | tf_op jit(solution)/shard_map/td,edf->etf/dot_general | solution.py:127
  128.6 0.0 slice-start
  128.6 1.1 multiply_reduce_fusion.6
  129.7 0.0 slice-start.1
  129.7 0.1 collective-permute-start.5
  129.8 11.4 %collective-permute-done.14 = bf16[256,1536]{1,0:T(8,128)(2,1)S(1)} collective-permute-done((bf16[256,1536]{1,0:T(8,128)(2,1)}, bf16[256,1536]{1,0:T(8,128)(2,1)S(1)}, u32[]{:S(2)}, u32[]{:S(2)}) %collective-permute-start.14) | collective-permute-done | bytes 786464 | tf_op jit(solution)/shard_map/ppermute | solution.py:147
  141.2 4.7 %convolution_bitcast_fusion.1 = f32[2,256,1024]{2,1,0:T(8,128)S(1)} fusion(bf16[2,1536,1024]{2,1,0:T(8,128)(2,1)} %param.28, bf16[256,1536]{1,0:T(8,128)(2,1)S(1)} %collective-permute-done.14), kind=kOutput, calls=%fused_computation.18 | convolution fusion | flops 1610612736 | bytes 9175040 | tf_op jit(solution)/shard_map/td,edf->etf/dot_general | solution.py:127
  145.9 1.0 multiply_reduce_fusion.1
  146.9 0.1 collective-permute-start.15
  147.0 11.8 %collective-permute-done.10 = bf16[256,1536]{1,0:T(8,128)(2,1)S(1)} collective-permute-done((bf16[256,1536]{1,0:T(8,128)(2,1)}, bf16[256,1536]{1,0:T(8,128)(2,1)S(1)}, u32[]{:S(2)}, u32[]{:S(2)}) %collective-permute-start.10) | collective-permute-done | bytes 786464 | tf_op jit(solution)/shard_map/ppermute | solution.py:147
  158.9 1.8 convolution_bitcast_fusion.3
  160.7 1.8 convolution_bitcast_fusion.5
  162.5 0.6 collective-permute-start.7
  163.0 1.1 multiply_reduce_fusion.3
  164.1 1.1 multiply_reduce_fusion.5
  165.2 1.8 convolution_bitcast_fusion
  167.0 1.1 multiply_reduce_fusion
  168.1 0.1 collective-permute-start.16
  168.2 2.0 convolution_bitcast_fusion.2
  170.2 1.1 multiply_reduce_fusion.2
  171.3 0.6 collective-permute-start.12
  171.9 1.8 convolution_bitcast_fusion.4
  173.7 1.1 multiply_reduce_fusion.4
  174.8 0.1 collective-permute-start.8
  174.9 0.2 add_convert_fusion.1
  175.1 0.6 collective-permute-start.17
  175.7 0.2 add_convert_fusion.2
  175.9 1.0 collective-permute-start.13
  177.0 0.2 collective-permute-done.8
  177.1 0.2 add_convert_fusion.3
  177.3 2.8 %collective-permute-start.9 = (bf16[256,1536]{1,0:T(8,128)(2,1)S(1)}, bf16[256,1536]{1,0:T(8,128)(2,1)S(1)}, u32[]{:S(2)}, u32[]{:S(2)}) collective-permute-start(bf16[256,1536]{1,0:T(8,128)(2,1)S(1)} %add_convert_fusion.3), channel_id=1, source_target_pairs={{0,6},{1,7},{2,0},{3,1},{4,2},{5,3},{6,4},{7,5},{8,14},{9,15},{10,... | collective-permute-start | bytes 2359304 | tf_op jit(solution)/shard_map/ppermute | solution.py:147
  180.1 3.0 %convolution_bitcast_fusion.7 = f32[2,256,1024]{2,1,0:T(8,128)S(1)} fusion(bf16[2,1536,1024]{2,1,0:T(8,128)(2,1)S(1)} %bitcast.113, bf16[256,1536]{1,0:T(8,128)(2,1)} %multiply_convert_fusion), kind=kOutput, calls=%fused_computation.24 | convolution fusion | flops 1610612736 | bytes 9175040 | tf_op jit(solution)/shard_map/td,edf->etf/dot_general | solution.py:127
  183.2 1.1 multiply_reduce_fusion.7
  184.3 12.1 %collective-permute-done.17 = bf16[256,1536]{1,0:T(8,128)(2,1)S(1)} collective-permute-done((bf16[256,1536]{1,0:T(8,128)(2,1)S(1)}, bf16[256,1536]{1,0:T(8,128)(2,1)S(1)}, u32[]{:S(2)}, u32[]{:S(2)}) %collective-permute-start.17) | collective-permute-done | bytes 786464 | tf_op jit(solution)/shard_map/ppermute | solution.py:147
  196.4 16.1 %collective-permute-done.13 = bf16[256,1536]{1,0:T(8,128)(2,1)S(1)} collective-permute-done((bf16[256,1536]{1,0:T(8,128)(2,1)S(1)}, bf16[256,1536]{1,0:T(8,128)(2,1)S(1)}, u32[]{:S(2)}, u32[]{:S(2)}) %collective-permute-start.13) | collective-permute-done | bytes 786464 | tf_op jit(solution)/shard_map/ppermute | solution.py:147
  212.5 0.4 collective-permute-done.9
  212.9 1.5 add_convert_fusion
  (36 shorter events, 0.1 us)
Async XLA Ops:
  0.0 128.6 %copy-start = (bf16[2,512,1536]{2,1,0:T(8,128)(2,1)S(1)}, bf16[2,512,1536]{2,1,0:T(8,128)(2,1)}, u32[]{:S(2)}) copy-start(bf16[2,512,1536]{2,1,0:T(8,128)(2,1)} %param.29) | copy-start | bytes 9437188
  0.0 54.3 %copy-start.4 = (s32[8]{0:T(128)S(1)}, s32[8]{0:T(128)}, u32[]{:S(2)}) copy-start(s32[8]{0:T(128)} %param.23) | copy-start | bytes 100
  0.0 51.3 %collective-permute-start = (bf16[2,256,1024]{2,1,0:T(8,128)(2,1)}, bf16[2,256,1024]{2,1,0:T(8,128)(2,1)}, u32[]{:S(2)}, u32[]{:S(2)}) collective-permute-start(bf16[2,256,1024]{2,1,0:T(8,128)(2,1)} %rest_0_), channel_id=1, source_target_pairs={{0,8},{8,16},{16,24},{24,0},{1,9},{9,17},{17,25},{25,1},{2,10},{10... | collective-permute-start | bytes 3145736 | tf_op jit(solution)/shard_map/ppermute | solution.py:203
  1.6 47.0 %collective-permute-start.2 = (bf16[2,256,1024]{2,1,0:T(8,128)(2,1)}, bf16[2,256,1024]{2,1,0:T(8,128)(2,1)}, u32[]{:S(2)}, u32[]{:S(2)}) collective-permute-start(bf16[2,256,1024]{2,1,0:T(8,128)(2,1)} %rest_0_), channel_id=1, source_target_pairs={{0,24},{8,0},{16,8},{24,16},{1,25},{9,1},{17,9},{25,17},{2,26},{10... | collective-permute-start | bytes 3145736 | tf_op jit(solution)/shard_map/ppermute | solution.py:203
  50.4 25.4 %collective-permute-start.3 = (bf16[1,256,1024]{2,1,0:T(8,128)(2,1)}, bf16[1,256,1024]{2,1,0:T(8,128)(2,1)}, u32[]{:S(2)}, u32[]{:S(2)}) collective-permute-start(bf16[1,256,1024]{2,1,0:T(8,128)(2,1)} %slice.73), channel_id=1, source_target_pairs={{0,24},{8,0},{16,8},{24,16},{1,25},{9,1},{17,9},{25,17},{2,26},{10... | collective-permute-start | bytes 1572872 | tf_op jit(solution)/shard_map/ppermute | solution.py:203
  53.2 22.6 %collective-permute-start.1 = (bf16[1,256,1024]{2,1,0:T(8,128)(2,1)}, bf16[1,256,1024]{2,1,0:T(8,128)(2,1)}, u32[]{:S(2)}, u32[]{:S(2)}) collective-permute-start(bf16[1,256,1024]{2,1,0:T(8,128)(2,1)} %slice.72), channel_id=1, source_target_pairs={{0,8},{8,16},{16,24},{24,0},{1,9},{9,17},{17,25},{25,1},{2,10},{10... | collective-permute-start | bytes 1572872 | tf_op jit(solution)/shard_map/ppermute | solution.py:203
  114.2 5.4 %copy-start.3 = (f32[1536]{0:T(1024)S(1)}, f32[1536]{0:T(1024)}, u32[]{:S(2)}) copy-start(f32[1536]{0:T(1024)} %param.25) | copy-start | bytes 18436
  118.4 1.2 copy-start.1
  120.7 3.1 %collective-permute-start.4 = (bf16[256,1536]{1,0:T(8,128)(2,1)}, bf16[256,1536]{1,0:T(8,128)(2,1)}, u32[]{:S(2)}, u32[]{:S(2)}) collective-permute-start(bf16[256,1536]{1,0:T(8,128)(2,1)} %multiply_convert_fusion), channel_id=1, source_target_pairs={{0,1},{1,0},{2,3},{3,2},{4,5},{5,4},{6,7},{7,6},{8,9},{9,8},{10,11... | collective-permute-start | bytes 2359304 | tf_op jit(solution)/shard_map/ppermute | solution.py:150
  120.7 20.5 %collective-permute-start.14 = (bf16[256,1536]{1,0:T(8,128)(2,1)}, bf16[256,1536]{1,0:T(8,128)(2,1)S(1)}, u32[]{:S(2)}, u32[]{:S(2)}) collective-permute-start(bf16[256,1536]{1,0:T(8,128)(2,1)} %multiply_convert_fusion), channel_id=1, source_target_pairs={{0,6},{1,7},{2,0},{3,1},{4,2},{5,3},{6,4},{7,5},{8,14},{9,15},{10,... | collective-permute-start | bytes 2359304 | tf_op jit(solution)/shard_map/ppermute | solution.py:147
  122.1 36.7 %collective-permute-start.10 = (bf16[256,1536]{1,0:T(8,128)(2,1)}, bf16[256,1536]{1,0:T(8,128)(2,1)S(1)}, u32[]{:S(2)}, u32[]{:S(2)}) collective-permute-start(bf16[256,1536]{1,0:T(8,128)(2,1)} %multiply_convert_fusion), channel_id=1, source_target_pairs={{0,4},{1,5},{2,6},{3,7},{4,0},{5,1},{6,2},{7,3},{8,12},{9,13},{10,... | collective-permute-start | bytes 2359304 | tf_op jit(solution)/shard_map/ppermute | solution.py:147
  123.6 37.0 %collective-permute-start.6 = (bf16[256,1536]{1,0:T(8,128)(2,1)}, bf16[256,1536]{1,0:T(8,128)(2,1)S(1)}, u32[]{:S(2)}, u32[]{:S(2)}) collective-permute-start(bf16[256,1536]{1,0:T(8,128)(2,1)} %multiply_convert_fusion), channel_id=1, source_target_pairs={{0,2},{1,3},{2,4},{3,5},{4,6},{5,7},{6,0},{7,1},{8,10},{9,11},{10,... | collective-permute-start | bytes 2359304 | tf_op jit(solution)/shard_map/ppermute | solution.py:147
  128.6 30.2 %slice-start = ((s8[6291456]{0:T(1024)(128)(4,1)}), s8[4194304]{0:T(1024)(128)(4,1)S(1)}, s32[]{:S(2)}) async-start(s8[6291456]{0:T(1024)(128)(4,1)} %bitcast.112), calls=%async_computation | async-start | bytes 8388608
  129.7 29.1 %slice-start.1 = ((s8[6291456]{0:T(1024)(128)(4,1)}), s8[2097152]{0:T(1024)(128)(4,1)S(1)}, s32[]{:S(2)}) async-start(s8[6291456]{0:T(1024)(128)(4,1)} %bitcast.112), calls=%async_computation.1 | async-start | bytes 4194304
  129.7 54.5 %collective-permute-start.5 = (bf16[256,1536]{1,0:T(8,128)(2,1)S(1)}, bf16[256,1536]{1,0:T(8,128)(2,1)S(1)}, u32[]{:S(2)}, u32[]{:S(2)}) collective-permute-start(bf16[256,1536]{1,0:T(8,128)(2,1)S(1)} %multiply_reduce_fusion.6), channel_id=1, source_target_pairs={{0,1},{1,0},{2,3},{3,2},{4,5},{5,4},{6,7},{7,6},{8,9},{9,8},{10,11... | collective-permute-start | bytes 2359304 | tf_op jit(solution)/shard_map/ppermute | solution.py:150
  146.9 18.3 %collective-permute-start.15 = (bf16[256,1536]{1,0:T(8,128)(2,1)S(1)}, bf16[256,1536]{1,0:T(8,128)(2,1)S(1)}, u32[]{:S(2)}, u32[]{:S(2)}) collective-permute-start(bf16[256,1536]{1,0:T(8,128)(2,1)S(1)} %collective-permute-done.14), channel_id=1, source_target_pairs={{0,1},{1,0},{2,3},{3,2},{4,5},{5,4},{6,7},{7,6},{8,9},{9,8},{10,11... | collective-permute-start | bytes 2359304 | tf_op jit(solution)/shard_map/ppermute | solution.py:150
  158.8 9.4 %collective-permute-start.11 = (bf16[256,1536]{1,0:T(8,128)(2,1)S(1)}, bf16[256,1536]{1,0:T(8,128)(2,1)S(1)}, u32[]{:S(2)}, u32[]{:S(2)}) collective-permute-start(bf16[256,1536]{1,0:T(8,128)(2,1)S(1)} %collective-permute-done.10), channel_id=1, source_target_pairs={{0,1},{1,0},{2,3},{3,2},{4,5},{5,4},{6,7},{7,6},{8,9},{9,8},{10,11... | collective-permute-start | bytes 2359304 | tf_op jit(solution)/shard_map/ppermute | solution.py:150
  162.5 9.4 %collective-permute-start.7 = (bf16[256,1536]{1,0:T(8,128)(2,1)S(1)}, bf16[256,1536]{1,0:T(8,128)(2,1)S(1)}, u32[]{:S(2)}, u32[]{:S(2)}) collective-permute-start(bf16[256,1536]{1,0:T(8,128)(2,1)S(1)} %collective-permute-done.6), channel_id=1, source_target_pairs={{0,1},{1,0},{2,3},{3,2},{4,5},{5,4},{6,7},{7,6},{8,9},{9,8},{10,11... | collective-permute-start | bytes 2359304 | tf_op jit(solution)/shard_map/ppermute | solution.py:150
  168.1 6.8 %collective-permute-start.16 = (bf16[256,1536]{1,0:T(8,128)(2,1)S(1)}, bf16[256,1536]{1,0:T(8,128)(2,1)S(1)}, u32[]{:S(2)}, u32[]{:S(2)}) collective-permute-start(bf16[256,1536]{1,0:T(8,128)(2,1)S(1)} %multiply_reduce_fusion), channel_id=1, source_target_pairs={{0,1},{1,0},{2,3},{3,2},{4,5},{5,4},{6,7},{7,6},{8,9},{9,8},{10,11... | collective-permute-start | bytes 2359304 | tf_op jit(solution)/shard_map/ppermute | solution.py:150
  171.3 4.4 %collective-permute-start.12 = (bf16[256,1536]{1,0:T(8,128)(2,1)S(1)}, bf16[256,1536]{1,0:T(8,128)(2,1)S(1)}, u32[]{:S(2)}, u32[]{:S(2)}) collective-permute-start(bf16[256,1536]{1,0:T(8,128)(2,1)S(1)} %multiply_reduce_fusion.2), channel_id=1, source_target_pairs={{0,1},{1,0},{2,3},{3,2},{4,5},{5,4},{6,7},{7,6},{8,9},{9,8},{10,11... | collective-permute-start | bytes 2359304 | tf_op jit(solution)/shard_map/ppermute | solution.py:150
  174.8 2.4 %collective-permute-start.8 = (bf16[256,1536]{1,0:T(8,128)(2,1)S(1)}, bf16[256,1536]{1,0:T(8,128)(2,1)S(1)}, u32[]{:S(2)}, u32[]{:S(2)}) collective-permute-start(bf16[256,1536]{1,0:T(8,128)(2,1)S(1)} %multiply_reduce_fusion.4), channel_id=1, source_target_pairs={{0,1},{1,0},{2,3},{3,2},{4,5},{5,4},{6,7},{7,6},{8,9},{9,8},{10,11... | collective-permute-start | bytes 2359304 | tf_op jit(solution)/shard_map/ppermute | solution.py:150
  175.1 21.3 %collective-permute-start.17 = (bf16[256,1536]{1,0:T(8,128)(2,1)S(1)}, bf16[256,1536]{1,0:T(8,128)(2,1)S(1)}, u32[]{:S(2)}, u32[]{:S(2)}) collective-permute-start(bf16[256,1536]{1,0:T(8,128)(2,1)S(1)} %add_convert_fusion.1), channel_id=1, source_target_pairs={{0,2},{1,3},{2,4},{3,5},{4,6},{5,7},{6,0},{7,1},{8,10},{9,11},{10,... | collective-permute-start | bytes 2359304 | tf_op jit(solution)/shard_map/ppermute | solution.py:147
  175.9 36.6 %collective-permute-start.13 = (bf16[256,1536]{1,0:T(8,128)(2,1)S(1)}, bf16[256,1536]{1,0:T(8,128)(2,1)S(1)}, u32[]{:S(2)}, u32[]{:S(2)}) collective-permute-start(bf16[256,1536]{1,0:T(8,128)(2,1)S(1)} %add_convert_fusion.2), channel_id=1, source_target_pairs={{0,4},{1,5},{2,6},{3,7},{4,0},{5,1},{6,2},{7,3},{8,12},{9,13},{10,... | collective-permute-start | bytes 2359304 | tf_op jit(solution)/shard_map/ppermute | solution.py:147
  177.3 35.6 %collective-permute-start.9 = (bf16[256,1536]{1,0:T(8,128)(2,1)S(1)}, bf16[256,1536]{1,0:T(8,128)(2,1)S(1)}, u32[]{:S(2)}, u32[]{:S(2)}) collective-permute-start(bf16[256,1536]{1,0:T(8,128)(2,1)S(1)} %add_convert_fusion.3), channel_id=1, source_target_pairs={{0,6},{1,7},{2,0},{3,1},{4,2},{5,3},{6,4},{7,5},{8,14},{9,15},{10,... | collective-permute-start | bytes 2359304 | tf_op jit(solution)/shard_map/ppermute | solution.py:147
  183.2 29.8 %copy-start.2 = (f32[256,1536]{1,0:T(8,128)S(1)}, f32[256,1536]{1,0:T(8,128)}, u32[]{:S(2)}) copy-start(f32[256,1536]{1,0:T(8,128)} %copy-done.1) | copy-start | bytes 4718596
